TPU v7x, 512 devices: a whole 4x8x8 slice. The times are simulated.
512 devices in a mesh: chan: 128 (over z, y, core), win: 4 (over x).
Axes of the slice: x: 4, y: 8, z: 8, core: 2. Of those that a mesh axis runs over, the one named last changes fastest.
Arguments:
- records: bfloat16 [16384, 16384], P('chan', 'win'), may hold values from -60 to 60
- offsets: int32 [4], replicated, may hold values from 1 to 15, as said below
- starts: int32 [4], P('win'), may hold values from 0 to 2048
Outputs:
- stacked: float32 [16, 4, 16384, 128], P('win', None, 'chan')
Inputs may be any that keep to these rules, and one draw needn't show every extreme that they name: The offsets are distinct, and the largest is 15.
All inputs are finite; a program needn't handle non-finite values.
Results may differ from a plain program's by a relative error of at most 0.006.
Values may be sent and summed in bfloat16 or wider, within the bound.
No kernel may reach another device: no remote copies, remote signals or barrier semaphores. Data moves between devices by JAX's collectives and lax.ppermute only.
A program may use at most 64 MiB of HBM per device.

v0:
```python
import math

import jax
import jax.numpy as jnp
import ml_dtypes
import numpy as np
from jax import lax
from jax.sharding import PartitionSpec as P

WIN = 2048
NBIN = 1024
BAND = 64
L = 16
K = 4
OFFCAP = 16


turn_full = 2.0 * math.pi


def dft_table():
    samples = np.arange(WIN, dtype=np.int64)
    bins = np.arange(NBIN, dtype=np.int64)
    turns = samples[:, None] * bins[None, :] % WIN
    angles = np.float32(turn_full / WIN) * turns.astype(np.float32)
    table = np.concatenate([np.cos(angles), -np.sin(angles)], axis=1)
    return jnp.asarray(table.astype(ml_dtypes.bfloat16))


def taper_weights():
    samples = jnp.arange(WIN, dtype=jnp.float32)
    return 0.5 - 0.5 * jnp.cos(turn_full / WIN * (samples + 0.5))


def band_matrix():
    bins = jnp.arange(NBIN, dtype=jnp.int32)
    near = (jnp.abs(bins[:, None] - bins[None, :]) <= BAND).astype(jnp.float32)
    return near / jnp.sum(near, axis=0, keepdims=True)


def phase_tables(windows_total):
    lags = jnp.arange(L, dtype=jnp.int32) - L // 2
    bins = jnp.arange(NBIN, dtype=jnp.int32)
    turns = bins[None, :] * (lags[:, None] + WIN) % WIN
    angles = turn_full / WIN * turns.astype(jnp.float32)
    weight = jnp.where(bins == 0, 1.0, 2.0).astype(jnp.float32) / (
        2.0 * math.sqrt(NBIN * windows_total)
    )
    return (jnp.cos(angles) * weight[None, :], jnp.sin(angles) * weight[None, :])


def whiten(frames, table, taper, band):
    values = frames.astype(jnp.float32)
    shaped = ((values - jnp.mean(values, axis=1, keepdims=True)) * taper[None, :]).astype(
        jnp.bfloat16
    )
    spec = jnp.dot(shaped, table, preferred_element_type=jnp.float32)
    real = spec[:, :NBIN]
    imag = spec[:, NBIN:]
    level = (
        jnp.dot(jnp.sqrt(real * real + imag * imag), band, precision=lax.Precision.HIGHEST) + 1e-05
    )
    return ((real / level).astype(jnp.bfloat16), (imag / level).astype(jnp.bfloat16))


def lag_terms(own_re, own_im, partner, cos_w, sin_w):
    ar = own_re.astype(jnp.float32)[:, None, :]
    ai = own_im.astype(jnp.float32)[:, None, :]
    first = (ar * cos_w[None] - ai * sin_w[None]).astype(jnp.bfloat16)
    second = (ar * sin_w[None] + ai * cos_w[None]).astype(jnp.bfloat16)
    return jnp.einsum(
        "ctf,kjf->tkcj", first, partner[:, 0], preferred_element_type=jnp.float32
    ) + jnp.einsum("ctf,kjf->tkcj", second, partner[:, 1], preferred_element_type=jnp.float32)


def on_device(records, offsets, starts):
    n_chan = lax.axis_size("chan")
    groups = lax.axis_size("win")
    me = lax.axis_index("chan")
    frames = lax.dynamic_slice_in_dim(records, starts[0], WIN, 1)
    own_re, own_im = whiten(frames, dft_table(), taper_weights(), band_matrix())
    spectra = jnp.stack((own_re, own_im), axis=0)

    down = [(i + 1, i) for i in range(n_chan - 1)]
    jump = [((i + OFFCAP) % n_chan, i) for i in range(n_chan)]
    up = [((i - 1) % n_chan, i) for i in range(n_chan)]

    near = jnp.minimum(offsets, OFFCAP - offsets)
    steps = jnp.max(near)

    def advance(carry):
        step, low, high, picked = carry
        step = step + 1
        low = lax.ppermute(low, "chan", down)
        high = lax.ppermute(high, "chan", up)
        hit_low = offsets == step
        hit_high = offsets == OFFCAP - step
        picked = jnp.where(hit_low[:, None, None, None], low[None], picked)
        picked = jnp.where(hit_high[:, None, None, None], high[None], picked)
        return (step, low, high, picked)

    high0 = lax.ppermute(spectra, "chan", jump)
    empty = jnp.zeros((K,) + spectra.shape, jnp.bfloat16)
    carry = (jnp.int32(0), spectra, high0, empty)
    moved = lax.while_loop(lambda c: c[0] < steps, advance, carry)[3]
    cos_w, sin_w = phase_tables(groups)
    corr = lag_terms(own_re, own_im, moved, cos_w, sin_w)
    summed = lax.psum_scatter(corr, "win", scatter_dimension=0, tiled=True)
    valid = me + offsets < n_chan
    return jnp.where(valid[None, :, None, None], summed, 0.0)


def solution(mesh):
    in_specs = (P("chan", "win"), P(), P("win"))
    out_specs = P("win", None, "chan", None)
    return jax.shard_map(
        on_device, mesh=mesh, in_specs=in_specs, out_specs=out_specs, check_vma=False
    )
```

profile of v0, /device:TPU:1, one launch (start us, length us, event | category | flops | bytes accessed | tf_op | source)
XLA Modules:
  0.0 305.0 jit_solution(4065213041469251976)
XLA Ops:
  8.8 4.9 %fusion.26 = f32[128,2048]{1,0:T(8,128)S(1)} fusion(bf16[2048,2048]{1,0:T(8,128)(2,1)} %constant.65.clone, f32[2048]{0:T(1024)S(1)} %multiply_subtract_fusion, f32[128]{0:T(128)S(1)} %broadcast_multiply_fusion, bf16[128,4096]{1,0:T(8,128)(2,1)} %param.6, s32[]{:T(128)S(6)} %select_n.48), kind=kOutput, calls=%fused_computation.39 | convolution fusion | flops 1074790400 | bytes 9970180 | tf_op jit(solution)/shard_map/dot_general | solution.py:57
  13.8 3.1 %fusion.40 = (f32[128,1024]{1,0:T(8,128)}, bf16[128,1024]{1,0:T(8,128)(2,1)S(1)}, f32[128,1024]{1,0:T(8,128)}, bf16[128,1024]{1,0:T(8,128)(2,1)S(1)}) fusion(f32[128,2048]{1,0:T(8,128)S(1)} %fusion.26, f32[1024]{0:T(1024)S(1)} %convert_reduce_fusion), kind=kOutput, calls=%fused_computation.64 | convolution fusion | flops 1617166336 | bytes 3674112 | tf_op jit(solution)/shard_map/dot_general | solution.py:61
  17.7 11.5 %collective-permute-start.2 = (bf16[2,128,1024]{2,1,0:T(8,128)(2,1)}, bf16[2,128,1024]{2,1,0:T(8,128)(2,1)}, u32[]{:S(2)}, u32[]{:S(2)}) collective-permute-start(bf16[2,128,1024]{2,1,0:T(8,128)(2,1)} %pad_maximum_fusion), channel_id=1, source_target_pairs={{64,0},{68,4},{72,8},{76,12},{80,16},{84,20},{88,24},{92,28},{96,3... | collective-permute-start | bytes 1572872 | tf_op jit(solution)/shard_map/ppermute | solution.py:102
  30.2 9.9 %collective-permute-done.2 = bf16[2,128,1024]{2,1,0:T(8,128)(2,1)} collective-permute-done((bf16[2,128,1024]{2,1,0:T(8,128)(2,1)}, bf16[2,128,1024]{2,1,0:T(8,128)(2,1)}, u32[]{:S(2)}, u32[]{:S(2)}) %collective-permute-start.2) | collective-permute-done | bytes 524320 | tf_op jit(solution)/shard_map/ppermute | solution.py:102
  40.4 140.4 %while.14 = (s32[]{:T(128)}, bf16[2,128,1024]{2,1,0:T(8,128)(2,1)}, bf16[2,128,1024]{2,1,0:T(8,128)(2,1)}, bf16[4,2,128,1024]{3,2,1,0:T(8,128)(2,1)S(1)}, s32[]{...) while((s32[]{:T(128)}, bf16[2,128,1024]{2,1,0:T(8,128)(2,1)}, bf16[2,128,1024]{2,1,0:T(8,128)(2,1)}, ...), condition=%wide.region_4.5_spmd, body=%wide.region_3.4_spmd.sunk | while | flops 2097163 | bytes 11534553 | solution.py:105
  41.0 3.5 %collective-permute-start = (bf16[2,128,1024]{2,1,0:T(8,128)(2,1)}, bf16[2,128,1024]{2,1,0:T(8,128)(2,1)S(1)}, u32[]{:S(2)}, u32[]{:S(2)}) collective-permute-start(bf16[2,128,1024]{2,1,0:T(8,128)(2,1)} %get-tuple-element.112), channel_id=1, source_target_pairs={{4,0},{8,4},{12,8},{16,12},{20,16},{24,20},{28,24},{32,28},{36,32}... | collective-permute-start | bytes 1572872 | tf_op jit(solution)/shard_map/while/body/ppermute | solution.py:94
  44.5 3.1 %collective-permute-start.1 = (bf16[2,128,1024]{2,1,0:T(8,128)(2,1)}, bf16[2,128,1024]{2,1,0:T(8,128)(2,1)S(1)}, u32[]{:S(2)}, u32[]{:S(2)}) collective-permute-start(bf16[2,128,1024]{2,1,0:T(8,128)(2,1)} %get-tuple-element.113), channel_id=1, source_target_pairs={{508,0},{0,4},{4,8},{8,12},{12,16},{16,20},{20,24},{24,28},{28,32}... | collective-permute-start | bytes 1572872 | tf_op jit(solution)/shard_map/while/body/ppermute | solution.py:95
  47.6 5.1 %collective-permute-done = bf16[2,128,1024]{2,1,0:T(8,128)(2,1)S(1)} collective-permute-done((bf16[2,128,1024]{2,1,0:T(8,128)(2,1)}, bf16[2,128,1024]{2,1,0:T(8,128)(2,1)S(1)}, u32[]{:S(2)}, u32[]{:S(2)}) %collective-permute-start) | collective-permute-done | bytes 524320 | tf_op jit(solution)/shard_map/while/body/ppermute | solution.py:94
  56.3 8.1 %collective-permute-start = (bf16[2,128,1024]{2,1,0:T(8,128)(2,1)}, bf16[2,128,1024]{2,1,0:T(8,128)(2,1)S(1)}, u32[]{:S(2)}, u32[]{:S(2)}) collective-permute-start(bf16[2,128,1024]{2,1,0:T(8,128)(2,1)} %get-tuple-element.112), channel_id=1, source_target_pairs={{4,0},{8,4},{12,8},{16,12},{20,16},{24,20},{28,24},{32,28},{36,32}... | collective-permute-start | bytes 1572872 | tf_op jit(solution)/shard_map/while/body/ppermute | solution.py:94
  64.4 1.9 collective-permute-start.1
  68.4 4.3 %collective-permute-done.1 = bf16[2,128,1024]{2,1,0:T(8,128)(2,1)S(1)} collective-permute-done((bf16[2,128,1024]{2,1,0:T(8,128)(2,1)}, bf16[2,128,1024]{2,1,0:T(8,128)(2,1)S(1)}, u32[]{:S(2)}, u32[]{:S(2)}) %collective-permute-start.1) | collective-permute-done | bytes 524320 | tf_op jit(solution)/shard_map/while/body/ppermute | solution.py:95
  75.0 7.0 %collective-permute-start = (bf16[2,128,1024]{2,1,0:T(8,128)(2,1)}, bf16[2,128,1024]{2,1,0:T(8,128)(2,1)S(1)}, u32[]{:S(2)}, u32[]{:S(2)}) collective-permute-start(bf16[2,128,1024]{2,1,0:T(8,128)(2,1)} %get-tuple-element.112), channel_id=1, source_target_pairs={{4,0},{8,4},{12,8},{16,12},{20,16},{24,20},{28,24},{32,28},{36,32}... | collective-permute-start | bytes 1572872 | tf_op jit(solution)/shard_map/while/body/ppermute | solution.py:94
  84.0 2.4 collective-permute-done
  87.2 3.2 %collective-permute-done.1 = bf16[2,128,1024]{2,1,0:T(8,128)(2,1)S(1)} collective-permute-done((bf16[2,128,1024]{2,1,0:T(8,128)(2,1)}, bf16[2,128,1024]{2,1,0:T(8,128)(2,1)S(1)}, u32[]{:S(2)}, u32[]{:S(2)}) %collective-permute-start.1) | collective-permute-done | bytes 524320 | tf_op jit(solution)/shard_map/while/body/ppermute | solution.py:95
  92.7 7.0 %collective-permute-start = (bf16[2,128,1024]{2,1,0:T(8,128)(2,1)}, bf16[2,128,1024]{2,1,0:T(8,128)(2,1)S(1)}, u32[]{:S(2)}, u32[]{:S(2)}) collective-permute-start(bf16[2,128,1024]{2,1,0:T(8,128)(2,1)} %get-tuple-element.112), channel_id=1, source_target_pairs={{4,0},{8,4},{12,8},{16,12},{20,16},{24,20},{28,24},{32,28},{36,32}... | collective-permute-start | bytes 1572872 | tf_op jit(solution)/shard_map/while/body/ppermute | solution.py:94
  101.6 2.4 collective-permute-done
  104.8 3.2 %collective-permute-done.1 = bf16[2,128,1024]{2,1,0:T(8,128)(2,1)S(1)} collective-permute-done((bf16[2,128,1024]{2,1,0:T(8,128)(2,1)}, bf16[2,128,1024]{2,1,0:T(8,128)(2,1)S(1)}, u32[]{:S(2)}, u32[]{:S(2)}) %collective-permute-start.1) | collective-permute-done | bytes 524320 | tf_op jit(solution)/shard_map/while/body/ppermute | solution.py:95
  110.3 7.0 %collective-permute-start = (bf16[2,128,1024]{2,1,0:T(8,128)(2,1)}, bf16[2,128,1024]{2,1,0:T(8,128)(2,1)S(1)}, u32[]{:S(2)}, u32[]{:S(2)}) collective-permute-start(bf16[2,128,1024]{2,1,0:T(8,128)(2,1)} %get-tuple-element.112), channel_id=1, source_target_pairs={{4,0},{8,4},{12,8},{16,12},{20,16},{24,20},{28,24},{32,28},{36,32}... | collective-permute-start | bytes 1572872 | tf_op jit(solution)/shard_map/while/body/ppermute | solution.py:94
  119.2 2.4 collective-permute-done
  122.4 3.2 %collective-permute-done.1 = bf16[2,128,1024]{2,1,0:T(8,128)(2,1)S(1)} collective-permute-done((bf16[2,128,1024]{2,1,0:T(8,128)(2,1)}, bf16[2,128,1024]{2,1,0:T(8,128)(2,1)S(1)}, u32[]{:S(2)}, u32[]{:S(2)}) %collective-permute-start.1) | collective-permute-done | bytes 524320 | tf_op jit(solution)/shard_map/while/body/ppermute | solution.py:95
  127.9 7.0 %collective-permute-start = (bf16[2,128,1024]{2,1,0:T(8,128)(2,1)}, bf16[2,128,1024]{2,1,0:T(8,128)(2,1)S(1)}, u32[]{:S(2)}, u32[]{:S(2)}) collective-permute-start(bf16[2,128,1024]{2,1,0:T(8,128)(2,1)} %get-tuple-element.112), channel_id=1, source_target_pairs={{4,0},{8,4},{12,8},{16,12},{20,16},{24,20},{28,24},{32,28},{36,32}... | collective-permute-start | bytes 1572872 | tf_op jit(solution)/shard_map/while/body/ppermute | solution.py:94
  136.9 2.4 collective-permute-done
  140.1 3.2 %collective-permute-done.1 = bf16[2,128,1024]{2,1,0:T(8,128)(2,1)S(1)} collective-permute-done((bf16[2,128,1024]{2,1,0:T(8,128)(2,1)}, bf16[2,128,1024]{2,1,0:T(8,128)(2,1)S(1)}, u32[]{:S(2)}, u32[]{:S(2)}) %collective-permute-start.1) | collective-permute-done | bytes 524320 | tf_op jit(solution)/shard_map/while/body/ppermute | solution.py:95
  145.6 7.0 %collective-permute-start = (bf16[2,128,1024]{2,1,0:T(8,128)(2,1)}, bf16[2,128,1024]{2,1,0:T(8,128)(2,1)S(1)}, u32[]{:S(2)}, u32[]{:S(2)}) collective-permute-start(bf16[2,128,1024]{2,1,0:T(8,128)(2,1)} %get-tuple-element.112), channel_id=1, source_target_pairs={{4,0},{8,4},{12,8},{16,12},{20,16},{24,20},{28,24},{32,28},{36,32}... | collective-permute-start | bytes 1572872 | tf_op jit(solution)/shard_map/while/body/ppermute | solution.py:94
  154.5 2.4 collective-permute-done
  157.7 3.2 %collective-permute-done.1 = bf16[2,128,1024]{2,1,0:T(8,128)(2,1)S(1)} collective-permute-done((bf16[2,128,1024]{2,1,0:T(8,128)(2,1)}, bf16[2,128,1024]{2,1,0:T(8,128)(2,1)S(1)}, u32[]{:S(2)}, u32[]{:S(2)}) %collective-permute-start.1) | collective-permute-done | bytes 524320 | tf_op jit(solution)/shard_map/while/body/ppermute | solution.py:95
  163.2 7.0 %collective-permute-start = (bf16[2,128,1024]{2,1,0:T(8,128)(2,1)}, bf16[2,128,1024]{2,1,0:T(8,128)(2,1)S(1)}, u32[]{:S(2)}, u32[]{:S(2)}) collective-permute-start(bf16[2,128,1024]{2,1,0:T(8,128)(2,1)} %get-tuple-element.112), channel_id=1, source_target_pairs={{4,0},{8,4},{12,8},{16,12},{20,16},{24,20},{28,24},{32,28},{36,32}... | collective-permute-start | bytes 1572872 | tf_op jit(solution)/shard_map/while/body/ppermute | solution.py:94
  172.1 2.4 collective-permute-done
  175.3 3.2 %collective-permute-done.1 = bf16[2,128,1024]{2,1,0:T(8,128)(2,1)S(1)} collective-permute-done((bf16[2,128,1024]{2,1,0:T(8,128)(2,1)}, bf16[2,128,1024]{2,1,0:T(8,128)(2,1)S(1)}, u32[]{:S(2)}, u32[]{:S(2)}) %collective-permute-start.1) | collective-permute-done | bytes 524320 | tf_op jit(solution)/shard_map/while/body/ppermute | solution.py:95
  180.8 3.7 %fusion.1 = f32[4,128,128,16]{2,1,3,0:T(8,128)S(1)} fusion(f32[16,1024]{1,0:T(8,128)S(1)} %get-tuple-element.60, f32[128,1024]{1,0:T(8,128)} %get-tuple-element.57, f32[16,1024]{1,0:T(8,128)S(1)} %get-tuple-element.59, f32[128,1024]{1,0:T(8,128)} %get-tuple-element.51, bf16[4,2,128,1024]{3,2,1,0:T(8,128)(2,1)S(1)} %get-tuple-element.38), kind=kOutput, calls=%fused_computation.8 | convolution fusion | flops 2155872256 | bytes 6422528 | tf_op jit(solution)/shard_map/ctf,kjf->tkcj/dot_general | solution.py:71
  184.5 4.0 %add_bitcast_fusion = f32[16,4,128,128]{2,3,0,1:T(8,128)} fusion(f32[4,128,128,16]{2,1,3,0:T(8,128)S(1)} %fusion.1, f32[16,1024]{1,0:T(8,128)S(1)} %get-tuple-element.60, f32[128,1024]{1,0:T(8,128)S(1)} %copy-done.2, f32[16,1024]{1,0:T(8,128)S(1)} %get-tuple-element.59, f32[128,1024]{1,0:T(8,128)S(1)} %copy-done.1, ...), kind=kOutput, calls=%fused_computation.11 | convolution fusion | flops 2156920832 | bytes 10616832 | tf_op jit(solution)/shard_map/ctf,kjf->tkcj/dot_general | solution.py:73
  190.5 104.9 %all-reduce.3.cloned.1.call-done = f32[16,4,128,128]{2,3,0,1:T(8,128)} async-done(((f32[16,4,128,128]{2,3,0,1:T(8,128)}), f32[16,4,128,128]{2,3,0,1:T(8,128)}) %all-reduce.3.cloned.1.call-update) | async-done | bytes 4194320
  (62 shorter events, 40.6 us)
Async XLA Ops:
  6.5 288.9 %all-reduce.3.cloned.1.call-start = ((), (), s32[]{:S(2)}) async-start(), calls=%async_computation | async-start | bytes 8388608
  13.8 15.4 %copy-start = (s32[4]{0:T(128)S(1)}, s32[4]{0:T(128)}, u32[]{:S(2)}) copy-start(s32[4]{0:T(128)} %param.7) | copy-start | bytes 52
  17.7 22.4 %collective-permute-start.2 = (bf16[2,128,1024]{2,1,0:T(8,128)(2,1)}, bf16[2,128,1024]{2,1,0:T(8,128)(2,1)}, u32[]{:S(2)}, u32[]{:S(2)}) collective-permute-start(bf16[2,128,1024]{2,1,0:T(8,128)(2,1)} %pad_maximum_fusion), channel_id=1, source_target_pairs={{64,0},{68,4},{72,8},{76,12},{80,16},{84,20},{88,24},{92,28},{96,3... | collective-permute-start | bytes 1572872 | tf_op jit(solution)/shard_map/ppermute | solution.py:102
  41.0 11.7 %collective-permute-start = (bf16[2,128,1024]{2,1,0:T(8,128)(2,1)}, bf16[2,128,1024]{2,1,0:T(8,128)(2,1)S(1)}, u32[]{:S(2)}, u32[]{:S(2)}) collective-permute-start(bf16[2,128,1024]{2,1,0:T(8,128)(2,1)} %get-tuple-element.112), channel_id=1, source_target_pairs={{4,0},{8,4},{12,8},{16,12},{20,16},{24,20},{28,24},{32,28},{36,32}... | collective-permute-start | bytes 1572872 | tf_op jit(solution)/shard_map/while/body/ppermute | solution.py:94
  44.5 9.5 %collective-permute-start.1 = (bf16[2,128,1024]{2,1,0:T(8,128)(2,1)}, bf16[2,128,1024]{2,1,0:T(8,128)(2,1)S(1)}, u32[]{:S(2)}, u32[]{:S(2)}) collective-permute-start(bf16[2,128,1024]{2,1,0:T(8,128)(2,1)} %get-tuple-element.113), channel_id=1, source_target_pairs={{508,0},{0,4},{4,8},{8,12},{12,16},{16,20},{20,24},{24,28},{28,32}... | collective-permute-start | bytes 1572872 | tf_op jit(solution)/shard_map/while/body/ppermute | solution.py:95
  56.3 11.4 %collective-permute-start = (bf16[2,128,1024]{2,1,0:T(8,128)(2,1)}, bf16[2,128,1024]{2,1,0:T(8,128)(2,1)S(1)}, u32[]{:S(2)}, u32[]{:S(2)}) collective-permute-start(bf16[2,128,1024]{2,1,0:T(8,128)(2,1)} %get-tuple-element.112), channel_id=1, source_target_pairs={{4,0},{8,4},{12,8},{16,12},{20,16},{24,20},{28,24},{32,28},{36,32}... | collective-permute-start | bytes 1572872 | tf_op jit(solution)/shard_map/while/body/ppermute | solution.py:94
  64.4 8.3 %collective-permute-start.1 = (bf16[2,128,1024]{2,1,0:T(8,128)(2,1)}, bf16[2,128,1024]{2,1,0:T(8,128)(2,1)S(1)}, u32[]{:S(2)}, u32[]{:S(2)}) collective-permute-start(bf16[2,128,1024]{2,1,0:T(8,128)(2,1)} %get-tuple-element.113), channel_id=1, source_target_pairs={{508,0},{0,4},{4,8},{8,12},{12,16},{16,20},{20,24},{24,28},{28,32}... | collective-permute-start | bytes 1572872 | tf_op jit(solution)/shard_map/while/body/ppermute | solution.py:95
  75.0 11.4 %collective-permute-start = (bf16[2,128,1024]{2,1,0:T(8,128)(2,1)}, bf16[2,128,1024]{2,1,0:T(8,128)(2,1)S(1)}, u32[]{:S(2)}, u32[]{:S(2)}) collective-permute-start(bf16[2,128,1024]{2,1,0:T(8,128)(2,1)} %get-tuple-element.112), channel_id=1, source_target_pairs={{4,0},{8,4},{12,8},{16,12},{20,16},{24,20},{28,24},{32,28},{36,32}... | collective-permute-start | bytes 1572872 | tf_op jit(solution)/shard_map/while/body/ppermute | solution.py:94
  82.0 8.3 %collective-permute-start.1 = (bf16[2,128,1024]{2,1,0:T(8,128)(2,1)}, bf16[2,128,1024]{2,1,0:T(8,128)(2,1)S(1)}, u32[]{:S(2)}, u32[]{:S(2)}) collective-permute-start(bf16[2,128,1024]{2,1,0:T(8,128)(2,1)} %get-tuple-element.113), channel_id=1, source_target_pairs={{508,0},{0,4},{4,8},{8,12},{12,16},{16,20},{20,24},{24,28},{28,32}... | collective-permute-start | bytes 1572872 | tf_op jit(solution)/shard_map/while/body/ppermute | solution.py:95
  92.7 11.4 %collective-permute-start = (bf16[2,128,1024]{2,1,0:T(8,128)(2,1)}, bf16[2,128,1024]{2,1,0:T(8,128)(2,1)S(1)}, u32[]{:S(2)}, u32[]{:S(2)}) collective-permute-start(bf16[2,128,1024]{2,1,0:T(8,128)(2,1)} %get-tuple-element.112), channel_id=1, source_target_pairs={{4,0},{8,4},{12,8},{16,12},{20,16},{24,20},{28,24},{32,28},{36,32}... | collective-permute-start | bytes 1572872 | tf_op jit(solution)/shard_map/while/body/ppermute | solution.py:94
  99.7 8.3 %collective-permute-start.1 = (bf16[2,128,1024]{2,1,0:T(8,128)(2,1)}, bf16[2,128,1024]{2,1,0:T(8,128)(2,1)S(1)}, u32[]{:S(2)}, u32[]{:S(2)}) collective-permute-start(bf16[2,128,1024]{2,1,0:T(8,128)(2,1)} %get-tuple-element.113), channel_id=1, source_target_pairs={{508,0},{0,4},{4,8},{8,12},{12,16},{16,20},{20,24},{24,28},{28,32}... | collective-permute-start | bytes 1572872 | tf_op jit(solution)/shard_map/while/body/ppermute | solution.py:95
  110.3 11.4 %collective-permute-start = (bf16[2,128,1024]{2,1,0:T(8,128)(2,1)}, bf16[2,128,1024]{2,1,0:T(8,128)(2,1)S(1)}, u32[]{:S(2)}, u32[]{:S(2)}) collective-permute-start(bf16[2,128,1024]{2,1,0:T(8,128)(2,1)} %get-tuple-element.112), channel_id=1, source_target_pairs={{4,0},{8,4},{12,8},{16,12},{20,16},{24,20},{28,24},{32,28},{36,32}... | collective-permute-start | bytes 1572872 | tf_op jit(solution)/shard_map/while/body/ppermute | solution.py:94
  117.3 8.3 %collective-permute-start.1 = (bf16[2,128,1024]{2,1,0:T(8,128)(2,1)}, bf16[2,128,1024]{2,1,0:T(8,128)(2,1)S(1)}, u32[]{:S(2)}, u32[]{:S(2)}) collective-permute-start(bf16[2,128,1024]{2,1,0:T(8,128)(2,1)} %get-tuple-element.113), channel_id=1, source_target_pairs={{508,0},{0,4},{4,8},{8,12},{12,16},{16,20},{20,24},{24,28},{28,32}... | collective-permute-start | bytes 1572872 | tf_op jit(solution)/shard_map/while/body/ppermute | solution.py:95
  127.9 11.4 %collective-permute-start = (bf16[2,128,1024]{2,1,0:T(8,128)(2,1)}, bf16[2,128,1024]{2,1,0:T(8,128)(2,1)S(1)}, u32[]{:S(2)}, u32[]{:S(2)}) collective-permute-start(bf16[2,128,1024]{2,1,0:T(8,128)(2,1)} %get-tuple-element.112), channel_id=1, source_target_pairs={{4,0},{8,4},{12,8},{16,12},{20,16},{24,20},{28,24},{32,28},{36,32}... | collective-permute-start | bytes 1572872 | tf_op jit(solution)/shard_map/while/body/ppermute | solution.py:94
  134.9 8.3 %collective-permute-start.1 = (bf16[2,128,1024]{2,1,0:T(8,128)(2,1)}, bf16[2,128,1024]{2,1,0:T(8,128)(2,1)S(1)}, u32[]{:S(2)}, u32[]{:S(2)}) collective-permute-start(bf16[2,128,1024]{2,1,0:T(8,128)(2,1)} %get-tuple-element.113), channel_id=1, source_target_pairs={{508,0},{0,4},{4,8},{8,12},{12,16},{16,20},{20,24},{24,28},{28,32}... | collective-permute-start | bytes 1572872 | tf_op jit(solution)/shard_map/while/body/ppermute | solution.py:95
  145.6 11.4 %collective-permute-start = (bf16[2,128,1024]{2,1,0:T(8,128)(2,1)}, bf16[2,128,1024]{2,1,0:T(8,128)(2,1)S(1)}, u32[]{:S(2)}, u32[]{:S(2)}) collective-permute-start(bf16[2,128,1024]{2,1,0:T(8,128)(2,1)} %get-tuple-element.112), channel_id=1, source_target_pairs={{4,0},{8,4},{12,8},{16,12},{20,16},{24,20},{28,24},{32,28},{36,32}... | collective-permute-start | bytes 1572872 | tf_op jit(solution)/shard_map/while/body/ppermute | solution.py:94
  152.5 8.3 %collective-permute-start.1 = (bf16[2,128,1024]{2,1,0:T(8,128)(2,1)}, bf16[2,128,1024]{2,1,0:T(8,128)(2,1)S(1)}, u32[]{:S(2)}, u32[]{:S(2)}) collective-permute-start(bf16[2,128,1024]{2,1,0:T(8,128)(2,1)} %get-tuple-element.113), channel_id=1, source_target_pairs={{508,0},{0,4},{4,8},{8,12},{12,16},{16,20},{20,24},{24,28},{28,32}... | collective-permute-start | bytes 1572872 | tf_op jit(solution)/shard_map/while/body/ppermute | solution.py:95
  163.2 11.4 %collective-permute-start = (bf16[2,128,1024]{2,1,0:T(8,128)(2,1)}, bf16[2,128,1024]{2,1,0:T(8,128)(2,1)S(1)}, u32[]{:S(2)}, u32[]{:S(2)}) collective-permute-start(bf16[2,128,1024]{2,1,0:T(8,128)(2,1)} %get-tuple-element.112), channel_id=1, source_target_pairs={{4,0},{8,4},{12,8},{16,12},{20,16},{24,20},{28,24},{32,28},{36,32}... | collective-permute-start | bytes 1572872 | tf_op jit(solution)/shard_map/while/body/ppermute | solution.py:94
  170.2 8.3 %collective-permute-start.1 = (bf16[2,128,1024]{2,1,0:T(8,128)(2,1)}, bf16[2,128,1024]{2,1,0:T(8,128)(2,1)S(1)}, u32[]{:S(2)}, u32[]{:S(2)}) collective-permute-start(bf16[2,128,1024]{2,1,0:T(8,128)(2,1)} %get-tuple-element.113), channel_id=1, source_target_pairs={{508,0},{0,4},{4,8},{8,12},{12,16},{16,20},{20,24},{24,28},{28,32}... | collective-permute-start | bytes 1572872 | tf_op jit(solution)/shard_map/while/body/ppermute | solution.py:95
  180.8 3.7 %copy-start.1 = (f32[128,1024]{1,0:T(8,128)S(1)}, f32[128,1024]{1,0:T(8,128)}, u32[]{:S(2)}) copy-start(f32[128,1024]{1,0:T(8,128)} %get-tuple-element.51) | copy-start | bytes 1572868
  180.8 3.7 %copy-start.2 = (f32[128,1024]{1,0:T(8,128)S(1)}, f32[128,1024]{1,0:T(8,128)}, u32[]{:S(2)}) copy-start(f32[128,1024]{1,0:T(8,128)} %get-tuple-element.57) | copy-start | bytes 1572868
Sparse Core Ops, SparseCore 0:
  188.7 106.6 all-reduce.2
where the time goes:
time: 306 us; the launch traced here: 305 us
  waiting for transfers between devices  160 us (52%)
  starting transfers between devices  81.4 us (27%)
  matrix products  15.7 us (5%)
  local copies, waits for them, and re-layouts  15.6 us (5%)
  between operations  14.8 us (5%)
  other arithmetic  11.6 us (4%)
  loops' own time  6.04 us (2%)
    unnamed x2, waiting for transfers between devices  105 us
    ppermute x8, starting transfers between devices, advance(): low = lax.ppermute(low, 'chan', down)  53.4 us
    ppermute x8, waiting for transfers between devices, advance(): high = lax.ppermute(high, 'chan', up)  23.9 us
    ppermute x8, waiting for transfers between devices, advance(): low = lax.ppermute(low, 'chan', down)  21 us
    ppermute x8, starting transfers between devices, advance(): high = lax.ppermute(high, 'chan', up)  16.5 us
    while x16, local copies, waits for them, and re-layouts  12.8 us
    ppermute x1, starting transfers between devices, on_device(): high0 = lax.ppermute(spectra, 'chan', jump)  11.5 us
    ppermute x1, waiting for transfers between devices, on_device(): high0 = lax.ppermute(spectra, 'chan', jump)  9.86 us
  transfers between devices with their start and end apart: 18, of which 18 were waited for; matrix products, arithmetic and copies ran while one was open for 3% of the time, Pallas kernels for 0%

commit v1 on v0

--- a/solution.py
+++ b/solution.py
@@ -73,6 +73,11 @@
     ) + jnp.einsum("ctf,kjf->tkcj", second, partner[:, 1], preferred_element_type=jnp.float32)
 
 
+def in_blocks(array, dim, size):
+    before, after = (array.shape[:dim], array.shape[dim + 1 :])
+    return jnp.moveaxis(array.reshape(*before, size, -1, *after), dim, 0)
+
+
 def on_device(records, offsets, starts):
     n_chan = lax.axis_size("chan")
     groups = lax.axis_size("win")
@@ -81,33 +86,19 @@
     own_re, own_im = whiten(frames, dft_table(), taper_weights(), band_matrix())
     spectra = jnp.stack((own_re, own_im), axis=0)
 
-    down = [(i + 1, i) for i in range(n_chan - 1)]
-    jump = [((i + OFFCAP) % n_chan, i) for i in range(n_chan)]
-    up = [((i - 1) % n_chan, i) for i in range(n_chan)]
+    def shifted(by):
+        pairs = [(i + by, i) for i in range(n_chan - by)]
+        return lambda x: lax.ppermute(x, "chan", pairs)
 
-    near = jnp.minimum(offsets, OFFCAP - offsets)
-    steps = jnp.max(near)
-
-    def advance(carry):
-        step, low, high, picked = carry
-        step = step + 1
-        low = lax.ppermute(low, "chan", down)
-        high = lax.ppermute(high, "chan", up)
-        hit_low = offsets == step
-        hit_high = offsets == OFFCAP - step
-        picked = jnp.where(hit_low[:, None, None, None], low[None], picked)
-        picked = jnp.where(hit_high[:, None, None, None], high[None], picked)
-        return (step, low, high, picked)
-
-    high0 = lax.ppermute(spectra, "chan", jump)
-    empty = jnp.zeros((K,) + spectra.shape, jnp.bfloat16)
-    carry = (jnp.int32(0), spectra, high0, empty)
-    moved = lax.while_loop(lambda c: c[0] < steps, advance, carry)[3]
+    branches = [shifted(by) for by in range(1, OFFCAP)]
+    moved = jnp.stack(
+        [lax.switch(offsets[k] - 1, branches, spectra) for k in range(K)], axis=0
+    )
     cos_w, sin_w = phase_tables(groups)
     corr = lag_terms(own_re, own_im, moved, cos_w, sin_w)
-    summed = lax.psum_scatter(corr, "win", scatter_dimension=0, tiled=True)
-    valid = me + offsets < n_chan
-    return jnp.where(valid[None, :, None, None], summed, 0.0)
+    pieces = in_blocks(corr, 0, groups).astype(jnp.bfloat16)
+    arrived = lax.all_to_all(pieces, "win", split_axis=0, concat_axis=0, tiled=True)
+    return arrived.astype(jnp.float32).sum(axis=0)
 
 
 def solution(mesh):

time: 306 us -> 148 us (0.48)
  the two profiles are of different devices: /device:TPU:1 before, /device:TPU:241 now
where the time goes in v1:
time: 148 us; the launch traced here: 147 us
  waiting for transfers between devices  84.7 us (57%)
  blocking collectives  29.6 us (20%)
  matrix products  12.2 us (8%)
  starting transfers between devices  10.5 us (7%)
  other arithmetic  4.21 us (3%)
  between operations  3.25 us (2%)
  local copies, waits for them, and re-layouts  2.91 us (2%)
    ppermute x4, waiting for transfers between devices, shifted(): return lambda x: lax.ppermute(x, 'chan', pairs)  84.7 us
    all_to_all x1, blocking collectives, on_device(): lax.all_to_all(pieces, 'win', split_axis=0, concat_axis=0, tiled=True)  29.6 us
    ppermute x4, starting transfers between devices, shifted(): return lambda x: lax.ppermute(x, 'chan', pairs)  10.5 us
    dot_general x1, matrix products, whiten(): spec = jnp.dot(shaped, table, preferred_element_type=jnp.float32)  4.94 us
  transfers between devices with their start and end apart: 4, of which 4 were waited for; matrix products, arithmetic and copies ran while one was open for 0% of the time, Pallas kernels for 0%

profile of v1, /device:TPU:241, one launch (start us, length us, event | category | flops | bytes accessed | tf_op | source)
XLA Modules:
  0.0 147.4 jit_solution(13727611729091289136)
XLA Ops:
  0.0 0.2 convert_reduce_fusion
  0.2 0.1 multiply_subtract_fusion
  1.0 1.4 convert_reduce_fusion.2
  2.3 1.5 fusion.41
  6.3 4.9 %fusion.26 = f32[128,2048]{1,0:T(8,128)S(1)} fusion(bf16[2048,2048]{1,0:T(8,128)(2,1)} %constant.68.clone, f32[2048]{0:T(1024)S(1)} %multiply_subtract_fusion, f32[128]{0:T(128)S(1)} %broadcast_multiply_fusion, bf16[128,4096]{1,0:T(8,128)(2,1)} %param.64, s32[]{:T(128)S(6)} %select_n.37), kind=kOutput, calls=%fused_computation.37 | convolution fusion | flops 1074790400 | bytes 9970180 | tf_op jit(solution)/shard_map/dot_general | solution.py:57
  11.3 2.1 %fusion.39 = (f32[128,1024]{1,0:T(8,128)S(1)}, bf16[128,1024]{1,0:T(8,128)(2,1)S(1)}, f32[128,1024]{1,0:T(8,128)S(1)}, bf16[128,1024]{1,0:T(8,128)(2,1)S(1)}) fusion(f32[128,2048]{1,0:T(8,128)S(1)} %fusion.26, f32[1024]{0:T(1024)S(1)} %convert_reduce_fusion), kind=kOutput, calls=%fused_computation.59 | convolution fusion | flops 1617166336 | bytes 3674112 | tf_op jit(solution)/shard_map/dot_general | solution.py:61
  13.4 0.1 pad_maximum_fusion.1
  13.5 31.7 %conditional.7 = (bf16[1,2,128,1024]{3,2,1,0:T(8,128)(2,1)}) conditional(s32[]{:T(128)} %bitcast.69, bf16[2,128,1024]{2,1,0:T(8,128)(2,1)S(1)} %pad_maximum_fusion.1, bf16[2,128,1024]{2,1,0:T(8,128)(2,1)S(1)} %pad_maximum_fusion.1, bf16[2,128,1024]{2,1,0:T(8,128)(2,1)S(1)} %pad_maximum_fusion.1, ...), branch_computations={%region_47.0_spmd, %region_48.0_spmd, %region_49.0_spmd, %region_5... | conditional | bytes 2097200 | solution.py:95
  13.5 4.1 %collective-permute-start.53 = (bf16[2,128,1024]{2,1,0:T(8,128)(2,1)S(1)}, bf16[2,128,1024]{2,1,0:T(8,128)(2,1)}, u32[]{:S(2)}, u32[]{:S(2)}) collective-permute-start(bf16[2,128,1024]{2,1,0:T(8,128)(2,1)S(1)} %param.53), channel_id=1, source_target_pairs={{36,0},{40,4},{44,8},{48,12},{52,16},{56,20},{60,24},{64,28},{68,3... | collective-permute-start | bytes 1572872 | tf_op jit(solution)/shard_map/cond/branch_8_fun/ppermute | solution.py:91
  17.6 27.6 %collective-permute-done.53 = bf16[2,128,1024]{2,1,0:T(8,128)(2,1)} collective-permute-done((bf16[2,128,1024]{2,1,0:T(8,128)(2,1)S(1)}, bf16[2,128,1024]{2,1,0:T(8,128)(2,1)}, u32[]{:S(2)}, u32[]{:S(2)}) %collective-permute-start.53) | collective-permute-done | bytes 524320 | tf_op jit(solution)/shard_map/cond/branch_8_fun/ppermute | solution.py:91
  45.2 23.9 %conditional.6 = (bf16[1,2,128,1024]{3,2,1,0:T(8,128)(2,1)}) conditional(s32[]{:T(128)} %bitcast.67, bf16[2,128,1024]{2,1,0:T(8,128)(2,1)S(1)} %pad_maximum_fusion.1, bf16[2,128,1024]{2,1,0:T(8,128)(2,1)S(1)} %pad_maximum_fusion.1, bf16[2,128,1024]{2,1,0:T(8,128)(2,1)S(1)} %pad_maximum_fusion.1, ...), branch_computations={%region_32.0_spmd, %region_33.0_spmd, %region_34.0_spmd, %region_3... | conditional | bytes 2097200 | solution.py:95
  45.2 1.9 %collective-permute-start.44 = (bf16[2,128,1024]{2,1,0:T(8,128)(2,1)S(1)}, bf16[2,128,1024]{2,1,0:T(8,128)(2,1)}, u32[]{:S(2)}, u32[]{:S(2)}) collective-permute-start(bf16[2,128,1024]{2,1,0:T(8,128)(2,1)S(1)} %param.44), channel_id=1, source_target_pairs={{60,0},{64,4},{68,8},{72,12},{76,16},{80,20},{84,24},{88,28},{92,3... | collective-permute-start | bytes 1572872 | tf_op jit(solution)/shard_map/cond/branch_14_fun/ppermute | solution.py:91
  47.1 22.0 %collective-permute-done.44 = bf16[2,128,1024]{2,1,0:T(8,128)(2,1)} collective-permute-done((bf16[2,128,1024]{2,1,0:T(8,128)(2,1)S(1)}, bf16[2,128,1024]{2,1,0:T(8,128)(2,1)}, u32[]{:S(2)}, u32[]{:S(2)}) %collective-permute-start.44) | collective-permute-done | bytes 524320 | tf_op jit(solution)/shard_map/cond/branch_14_fun/ppermute | solution.py:91
  69.1 29.1 %conditional.5 = (bf16[1,2,128,1024]{3,2,1,0:T(8,128)(2,1)}) conditional(s32[]{:T(128)} %bitcast.65, bf16[2,128,1024]{2,1,0:T(8,128)(2,1)S(1)} %pad_maximum_fusion.1, bf16[2,128,1024]{2,1,0:T(8,128)(2,1)S(1)} %pad_maximum_fusion.1, bf16[2,128,1024]{2,1,0:T(8,128)(2,1)S(1)} %pad_maximum_fusion.1, ...), branch_computations={%region_17.0_spmd, %region_18.0_spmd, %region_19.0_spmd, %region_2... | conditional | bytes 2097200 | solution.py:95
  69.1 2.2 %collective-permute-start.22 = (bf16[2,128,1024]{2,1,0:T(8,128)(2,1)S(1)}, bf16[2,128,1024]{2,1,0:T(8,128)(2,1)}, u32[]{:S(2)}, u32[]{:S(2)}) collective-permute-start(bf16[2,128,1024]{2,1,0:T(8,128)(2,1)S(1)} %param.22), channel_id=1, source_target_pairs={{32,0},{36,4},{40,8},{44,12},{48,16},{52,20},{56,24},{60,28},{64,3... | collective-permute-start | bytes 1572872 | tf_op jit(solution)/shard_map/cond/branch_7_fun/ppermute | solution.py:91
  71.3 26.8 %collective-permute-done.22 = bf16[2,128,1024]{2,1,0:T(8,128)(2,1)} collective-permute-done((bf16[2,128,1024]{2,1,0:T(8,128)(2,1)S(1)}, bf16[2,128,1024]{2,1,0:T(8,128)(2,1)}, u32[]{:S(2)}, u32[]{:S(2)}) %collective-permute-start.22) | collective-permute-done | bytes 524320 | tf_op jit(solution)/shard_map/cond/branch_7_fun/ppermute | solution.py:91
  98.1 10.6 %conditional.4 = (bf16[1,2,128,1024]{3,2,1,0:T(8,128)(2,1)}) conditional(s32[]{:T(128)} %bitcast.60, bf16[2,128,1024]{2,1,0:T(8,128)(2,1)S(1)} %pad_maximum_fusion.1, bf16[2,128,1024]{2,1,0:T(8,128)(2,1)S(1)} %pad_maximum_fusion.1, bf16[2,128,1024]{2,1,0:T(8,128)(2,1)S(1)} %pad_maximum_fusion.1, ...), branch_computations={%region_2.0_spmd, %region_3.0_spmd, %region_4.0_spmd, %region_5.0_... | conditional | bytes 2097200 | solution.py:95
  98.1 2.3 %collective-permute-start = (bf16[2,128,1024]{2,1,0:T(8,128)(2,1)S(1)}, bf16[2,128,1024]{2,1,0:T(8,128)(2,1)}, u32[]{:S(2)}, u32[]{:S(2)}) collective-permute-start(bf16[2,128,1024]{2,1,0:T(8,128)(2,1)S(1)} %param), channel_id=1, source_target_pairs={{4,0},{8,4},{12,8},{16,12},{20,16},{24,20},{28,24},{32,28},{36,32}... | collective-permute-start | bytes 1572872 | tf_op jit(solution)/shard_map/cond/branch_0_fun/ppermute | solution.py:91
  100.4 8.3 %collective-permute-done = bf16[2,128,1024]{2,1,0:T(8,128)(2,1)} collective-permute-done((bf16[2,128,1024]{2,1,0:T(8,128)(2,1)S(1)}, bf16[2,128,1024]{2,1,0:T(8,128)(2,1)}, u32[]{:S(2)}, u32[]{:S(2)}) %collective-permute-start) | collective-permute-done | bytes 524320 | tf_op jit(solution)/shard_map/cond/branch_0_fun/ppermute | solution.py:91
  108.7 0.3 cosine_multiply_fusion
  109.1 1.8 %pad_maximum_fusion = bf16[4,2,128,1024]{3,2,0,1:T(8,128)(2,1)S(1)} fusion(bf16[1,2,128,1024]{3,2,0,1:T(8,128)(2,1)} %bitcast.70, bf16[1,2,128,1024]{3,2,0,1:T(8,128)(2,1)} %bitcast.68, bf16[1,2,128,1024]{3,2,0,1:T(8,128)(2,1)} %bitcast.66, bf16[1,2,128,1024]{3,2,0,1:T(8,128)(2,1)} %bitcast.64), kind=kLoop, calls=%fused_computation.20 | loop fusion | flops 3145728 | bytes 4194304 | tf_op jit(solution)/shard_map/stack | solution.py:94
  110.9 2.4 %fusion.1 = f32[4,128,128,16]{2,1,3,0:T(8,128)S(1)} fusion(f32[16,1024]{1,0:T(8,128)S(1)} %get-tuple-element.140, f32[128,1024]{1,0:T(8,128)S(1)} %get-tuple-element.137, f32[16,1024]{1,0:T(8,128)S(1)} %get-tuple-element.139, f32[128,1024]{1,0:T(8,128)S(1)} %get-tuple-element.133, bf16[4,2,128,1024]{3,2,0,1:T(8,128)(2,1)S(1)} %pad_maximum_fusion), kind=kOutput, calls=%fused_computation.5 | convolution fusion | flops 2155872256 | bytes 6422528 | tf_op jit(solution)/shard_map/ctf,kjf->tkcj/dot_general | solution.py:71
  113.3 2.7 %add_convert_fusion.1 = bf16[4,128,128,16]{2,1,3,0:T(8,128)(2,1)S(1)} fusion(f32[4,128,128,16]{2,1,3,0:T(8,128)S(1)} %fusion.1, f32[16,1024]{1,0:T(8,128)S(1)} %get-tuple-element.140, f32[128,1024]{1,0:T(8,128)S(1)} %get-tuple-element.137, f32[16,1024]{1,0:T(8,128)S(1)} %get-tuple-element.139, f32[128,1024]{1,0:T(8,128)S(1)} %get-tuple-element.133, ...), kind=kOutput, calls=%fused_computation.9 | convolution fusion | flops 2157969408 | bytes 8519680 | tf_op jit(solution)/shard_map/ctf,kjf->tkcj/dot_general | solution.py:73
  116.0 0.1 copy.20
  116.2 29.6 %all_to_all.5 = bf16[4,4,4,128,128]{3,4,1,2,0:T(8,128)(2,1)S(1)} all-to-all(bf16[4,4,4,128,128]{3,4,1,2,0:T(8,128)(2,1)S(1)} %copy.20), channel_id=1, replica_groups=mesh['chan'=128,'win'=4] {'win'}, dimensions={0} | all-to-all | bytes 4194304 | tf_op jit(solution)/shard_map/all_to_all | solution.py:100
  145.7 0.4 convert_reduce_fusion.1
  146.1 1.3 copy.22
  (3 shorter events, 0.0 us)
Async XLA Ops:
  13.5 31.7 %collective-permute-start.53 = (bf16[2,128,1024]{2,1,0:T(8,128)(2,1)S(1)}, bf16[2,128,1024]{2,1,0:T(8,128)(2,1)}, u32[]{:S(2)}, u32[]{:S(2)}) collective-permute-start(bf16[2,128,1024]{2,1,0:T(8,128)(2,1)S(1)} %param.53), channel_id=1, source_target_pairs={{36,0},{40,4},{44,8},{48,12},{52,16},{56,20},{60,24},{64,28},{68,3... | collective-permute-start | bytes 1572872 | tf_op jit(solution)/shard_map/cond/branch_8_fun/ppermute | solution.py:91
  45.2 23.9 %collective-permute-start.44 = (bf16[2,128,1024]{2,1,0:T(8,128)(2,1)S(1)}, bf16[2,128,1024]{2,1,0:T(8,128)(2,1)}, u32[]{:S(2)}, u32[]{:S(2)}) collective-permute-start(bf16[2,128,1024]{2,1,0:T(8,128)(2,1)S(1)} %param.44), channel_id=1, source_target_pairs={{60,0},{64,4},{68,8},{72,12},{76,16},{80,20},{84,24},{88,28},{92,3... | collective-permute-start | bytes 1572872 | tf_op jit(solution)/shard_map/cond/branch_14_fun/ppermute | solution.py:91
  69.1 29.1 %collective-permute-start.22 = (bf16[2,128,1024]{2,1,0:T(8,128)(2,1)S(1)}, bf16[2,128,1024]{2,1,0:T(8,128)(2,1)}, u32[]{:S(2)}, u32[]{:S(2)}) collective-permute-start(bf16[2,128,1024]{2,1,0:T(8,128)(2,1)S(1)} %param.22), channel_id=1, source_target_pairs={{32,0},{36,4},{40,8},{44,12},{48,16},{52,20},{56,24},{60,28},{64,3... | collective-permute-start | bytes 1572872 | tf_op jit(solution)/shard_map/cond/branch_7_fun/ppermute | solution.py:91
  98.1 10.6 %collective-permute-start = (bf16[2,128,1024]{2,1,0:T(8,128)(2,1)S(1)}, bf16[2,128,1024]{2,1,0:T(8,128)(2,1)}, u32[]{:S(2)}, u32[]{:S(2)}) collective-permute-start(bf16[2,128,1024]{2,1,0:T(8,128)(2,1)S(1)} %param), channel_id=1, source_target_pairs={{4,0},{8,4},{12,8},{16,12},{20,16},{24,20},{28,24},{32,28},{36,32}... | collective-permute-start | bytes 1572872 | tf_op jit(solution)/shard_map/cond/branch_0_fun/ppermute | solution.py:91

commit v2 on v1

--- a/solution.py
+++ b/solution.py
@@ -90,9 +90,15 @@
         pairs = [(i + by, i) for i in range(n_chan - by)]
         return lambda x: lax.ppermute(x, "chan", pairs)
 
-    branches = [shifted(by) for by in range(1, OFFCAP)]
+    far = OFFCAP - 1
+    farthest = shifted(far)(spectra)
+    branches = [shifted(by) for by in range(1, far)] + [jnp.zeros_like]
     moved = jnp.stack(
-        [lax.switch(offsets[k] - 1, branches, spectra) for k in range(K)], axis=0
+        [
+            jnp.where(offsets[k] == far, farthest, lax.switch(offsets[k] - 1, branches, spectra))
+            for k in range(K)
+        ],
+        axis=0,
     )
     cos_w, sin_w = phase_tables(groups)
     corr = lag_terms(own_re, own_im, moved, cos_w, sin_w)

time: 148 us -> 157 us (1.061)
  the two profiles are of different devices: /device:TPU:241 before, /device:TPU:208 now
where the time goes in v2:
time: 157 us
  waiting for transfers between devices  89.5 us (57%)
  blocking collectives  31.5 us (20%)
  matrix products  12.1 us (8%)
  starting transfers between devices  9.92 us (6%)
  between operations  5.74 us (4%)
  other arithmetic  5 us (3%)
  local copies, waits for them, and re-layouts  2.97 us (2%)
    ppermute x4, waiting for transfers between devices, shifted(): return lambda x: lax.ppermute(x, 'chan', pairs)  89.5 us
    all_to_all x1, blocking collectives, on_device(): lax.all_to_all(pieces, 'win', split_axis=0, concat_axis=0, tiled=True)  31.5 us
    ppermute x4, starting transfers between devices, shifted(): return lambda x: lax.ppermute(x, 'chan', pairs)  9.92 us
    dot_general x1, matrix products, whiten(): spec = jnp.dot(shaped, table, preferred_element_type=jnp.float32)  4.94 us
  transfers between devices with their start and end apart: 4, of which 3 were waited for; matrix products, arithmetic and copies ran while one was open for 1% of the time, Pallas kernels for 0%

profile of v2, /device:TPU:208, one launch (start us, length us, event | category | flops | bytes accessed | tf_op | source)
XLA Modules:
  0.0 156.8 jit_solution(8585036637999779590)
XLA Ops:
  0.0 0.2 convert_reduce_fusion
  0.2 0.1 multiply_subtract_fusion
  0.9 1.4 convert_reduce_fusion.2
  2.3 4.9 %fusion.26 = f32[128,2048]{1,0:T(8,128)S(1)} fusion(bf16[2048,2048]{1,0:T(8,128)(2,1)} %constant.82.clone, f32[2048]{0:T(1024)S(1)} %multiply_subtract_fusion, f32[128]{0:T(128)S(1)} %broadcast_multiply_fusion, bf16[128,4096]{1,0:T(8,128)(2,1)} %param.64, s32[]{:T(128)S(6)} %select_n.64), kind=kOutput, calls=%fused_computation.41 | convolution fusion | flops 1074790400 | bytes 9970180 | tf_op jit(solution)/shard_map/dot_general | solution.py:57
  7.2 0.0 copy-start
  7.3 2.1 %fusion.39 = (f32[128,1024]{1,0:T(8,128)S(1)}, bf16[128,1024]{1,0:T(8,128)(2,1)S(1)}, f32[128,1024]{1,0:T(8,128)S(1)}, bf16[128,1024]{1,0:T(8,128)(2,1)S(1)}) fusion(f32[128,2048]{1,0:T(8,128)S(1)} %fusion.26, f32[1024]{0:T(1024)S(1)} %convert_reduce_fusion), kind=kOutput, calls=%fused_computation.63 | convolution fusion | flops 1617166336 | bytes 3674112 | tf_op jit(solution)/shard_map/dot_general | solution.py:61
  9.4 0.8 pad_maximum_fusion.1
  10.2 1.9 %collective-permute-start.56 = (bf16[2,128,1024]{2,1,0:T(8,128)(2,1)}, bf16[2,128,1024]{2,1,0:T(8,128)(2,1)S(1)}, u32[]{:S(2)}, u32[]{:S(2)}) collective-permute-start(bf16[2,128,1024]{2,1,0:T(8,128)(2,1)} %pad_maximum_fusion.1), channel_id=1, source_target_pairs={{60,0},{64,4},{68,8},{72,12},{76,16},{80,20},{84,24},{88,28},{92,3... | collective-permute-start | bytes 1572872 | tf_op jit(solution)/shard_map/ppermute | solution.py:91
  12.2 0.0 copy-done
  12.2 0.7 fusion.41
  17.8 22.7 %conditional.7 = (bf16[2,128,1024]{2,1,0:T(8,128)(2,1)}) conditional(s32[]{:T(128)} %bitcast.13, bf16[2,128,1024]{2,1,0:T(8,128)(2,1)} %pad_maximum_fusion.1, bf16[2,128,1024]{2,1,0:T(8,128)(2,1)} %pad_maximum_fusion.1, bf16[2,128,1024]{2,1,0:T(8,128)(2,1)} %pad_maximum_fusion.1, ...), branch_computations={%region_47.48_spmd, %region_48.49_spmd, %region_49.50_spmd, %regio... | conditional | bytes 2097200 | solution.py:98
  17.8 2.6 %collective-permute-start.44 = (bf16[2,128,1024]{2,1,0:T(8,128)(2,1)}, bf16[2,128,1024]{2,1,0:T(8,128)(2,1)}, u32[]{:S(2)}, u32[]{:S(2)}) collective-permute-start(bf16[2,128,1024]{2,1,0:T(8,128)(2,1)} %param.47), channel_id=1, source_target_pairs={{12,0},{16,4},{20,8},{24,12},{28,16},{32,20},{36,24},{40,28},{44,3... | collective-permute-start | bytes 1572872 | tf_op jit(solution)/shard_map/cond/branch_2_fun/ppermute | solution.py:91
  20.5 20.0 %collective-permute-done.44 = bf16[2,128,1024]{2,1,0:T(8,128)(2,1)} collective-permute-done((bf16[2,128,1024]{2,1,0:T(8,128)(2,1)}, bf16[2,128,1024]{2,1,0:T(8,128)(2,1)}, u32[]{:S(2)}, u32[]{:S(2)}) %collective-permute-start.44) | collective-permute-done | bytes 524320 | tf_op jit(solution)/shard_map/cond/branch_2_fun/ppermute | solution.py:91
  40.5 40.8 %conditional.6 = (bf16[2,128,1024]{2,1,0:T(8,128)(2,1)}) conditional(s32[]{:T(128)} %bitcast.10, bf16[2,128,1024]{2,1,0:T(8,128)(2,1)} %pad_maximum_fusion.1, bf16[2,128,1024]{2,1,0:T(8,128)(2,1)} %pad_maximum_fusion.1, bf16[2,128,1024]{2,1,0:T(8,128)(2,1)} %pad_maximum_fusion.1, ...), branch_computations={%region_32.33_spmd, %region_33.34_spmd, %region_34.35_spmd, %regio... | conditional | bytes 2097200 | solution.py:98
  40.5 3.5 %collective-permute-start.37 = (bf16[2,128,1024]{2,1,0:T(8,128)(2,1)}, bf16[2,128,1024]{2,1,0:T(8,128)(2,1)}, u32[]{:S(2)}, u32[]{:S(2)}) collective-permute-start(bf16[2,128,1024]{2,1,0:T(8,128)(2,1)} %param.39), channel_id=1, source_target_pairs={{40,0},{44,4},{48,8},{52,12},{56,16},{60,20},{64,24},{68,28},{72,3... | collective-permute-start | bytes 1572872 | tf_op jit(solution)/shard_map/cond/branch_9_fun/ppermute | solution.py:91
  44.0 37.3 %collective-permute-done.37 = bf16[2,128,1024]{2,1,0:T(8,128)(2,1)} collective-permute-done((bf16[2,128,1024]{2,1,0:T(8,128)(2,1)}, bf16[2,128,1024]{2,1,0:T(8,128)(2,1)}, u32[]{:S(2)}, u32[]{:S(2)}) %collective-permute-start.37) | collective-permute-done | bytes 524320 | tf_op jit(solution)/shard_map/cond/branch_9_fun/ppermute | solution.py:91
  81.3 0.9 conditional.5
  81.3 0.9 broadcast.149
  82.1 34.1 %conditional.4 = (bf16[2,128,1024]{2,1,0:T(8,128)(2,1)}) conditional(s32[]{:T(128)} %bitcast.4, bf16[2,128,1024]{2,1,0:T(8,128)(2,1)} %pad_maximum_fusion.1, bf16[2,128,1024]{2,1,0:T(8,128)(2,1)} %pad_maximum_fusion.1, bf16[2,128,1024]{2,1,0:T(8,128)(2,1)} %pad_maximum_fusion.1, ...), branch_computations={%region_2.0_spmd, %region_3.0_spmd, %region_4.0_spmd, %region_5.0_... | conditional | bytes 2097200 | solution.py:98
  82.1 1.9 %collective-permute-start.4 = (bf16[2,128,1024]{2,1,0:T(8,128)(2,1)}, bf16[2,128,1024]{2,1,0:T(8,128)(2,1)}, u32[]{:S(2)}, u32[]{:S(2)}) collective-permute-start(bf16[2,128,1024]{2,1,0:T(8,128)(2,1)} %param.4), channel_id=1, source_target_pairs={{20,0},{24,4},{28,8},{32,12},{36,16},{40,20},{44,24},{48,28},{52,3... | collective-permute-start | bytes 1572872 | tf_op jit(solution)/shard_map/cond/branch_4_fun/ppermute | solution.py:91
  84.0 32.2 %collective-permute-done.4 = bf16[2,128,1024]{2,1,0:T(8,128)(2,1)} collective-permute-done((bf16[2,128,1024]{2,1,0:T(8,128)(2,1)}, bf16[2,128,1024]{2,1,0:T(8,128)(2,1)}, u32[]{:S(2)}, u32[]{:S(2)}) %collective-permute-start.4) | collective-permute-done | bytes 524320 | tf_op jit(solution)/shard_map/cond/branch_4_fun/ppermute | solution.py:91
  116.3 0.3 cosine_multiply_fusion
  116.6 0.0 collective-permute-done.56
  116.6 1.5 select_bitcast_fusion.3
  118.2 0.3 pad_maximum_fusion
  118.4 2.4 %fusion.1 = f32[4,128,128,16]{2,1,3,0:T(8,128)S(1)} fusion(f32[16,1024]{1,0:T(8,128)S(1)} %get-tuple-element.136, f32[128,1024]{1,0:T(8,128)S(1)} %get-tuple-element.129, f32[16,1024]{1,0:T(8,128)S(1)} %get-tuple-element.135, f32[128,1024]{1,0:T(8,128)S(1)} %get-tuple-element.125, bf16[4,2,128,1024]{3,2,1,0:T(8,128)(2,1)S(1)} %pad_maximum_fusion), kind=kOutput, calls=%fused_computation.5 | convolution fusion | flops 2155872256 | bytes 6422528 | tf_op jit(solution)/shard_map/ctf,kjf->tkcj/dot_general | solution.py:71
  120.8 2.7 %add_convert_fusion.1 = bf16[4,128,128,16]{2,1,3,0:T(8,128)(2,1)S(1)} fusion(f32[4,128,128,16]{2,1,3,0:T(8,128)S(1)} %fusion.1, f32[16,1024]{1,0:T(8,128)S(1)} %get-tuple-element.136, f32[128,1024]{1,0:T(8,128)S(1)} %get-tuple-element.129, f32[16,1024]{1,0:T(8,128)S(1)} %get-tuple-element.135, f32[128,1024]{1,0:T(8,128)S(1)} %get-tuple-element.125, ...), kind=kOutput, calls=%fused_computation.9 | convolution fusion | flops 2157969408 | bytes 8519680 | tf_op jit(solution)/shard_map/ctf,kjf->tkcj/dot_general | solution.py:73
  123.5 0.1 copy.8
  123.6 31.5 %all_to_all.5 = bf16[4,4,4,128,128]{3,4,1,2,0:T(8,128)(2,1)S(1)} all-to-all(bf16[4,4,4,128,128]{3,4,1,2,0:T(8,128)(2,1)S(1)} %copy.8), channel_id=1, replica_groups=mesh['chan'=128,'win'=4] {'win'}, dimensions={0} | all-to-all | bytes 4194304 | tf_op jit(solution)/shard_map/all_to_all | solution.py:106
  155.1 0.4 convert_reduce_fusion.1
  155.5 1.3 copy.10
  (3 shorter events, 0.0 us)
Async XLA Ops:
  7.2 4.9 %copy-start = (s32[4]{0:T(128)S(1)}, s32[4]{0:T(128)}, u32[]{:S(2)}) copy-start(s32[4]{0:T(128)} %param.65) | copy-start | bytes 52
  10.2 106.4 %collective-permute-start.56 = (bf16[2,128,1024]{2,1,0:T(8,128)(2,1)}, bf16[2,128,1024]{2,1,0:T(8,128)(2,1)S(1)}, u32[]{:S(2)}, u32[]{:S(2)}) collective-permute-start(bf16[2,128,1024]{2,1,0:T(8,128)(2,1)} %pad_maximum_fusion.1), channel_id=1, source_target_pairs={{60,0},{64,4},{68,8},{72,12},{76,16},{80,20},{84,24},{88,28},{92,3... | collective-permute-start | bytes 1572872 | tf_op jit(solution)/shard_map/ppermute | solution.py:91
  17.8 22.7 %collective-permute-start.44 = (bf16[2,128,1024]{2,1,0:T(8,128)(2,1)}, bf16[2,128,1024]{2,1,0:T(8,128)(2,1)}, u32[]{:S(2)}, u32[]{:S(2)}) collective-permute-start(bf16[2,128,1024]{2,1,0:T(8,128)(2,1)} %param.47), channel_id=1, source_target_pairs={{12,0},{16,4},{20,8},{24,12},{28,16},{32,20},{36,24},{40,28},{44,3... | collective-permute-start | bytes 1572872 | tf_op jit(solution)/shard_map/cond/branch_2_fun/ppermute | solution.py:91
  40.5 40.8 %collective-permute-start.37 = (bf16[2,128,1024]{2,1,0:T(8,128)(2,1)}, bf16[2,128,1024]{2,1,0:T(8,128)(2,1)}, u32[]{:S(2)}, u32[]{:S(2)}) collective-permute-start(bf16[2,128,1024]{2,1,0:T(8,128)(2,1)} %param.39), channel_id=1, source_target_pairs={{40,0},{44,4},{48,8},{52,12},{56,16},{60,20},{64,24},{68,28},{72,3... | collective-permute-start | bytes 1572872 | tf_op jit(solution)/shard_map/cond/branch_9_fun/ppermute | solution.py:91
  82.1 34.1 %collective-permute-start.4 = (bf16[2,128,1024]{2,1,0:T(8,128)(2,1)}, bf16[2,128,1024]{2,1,0:T(8,128)(2,1)}, u32[]{:S(2)}, u32[]{:S(2)}) collective-permute-start(bf16[2,128,1024]{2,1,0:T(8,128)(2,1)} %param.4), channel_id=1, source_target_pairs={{20,0},{24,4},{28,8},{32,12},{36,16},{40,20},{44,24},{48,28},{52,3... | collective-permute-start | bytes 1572872 | tf_op jit(solution)/shard_map/cond/branch_4_fun/ppermute | solution.py:91

commit v3 on v1

--- a/solution.py
+++ b/solution.py
@@ -63,14 +63,45 @@
     return ((real / level).astype(jnp.bfloat16), (imag / level).astype(jnp.bfloat16))
 
 
-def lag_terms(own_re, own_im, partner, cos_w, sin_w):
+def lag_factors(own_re, own_im, cos_w, sin_w):
     ar = own_re.astype(jnp.float32)[:, None, :]
     ai = own_im.astype(jnp.float32)[:, None, :]
     first = (ar * cos_w[None] - ai * sin_w[None]).astype(jnp.bfloat16)
     second = (ar * sin_w[None] + ai * cos_w[None]).astype(jnp.bfloat16)
+    return first, second
+
+
+def lag_terms(first, second, partner):
     return jnp.einsum(
-        "ctf,kjf->tkcj", first, partner[:, 0], preferred_element_type=jnp.float32
-    ) + jnp.einsum("ctf,kjf->tkcj", second, partner[:, 1], preferred_element_type=jnp.float32)
+        "ctf,jf->tcj", first, partner[0], preferred_element_type=jnp.float32
+    ) + jnp.einsum("ctf,jf->tcj", second, partner[1], preferred_element_type=jnp.float32)
+
+
+def split_for_win(corr):
+    groups = lax.axis_size("win")
+    me = lax.axis_index("win")
+    pieces = corr.reshape(groups, -1, *corr.shape[1:])
+    own = lax.dynamic_index_in_dim(pieces, me, 0, keepdims=False)
+    sent = [
+        lax.dynamic_index_in_dim(pieces, (me + by) % groups, 0, keepdims=False).astype(jnp.bfloat16)
+        for by in range(1, groups)
+    ]
+    return own, sent
+
+
+def pass_over_win(sent):
+    groups = lax.axis_size("win")
+    return [
+        lax.ppermute(piece, "win", [(w, (w + by) % groups) for w in range(groups)])
+        for by, piece in enumerate(sent, start=1)
+    ]
+
+
+def sum_over_win(own, arrived):
+    total = own
+    for piece in arrived:
+        total = total + piece.astype(jnp.float32)
+    return total
 
 
 def in_blocks(array, dim, size):
@@ -90,15 +121,27 @@
         pairs = [(i + by, i) for i in range(n_chan - by)]
         return lambda x: lax.ppermute(x, "chan", pairs)
 
-    branches = [shifted(by) for by in range(1, OFFCAP)]
-    moved = jnp.stack(
-        [lax.switch(offsets[k] - 1, branches, spectra) for k in range(K)], axis=0
-    )
+    def with_win(move):
+        return lambda x, sent: (move(x), pass_over_win(sent))
+
+    far = OFFCAP - 1
+    farthest = shifted(far)(spectra)
+    moves = [shifted(by) for by in range(1, far)] + [jnp.zeros_like]
+    paired = [with_win(move) for move in moves]
     cos_w, sin_w = phase_tables(groups)
-    corr = lag_terms(own_re, own_im, moved, cos_w, sin_w)
-    pieces = in_blocks(corr, 0, groups).astype(jnp.bfloat16)
-    arrived = lax.all_to_all(pieces, "win", split_axis=0, concat_axis=0, tiled=True)
-    return arrived.astype(jnp.float32).sum(axis=0)
+    first, second = lag_factors(own_re, own_im, cos_w, sin_w)
+    parts = []
+    pending = None
+    for k in range(K):
+        if pending is None:
+            moved = lax.switch(offsets[k] - 1, moves, spectra)
+        else:
+            moved, arrived = lax.switch(offsets[k] - 1, paired, spectra, pending[1])
+            parts.append(sum_over_win(pending[0], arrived))
+        partner = jnp.where(offsets[k] == far, farthest, moved)
+        pending = split_for_win(lag_terms(first, second, partner))
+    parts.append(sum_over_win(pending[0], pass_over_win(pending[1])))
+    return jnp.stack(parts, axis=1)
 
 
 def solution(mesh):

time: 148 us -> 163 us (1.10)
  the two profiles are of different devices: /device:TPU:241 before, /device:TPU:224 now
where the time goes in v3:
time: 163 us; the launch traced here: 162 us
  waiting for transfers between devices  60.4 us (37%)
  starting transfers between devices  54.3 us (33%)
  matrix products  25.4 us (16%)
  other arithmetic  9.97 us (6%)
  between operations  6.33 us (4%)
  local copies, waits for them, and re-layouts  5.37 us (3%)
    ppermute x4, waiting for transfers between devices, shifted(): return lambda x: lax.ppermute(x, 'chan', pairs)  48.8 us
    ppermute x12, starting transfers between devices, pass_over_win(): lax.ppermute(piece, 'win', [(w, (w + by) % groups) for w in range(groups)])  45.4 us
    ppermute x12, waiting for transfers between devices, pass_over_win(): lax.ppermute(piece, 'win', [(w, (w + by) % groups) for w in range(groups)])  11.6 us
    dot_general x4, matrix products, lag_terms(): jnp.einsum('ctf,jf->tcj', second, partner[1], preferred_element_type=jnp....  9.76 us
    ppermute x4, starting transfers between devices, shifted(): return lambda x: lax.ppermute(x, 'chan', pairs)  8.92 us
    dot_general x4, matrix products, lag_terms(): jnp.einsum('ctf,jf->tcj', first, partner[0], preferred_element_type=jnp.f...  8.6 us
    dot_general x1, matrix products, whiten(): spec = jnp.dot(shaped, table, preferred_element_type=jnp.float32)  4.94 us
    another operation x5, other arithmetic, on_device(): return jnp.stack(parts, axis=1)  4.39 us
  transfers between devices with their start and end apart: 16, of which 11 were waited for; matrix products, arithmetic and copies ran while one was open for 3% of the time, Pallas kernels for 0%

profile of v3, /device:TPU:224, one launch (start us, length us, event | category | flops | bytes accessed | tf_op | source)
XLA Modules:
  0.0 162.2 jit_solution(5518811348665481642)
XLA Ops:
  2.3 4.9 %fusion.54 = f32[128,2048]{1,0:T(8,128)S(1)} fusion(bf16[2048,2048]{1,0:T(8,128)(2,1)} %constant.162.clone, f32[2048]{0:T(1024)S(1)} %multiply_subtract_fusion, f32[128]{0:T(128)S(1)} %broadcast_multiply_fusion, bf16[128,4096]{1,0:T(8,128)(2,1)} %param.64, s32[]{:T(128)S(6)} %select_n.121), kind=kOutput, calls=%fused_computation.69 | convolution fusion | flops 1074790400 | bytes 9970180 | tf_op jit(solution)/shard_map/dot_general | solution.py:57
  7.3 2.1 %fusion.73 = (f32[128,1024]{1,0:T(8,128)S(1)}, bf16[128,1024]{1,0:T(8,128)(2,1)S(1)}, f32[128,1024]{1,0:T(8,128)S(1)}, bf16[128,1024]{1,0:T(8,128)(2,1)S(1)}) fusion(f32[128,2048]{1,0:T(8,128)S(1)} %fusion.54, f32[1024]{0:T(1024)S(1)} %convert_reduce_fusion), kind=kOutput, calls=%fused_computation.143 | convolution fusion | flops 1617166336 | bytes 3674112 | tf_op jit(solution)/shard_map/dot_general | solution.py:61
  9.5 1.9 %collective-permute-start.191 = (bf16[2,128,1024]{2,1,0:T(8,128)(2,1)S(1)}, bf16[2,128,1024]{2,1,0:T(8,128)(2,1)S(1)}, u32[]{:S(2)}, u32[]{:S(2)}) collective-permute-start(bf16[2,128,1024]{2,1,0:T(8,128)(2,1)S(1)} %pad_maximum_fusion.1), channel_id=1, source_target_pairs={{60,0},{64,4},{68,8},{72,12},{76,16},{80,20},{84,24},{88,28},{92,3... | collective-permute-start | bytes 1572872 | tf_op jit(solution)/shard_map/ppermute | solution.py:122
  18.6 5.1 %collective-permute-done.191 = bf16[2,128,1024]{2,1,0:T(8,128)(2,1)S(1)} collective-permute-done((bf16[2,128,1024]{2,1,0:T(8,128)(2,1)S(1)}, bf16[2,128,1024]{2,1,0:T(8,128)(2,1)S(1)}, u32[]{:S(2)}, u32[]{:S(2)}) %collective-permute-start.191) | collective-permute-done | bytes 524320 | tf_op jit(solution)/shard_map/ppermute | solution.py:122
  25.4 2.7 %fusion.43 = f32[128,128,16]{1,0,2:T(8,128)S(1)} fusion(f32[128,128,16]{1,0,2:T(8,128)S(1)} %fusion.7, f32[16,1024]{1,0:T(8,128)S(1)} %get-tuple-element.699, f32[128,1024]{1,0:T(8,128)} %copy-done.10, f32[16,1024]{1,0:T(8,128)S(1)} %get-tuple-element.698, f32[128,1024]{1,0:T(8,128)} %copy-done.7, bf16[2,128,1024]{2,1,0:T(8,128)(2,1)S(1)} %broadcast_select_fusion.3), kind=kOutput, calls=%fused_computation.48 | convolution fusion | flops 545521664 | bytes 3538944 | tf_op jit(solution)/shard_map/ctf,jf->tcj/dot_general | solution.py:75
  28.6 24.2 %conditional.14 = (bf16[2,128,1024]{2,1,0:T(8,128)(2,1)}, bf16[4,128,128]{2,1,0:T(8,128)(2,1)}, bf16[4,128,128]{2,1,0:T(8,128)(2,1)}, bf16[4,128,128]{2,1,0:T(8,128)(2,1)}) conditional(s32[]{:T(128)} %bitcast.12, (bf16[2,128,1024]{2,1,0:T(8,128)(2,1)S(1)}, bf16[4,128,128]{2,1,0:T(8,128)(2,1)S(1)}, ...), branch_computations={%region_17.18_spmd, %region_18.19_spmd, %region_19.20_spmd, %regio... | conditional | bytes 3670208
  28.6 1.9 %collective-permute-start.58 = (bf16[2,128,1024]{2,1,0:T(8,128)(2,1)S(1)}, bf16[2,128,1024]{2,1,0:T(8,128)(2,1)}, u32[]{:S(2)}, u32[]{:S(2)}) collective-permute-start(bf16[2,128,1024]{2,1,0:T(8,128)(2,1)S(1)} %get-tuple-element.493), channel_id=1, source_target_pairs={{48,0},{52,4},{56,8},{60,12},{64,16},{68,20},{72,24},{76,28},{80,3... | collective-permute-start | bytes 1572872 | tf_op jit(solution)/shard_map/cond/branch_11_fun/ppermute | solution.py:122
  30.6 3.4 %collective-permute-start.59 = (bf16[4,128,128]{2,1,0:T(8,128)(2,1)S(1)}, bf16[4,128,128]{2,1,0:T(8,128)(2,1)}, u32[]{:S(2)}, u32[]{:S(2)}) collective-permute-start(bf16[4,128,128]{2,1,0:T(8,128)(2,1)S(1)} %get-tuple-element.494), channel_id=1, source_target_pairs={{0,1},{1,2},{2,3},{3,0},{4,5},{5,6},{6,7},{7,4},{8,9},{9,10},{10,1... | collective-permute-start | bytes 393224 | tf_op jit(solution)/shard_map/cond/branch_11_fun/ppermute | solution.py:95
  34.0 4.7 %collective-permute-start.60 = (bf16[4,128,128]{2,1,0:T(8,128)(2,1)S(1)}, bf16[4,128,128]{2,1,0:T(8,128)(2,1)}, u32[]{:S(2)}, u32[]{:S(2)}) collective-permute-start(bf16[4,128,128]{2,1,0:T(8,128)(2,1)S(1)} %get-tuple-element.495), channel_id=1, source_target_pairs={{0,2},{1,3},{2,0},{3,1},{4,6},{5,7},{6,4},{7,5},{8,10},{9,11},{10,... | collective-permute-start | bytes 393224 | tf_op jit(solution)/shard_map/cond/branch_11_fun/ppermute | solution.py:95
  38.6 3.3 %collective-permute-start.61 = (bf16[4,128,128]{2,1,0:T(8,128)(2,1)S(1)}, bf16[4,128,128]{2,1,0:T(8,128)(2,1)}, u32[]{:S(2)}, u32[]{:S(2)}) collective-permute-start(bf16[4,128,128]{2,1,0:T(8,128)(2,1)S(1)} %get-tuple-element.496), channel_id=1, source_target_pairs={{0,3},{1,0},{2,1},{3,2},{4,7},{5,4},{6,5},{7,6},{8,11},{9,8},{10,9... | collective-permute-start | bytes 393224 | tf_op jit(solution)/shard_map/cond/branch_11_fun/ppermute | solution.py:95
  43.6 2.0 %collective-permute-done.61 = bf16[4,128,128]{2,1,0:T(8,128)(2,1)} collective-permute-done((bf16[4,128,128]{2,1,0:T(8,128)(2,1)S(1)}, bf16[4,128,128]{2,1,0:T(8,128)(2,1)}, u32[]{:S(2)}, u32[]{:S(2)}) %collective-permute-start.61) | collective-permute-done | bytes 131104 | tf_op jit(solution)/shard_map/cond/branch_11_fun/ppermute | solution.py:95
  45.6 7.2 %collective-permute-done.58 = bf16[2,128,1024]{2,1,0:T(8,128)(2,1)} collective-permute-done((bf16[2,128,1024]{2,1,0:T(8,128)(2,1)S(1)}, bf16[2,128,1024]{2,1,0:T(8,128)(2,1)}, u32[]{:S(2)}, u32[]{:S(2)}) %collective-permute-start.58) | collective-permute-done | bytes 524320 | tf_op jit(solution)/shard_map/cond/branch_11_fun/ppermute | solution.py:122
  54.0 2.7 %fusion.6 = f32[128,128,16]{1,0,2:T(8,128)S(1)} fusion(f32[16,1024]{1,0:T(8,128)S(1)} %get-tuple-element.699, f32[128,1024]{1,0:T(8,128)} %copy-done.10, f32[16,1024]{1,0:T(8,128)S(1)} %get-tuple-element.698, f32[128,1024]{1,0:T(8,128)} %copy-done.7, bf16[2,128,1024]{2,1,0:T(8,128)(2,1)S(1)} %broadcast_select_fusion.2), kind=kOutput, calls=%fused_computation.8 | convolution fusion | flops 545259520 | bytes 2490368 | tf_op jit(solution)/shard_map/ctf,jf->tcj/dot_general | solution.py:77
  60.2 39.0 %conditional.15 = (bf16[2,128,1024]{2,1,0:T(8,128)(2,1)}, bf16[4,128,128]{2,1,0:T(8,128)(2,1)}, bf16[4,128,128]{2,1,0:T(8,128)(2,1)}, bf16[4,128,128]{2,1,0:T(8,128)(2,1)}) conditional(s32[]{:T(128)} %bitcast.26, (bf16[2,128,1024]{2,1,0:T(8,128)(2,1)S(1)}, bf16[4,128,128]{2,1,0:T(8,128)(2,1)}, ...), branch_computations={%region_32.33_spmd, %region_33.34_spmd, %region_34.35_spmd, %regio... | conditional | bytes 3670208
  60.2 3.2 %collective-permute-start.113 = (bf16[2,128,1024]{2,1,0:T(8,128)(2,1)S(1)}, bf16[2,128,1024]{2,1,0:T(8,128)(2,1)}, u32[]{:S(2)}, u32[]{:S(2)}) collective-permute-start(bf16[2,128,1024]{2,1,0:T(8,128)(2,1)S(1)} %get-tuple-element.548), channel_id=1, source_target_pairs={{44,0},{48,4},{52,8},{56,12},{60,16},{64,20},{68,24},{72,28},{76,3... | collective-permute-start | bytes 1572872 | tf_op jit(solution)/shard_map/cond/branch_10_fun/ppermute | solution.py:122
  63.3 3.4 %collective-permute-start.114 = (bf16[4,128,128]{2,1,0:T(8,128)(2,1)}, bf16[4,128,128]{2,1,0:T(8,128)(2,1)}, u32[]{:S(2)}, u32[]{:S(2)}) collective-permute-start(bf16[4,128,128]{2,1,0:T(8,128)(2,1)} %get-tuple-element.549), channel_id=1, source_target_pairs={{0,1},{1,2},{2,3},{3,0},{4,5},{5,6},{6,7},{7,4},{8,9},{9,10},{10,1... | collective-permute-start | bytes 393224 | tf_op jit(solution)/shard_map/cond/branch_10_fun/ppermute | solution.py:95
  66.7 4.7 %collective-permute-start.115 = (bf16[4,128,128]{2,1,0:T(8,128)(2,1)S(1)}, bf16[4,128,128]{2,1,0:T(8,128)(2,1)}, u32[]{:S(2)}, u32[]{:S(2)}) collective-permute-start(bf16[4,128,128]{2,1,0:T(8,128)(2,1)S(1)} %get-tuple-element.550), channel_id=1, source_target_pairs={{0,2},{1,3},{2,0},{3,1},{4,6},{5,7},{6,4},{7,5},{8,10},{9,11},{10,... | collective-permute-start | bytes 393224 | tf_op jit(solution)/shard_map/cond/branch_10_fun/ppermute | solution.py:95
  71.4 3.3 %collective-permute-start.116 = (bf16[4,128,128]{2,1,0:T(8,128)(2,1)}, bf16[4,128,128]{2,1,0:T(8,128)(2,1)}, u32[]{:S(2)}, u32[]{:S(2)}) collective-permute-start(bf16[4,128,128]{2,1,0:T(8,128)(2,1)} %get-tuple-element.551), channel_id=1, source_target_pairs={{0,3},{1,0},{2,1},{3,2},{4,7},{5,4},{6,5},{7,6},{8,11},{9,8},{10,9... | collective-permute-start | bytes 393224 | tf_op jit(solution)/shard_map/cond/branch_10_fun/ppermute | solution.py:95
  75.2 3.7 %collective-permute-done.116 = bf16[4,128,128]{2,1,0:T(8,128)(2,1)} collective-permute-done((bf16[4,128,128]{2,1,0:T(8,128)(2,1)}, bf16[4,128,128]{2,1,0:T(8,128)(2,1)}, u32[]{:S(2)}, u32[]{:S(2)}) %collective-permute-start.116) | collective-permute-done | bytes 131104 | tf_op jit(solution)/shard_map/cond/branch_10_fun/ppermute | solution.py:95
  78.9 20.2 %collective-permute-done.113 = bf16[2,128,1024]{2,1,0:T(8,128)(2,1)} collective-permute-done((bf16[2,128,1024]{2,1,0:T(8,128)(2,1)S(1)}, bf16[2,128,1024]{2,1,0:T(8,128)(2,1)}, u32[]{:S(2)}, u32[]{:S(2)}) %collective-permute-start.113) | collective-permute-done | bytes 524320 | tf_op jit(solution)/shard_map/cond/branch_10_fun/ppermute | solution.py:122
  100.3 2.8 %fusion.5 = f32[128,128,16]{1,0,2:T(8,128)S(1)} fusion(f32[16,1024]{1,0:T(8,128)} %copy-done.3, f32[128,1024]{1,0:T(8,128)} %copy-done.10, f32[16,1024]{1,0:T(8,128)} %copy-done, f32[128,1024]{1,0:T(8,128)} %copy-done.7, bf16[2,128,1024]{2,1,0:T(8,128)(2,1)S(1)} %broadcast_select_fusion.1), kind=kOutput, calls=%fused_computation.7 | convolution fusion | flops 545259520 | bytes 2490368 | tf_op jit(solution)/shard_map/ctf,jf->tcj/dot_general | solution.py:77
  105.3 33.4 %conditional.16 = (bf16[2,128,1024]{2,1,0:T(8,128)(2,1)}, bf16[4,128,128]{2,1,0:T(8,128)(2,1)}, bf16[4,128,128]{2,1,0:T(8,128)(2,1)}, bf16[4,128,128]{2,1,0:T(8,128)(2,1)}) conditional(s32[]{:T(128)} %bitcast.40, (bf16[2,128,1024]{2,1,0:T(8,128)(2,1)S(1)}, bf16[4,128,128]{2,1,0:T(8,128)(2,1)S(1)}, ...), branch_computations={%region_47.48_spmd, %region_48.49_spmd, %region_49.50_spmd, %regio... | conditional | bytes 3670208
  105.5 1.9 %collective-permute-start.160 = (bf16[2,128,1024]{2,1,0:T(8,128)(2,1)S(1)}, bf16[2,128,1024]{2,1,0:T(8,128)(2,1)}, u32[]{:S(2)}, u32[]{:S(2)}) collective-permute-start(bf16[2,128,1024]{2,1,0:T(8,128)(2,1)S(1)} %get-tuple-element.595), channel_id=1, source_target_pairs={{32,0},{36,4},{40,8},{44,12},{48,16},{52,20},{56,24},{60,28},{64,3... | collective-permute-start | bytes 1572872 | tf_op jit(solution)/shard_map/cond/branch_7_fun/ppermute | solution.py:122
  107.4 3.4 %collective-permute-start.161 = (bf16[4,128,128]{2,1,0:T(8,128)(2,1)S(1)}, bf16[4,128,128]{2,1,0:T(8,128)(2,1)}, u32[]{:S(2)}, u32[]{:S(2)}) collective-permute-start(bf16[4,128,128]{2,1,0:T(8,128)(2,1)S(1)} %get-tuple-element.596), channel_id=1, source_target_pairs={{0,1},{1,2},{2,3},{3,0},{4,5},{5,6},{6,7},{7,4},{8,9},{9,10},{10,1... | collective-permute-start | bytes 393224 | tf_op jit(solution)/shard_map/cond/branch_7_fun/ppermute | solution.py:95
  110.8 4.7 %collective-permute-start.162 = (bf16[4,128,128]{2,1,0:T(8,128)(2,1)S(1)}, bf16[4,128,128]{2,1,0:T(8,128)(2,1)}, u32[]{:S(2)}, u32[]{:S(2)}) collective-permute-start(bf16[4,128,128]{2,1,0:T(8,128)(2,1)S(1)} %get-tuple-element.597), channel_id=1, source_target_pairs={{0,2},{1,3},{2,0},{3,1},{4,6},{5,7},{6,4},{7,5},{8,10},{9,11},{10,... | collective-permute-start | bytes 393224 | tf_op jit(solution)/shard_map/cond/branch_7_fun/ppermute | solution.py:95
  115.5 3.3 %collective-permute-start.163 = (bf16[4,128,128]{2,1,0:T(8,128)(2,1)S(1)}, bf16[4,128,128]{2,1,0:T(8,128)(2,1)}, u32[]{:S(2)}, u32[]{:S(2)}) collective-permute-start(bf16[4,128,128]{2,1,0:T(8,128)(2,1)S(1)} %get-tuple-element.598), channel_id=1, source_target_pairs={{0,3},{1,0},{2,1},{3,2},{4,7},{5,4},{6,5},{7,6},{8,11},{9,8},{10,9... | collective-permute-start | bytes 393224 | tf_op jit(solution)/shard_map/cond/branch_7_fun/ppermute | solution.py:95
  122.5 16.2 %collective-permute-done.160 = bf16[2,128,1024]{2,1,0:T(8,128)(2,1)} collective-permute-done((bf16[2,128,1024]{2,1,0:T(8,128)(2,1)S(1)}, bf16[2,128,1024]{2,1,0:T(8,128)(2,1)}, u32[]{:S(2)}, u32[]{:S(2)}) %collective-permute-start.160) | collective-permute-done | bytes 524320 | tf_op jit(solution)/shard_map/cond/branch_7_fun/ppermute | solution.py:122
  139.8 2.7 %fusion.4 = f32[128,128,16]{1,0,2:T(8,128)S(1)} fusion(f32[16,1024]{1,0:T(8,128)S(1)} %copy-done.5, f32[128,1024]{1,0:T(8,128)} %copy-done.10, f32[16,1024]{1,0:T(8,128)S(1)} %copy-done.2, f32[128,1024]{1,0:T(8,128)} %copy-done.7, bf16[2,128,1024]{2,1,0:T(8,128)(2,1)S(1)} %broadcast_select_fusion), kind=kOutput, calls=%fused_computation.6 | convolution fusion | flops 545259520 | bytes 2490368 | tf_op jit(solution)/shard_map/ctf,jf->tcj/dot_general | solution.py:77
  142.5 2.7 %fusion.46 = f32[128,128,16]{1,0,2:T(8,128)S(1)} fusion(f32[128,128,16]{1,0,2:T(8,128)S(1)} %fusion.4, f32[16,1024]{1,0:T(8,128)S(1)} %copy-done.5, f32[128,1024]{1,0:T(8,128)} %copy-done.10, f32[16,1024]{1,0:T(8,128)S(1)} %copy-done.2, f32[128,1024]{1,0:T(8,128)} %copy-done.7, bf16[2,128,1024]{2,1,0:T(8,128)(2,1)S(1)} %broadcast_select_fusion), kind=kOutput, calls=%fused_computation.51 | convolution fusion | flops 545521664 | bytes 3538944 | tf_op jit(solution)/shard_map/ctf,jf->tcj/dot_general | solution.py:75
  145.9 3.4 %collective-permute-start.192 = (bf16[4,128,128]{2,1,0:T(8,128)(2,1)S(1)}, bf16[4,128,128]{2,1,0:T(8,128)(2,1)S(1)}, u32[]{:S(2)}, u32[]{:S(2)}) collective-permute-start(bf16[4,128,128]{2,1,0:T(8,128)(2,1)S(1)} %bitcast.262), channel_id=1, source_target_pairs={{0,1},{1,2},{2,3},{3,0},{4,5},{5,6},{6,7},{7,4},{8,9},{9,10},{10,1... | collective-permute-start | bytes 393224 | tf_op jit(solution)/shard_map/ppermute | solution.py:95
  149.4 4.7 %collective-permute-start.193 = (bf16[4,128,128]{2,1,0:T(8,128)(2,1)S(1)}, bf16[4,128,128]{2,1,0:T(8,128)(2,1)S(1)}, u32[]{:S(2)}, u32[]{:S(2)}) collective-permute-start(bf16[4,128,128]{2,1,0:T(8,128)(2,1)S(1)} %bitcast.263), channel_id=1, source_target_pairs={{0,2},{1,3},{2,0},{3,1},{4,6},{5,7},{6,4},{7,5},{8,10},{9,11},{10,... | collective-permute-start | bytes 393224 | tf_op jit(solution)/shard_map/ppermute | solution.py:95
  154.2 3.3 %collective-permute-start.194 = (bf16[4,128,128]{2,1,0:T(8,128)(2,1)S(1)}, bf16[4,128,128]{2,1,0:T(8,128)(2,1)S(1)}, u32[]{:S(2)}, u32[]{:S(2)}) collective-permute-start(bf16[4,128,128]{2,1,0:T(8,128)(2,1)S(1)} %bitcast.264), channel_id=1, source_target_pairs={{0,3},{1,0},{2,1},{3,2},{4,7},{5,4},{6,5},{7,6},{8,11},{9,8},{10,9... | collective-permute-start | bytes 393224 | tf_op jit(solution)/shard_map/ppermute | solution.py:95
  (82 shorter events, 26.9 us)
Async XLA Ops:
  7.2 4.2 %copy-start.6 = (s32[4]{0:T(128)S(1)}, s32[4]{0:T(128)}, u32[]{:S(2)}) copy-start(s32[4]{0:T(128)} %param.65) | copy-start | bytes 52
  9.4 14.4 %copy-start.7 = (f32[128,1024]{1,0:T(8,128)}, f32[128,1024]{1,0:T(8,128)S(1)}, u32[]{:S(2)}) copy-start(f32[128,1024]{1,0:T(8,128)S(1)} %get-tuple-element.680) | copy-start | bytes 1572868
  9.4 14.4 %copy-start.10 = (f32[128,1024]{1,0:T(8,128)}, f32[128,1024]{1,0:T(8,128)S(1)}, u32[]{:S(2)}) copy-start(f32[128,1024]{1,0:T(8,128)S(1)} %get-tuple-element.684) | copy-start | bytes 1572868
  9.5 14.2 %collective-permute-start.191 = (bf16[2,128,1024]{2,1,0:T(8,128)(2,1)S(1)}, bf16[2,128,1024]{2,1,0:T(8,128)(2,1)S(1)}, u32[]{:S(2)}, u32[]{:S(2)}) collective-permute-start(bf16[2,128,1024]{2,1,0:T(8,128)(2,1)S(1)} %pad_maximum_fusion.1), channel_id=1, source_target_pairs={{60,0},{64,4},{68,8},{72,12},{76,16},{80,20},{84,24},{88,28},{92,3... | collective-permute-start | bytes 1572872 | tf_op jit(solution)/shard_map/ppermute | solution.py:122
  18.6 38.2 %copy-start = (f32[16,1024]{1,0:T(8,128)}, f32[16,1024]{1,0:T(8,128)S(1)}, u32[]{:S(2)}) copy-start(f32[16,1024]{1,0:T(8,128)S(1)} %get-tuple-element.698) | copy-start | bytes 196612
  18.6 38.2 %copy-start.3 = (f32[16,1024]{1,0:T(8,128)}, f32[16,1024]{1,0:T(8,128)S(1)}, u32[]{:S(2)}) copy-start(f32[16,1024]{1,0:T(8,128)S(1)} %get-tuple-element.699) | copy-start | bytes 196612
  28.6 24.2 %collective-permute-start.58 = (bf16[2,128,1024]{2,1,0:T(8,128)(2,1)S(1)}, bf16[2,128,1024]{2,1,0:T(8,128)(2,1)}, u32[]{:S(2)}, u32[]{:S(2)}) collective-permute-start(bf16[2,128,1024]{2,1,0:T(8,128)(2,1)S(1)} %get-tuple-element.493), channel_id=1, source_target_pairs={{48,0},{52,4},{56,8},{60,12},{64,16},{68,20},{72,24},{76,28},{80,3... | collective-permute-start | bytes 1572872 | tf_op jit(solution)/shard_map/cond/branch_11_fun/ppermute | solution.py:122
  30.6 11.4 %collective-permute-start.59 = (bf16[4,128,128]{2,1,0:T(8,128)(2,1)S(1)}, bf16[4,128,128]{2,1,0:T(8,128)(2,1)}, u32[]{:S(2)}, u32[]{:S(2)}) collective-permute-start(bf16[4,128,128]{2,1,0:T(8,128)(2,1)S(1)} %get-tuple-element.494), channel_id=1, source_target_pairs={{0,1},{1,2},{2,3},{3,0},{4,5},{5,6},{6,7},{7,4},{8,9},{9,10},{10,1... | collective-permute-start | bytes 393224 | tf_op jit(solution)/shard_map/cond/branch_11_fun/ppermute | solution.py:95
  34.0 9.7 %collective-permute-start.60 = (bf16[4,128,128]{2,1,0:T(8,128)(2,1)S(1)}, bf16[4,128,128]{2,1,0:T(8,128)(2,1)}, u32[]{:S(2)}, u32[]{:S(2)}) collective-permute-start(bf16[4,128,128]{2,1,0:T(8,128)(2,1)S(1)} %get-tuple-element.495), channel_id=1, source_target_pairs={{0,2},{1,3},{2,0},{3,1},{4,6},{5,7},{6,4},{7,5},{8,10},{9,11},{10,... | collective-permute-start | bytes 393224 | tf_op jit(solution)/shard_map/cond/branch_11_fun/ppermute | solution.py:95
  38.6 7.0 %collective-permute-start.61 = (bf16[4,128,128]{2,1,0:T(8,128)(2,1)S(1)}, bf16[4,128,128]{2,1,0:T(8,128)(2,1)}, u32[]{:S(2)}, u32[]{:S(2)}) collective-permute-start(bf16[4,128,128]{2,1,0:T(8,128)(2,1)S(1)} %get-tuple-element.496), channel_id=1, source_target_pairs={{0,3},{1,0},{2,1},{3,2},{4,7},{5,4},{6,5},{7,6},{8,11},{9,8},{10,9... | collective-permute-start | bytes 393224 | tf_op jit(solution)/shard_map/cond/branch_11_fun/ppermute | solution.py:95
  52.8 4.0 %copy-start.8 = (f32[128,1024]{1,0:T(8,128)S(1)}, f32[128,1024]{1,0:T(8,128)}, u32[]{:S(2)}) copy-start(f32[128,1024]{1,0:T(8,128)} %copy-done.7) | copy-start | bytes 1572868
  52.8 4.0 %copy-start.11 = (f32[128,1024]{1,0:T(8,128)S(1)}, f32[128,1024]{1,0:T(8,128)}, u32[]{:S(2)}) copy-start(f32[128,1024]{1,0:T(8,128)} %copy-done.10) | copy-start | bytes 1572868
  60.1 43.0 %copy-start.1 = (f32[16,1024]{1,0:T(8,128)S(1)}, f32[16,1024]{1,0:T(8,128)}, u32[]{:S(2)}) copy-start(f32[16,1024]{1,0:T(8,128)} %copy-done) | copy-start | bytes 196612
  60.1 43.0 %copy-start.4 = (f32[16,1024]{1,0:T(8,128)S(1)}, f32[16,1024]{1,0:T(8,128)}, u32[]{:S(2)}) copy-start(f32[16,1024]{1,0:T(8,128)} %copy-done.3) | copy-start | bytes 196612
  60.2 38.9 %collective-permute-start.113 = (bf16[2,128,1024]{2,1,0:T(8,128)(2,1)S(1)}, bf16[2,128,1024]{2,1,0:T(8,128)(2,1)}, u32[]{:S(2)}, u32[]{:S(2)}) collective-permute-start(bf16[2,128,1024]{2,1,0:T(8,128)(2,1)S(1)} %get-tuple-element.548), channel_id=1, source_target_pairs={{44,0},{48,4},{52,8},{56,12},{60,16},{64,20},{68,24},{72,28},{76,3... | collective-permute-start | bytes 1572872 | tf_op jit(solution)/shard_map/cond/branch_10_fun/ppermute | solution.py:122
  63.3 11.4 %collective-permute-start.114 = (bf16[4,128,128]{2,1,0:T(8,128)(2,1)}, bf16[4,128,128]{2,1,0:T(8,128)(2,1)}, u32[]{:S(2)}, u32[]{:S(2)}) collective-permute-start(bf16[4,128,128]{2,1,0:T(8,128)(2,1)} %get-tuple-element.549), channel_id=1, source_target_pairs={{0,1},{1,2},{2,3},{3,0},{4,5},{5,6},{6,7},{7,4},{8,9},{9,10},{10,1... | collective-permute-start | bytes 393224 | tf_op jit(solution)/shard_map/cond/branch_10_fun/ppermute | solution.py:95
  66.7 8.5 %collective-permute-start.115 = (bf16[4,128,128]{2,1,0:T(8,128)(2,1)S(1)}, bf16[4,128,128]{2,1,0:T(8,128)(2,1)}, u32[]{:S(2)}, u32[]{:S(2)}) collective-permute-start(bf16[4,128,128]{2,1,0:T(8,128)(2,1)S(1)} %get-tuple-element.550), channel_id=1, source_target_pairs={{0,2},{1,3},{2,0},{3,1},{4,6},{5,7},{6,4},{7,5},{8,10},{9,11},{10,... | collective-permute-start | bytes 393224 | tf_op jit(solution)/shard_map/cond/branch_10_fun/ppermute | solution.py:95
  71.4 7.5 %collective-permute-start.116 = (bf16[4,128,128]{2,1,0:T(8,128)(2,1)}, bf16[4,128,128]{2,1,0:T(8,128)(2,1)}, u32[]{:S(2)}, u32[]{:S(2)}) collective-permute-start(bf16[4,128,128]{2,1,0:T(8,128)(2,1)} %get-tuple-element.551), channel_id=1, source_target_pairs={{0,3},{1,0},{2,1},{3,2},{4,7},{5,4},{6,5},{7,6},{8,11},{9,8},{10,9... | collective-permute-start | bytes 393224 | tf_op jit(solution)/shard_map/cond/branch_10_fun/ppermute | solution.py:95
  99.1 4.0 %copy-start.9 = (f32[128,1024]{1,0:T(8,128)S(1)}, f32[128,1024]{1,0:T(8,128)}, u32[]{:S(2)}) copy-start(f32[128,1024]{1,0:T(8,128)} %copy-done.7) | copy-start | bytes 1572868
  99.1 4.0 %copy-start.12 = (f32[128,1024]{1,0:T(8,128)S(1)}, f32[128,1024]{1,0:T(8,128)}, u32[]{:S(2)}) copy-start(f32[128,1024]{1,0:T(8,128)} %copy-done.10) | copy-start | bytes 1572868
  103.1 36.6 %copy-start.2 = (f32[16,1024]{1,0:T(8,128)S(1)}, f32[16,1024]{1,0:T(8,128)}, u32[]{:S(2)}) copy-start(f32[16,1024]{1,0:T(8,128)} %copy-done) | copy-start | bytes 196612
  103.1 36.6 %copy-start.5 = (f32[16,1024]{1,0:T(8,128)S(1)}, f32[16,1024]{1,0:T(8,128)}, u32[]{:S(2)}) copy-start(f32[16,1024]{1,0:T(8,128)} %copy-done.3) | copy-start | bytes 196612
  105.5 33.1 %collective-permute-start.160 = (bf16[2,128,1024]{2,1,0:T(8,128)(2,1)S(1)}, bf16[2,128,1024]{2,1,0:T(8,128)(2,1)}, u32[]{:S(2)}, u32[]{:S(2)}) collective-permute-start(bf16[2,128,1024]{2,1,0:T(8,128)(2,1)S(1)} %get-tuple-element.595), channel_id=1, source_target_pairs={{32,0},{36,4},{40,8},{44,12},{48,16},{52,20},{56,24},{60,28},{64,3... | collective-permute-start | bytes 1572872 | tf_op jit(solution)/shard_map/cond/branch_7_fun/ppermute | solution.py:122
  107.4 11.3 %collective-permute-start.161 = (bf16[4,128,128]{2,1,0:T(8,128)(2,1)S(1)}, bf16[4,128,128]{2,1,0:T(8,128)(2,1)}, u32[]{:S(2)}, u32[]{:S(2)}) collective-permute-start(bf16[4,128,128]{2,1,0:T(8,128)(2,1)S(1)} %get-tuple-element.596), channel_id=1, source_target_pairs={{0,1},{1,2},{2,3},{3,0},{4,5},{5,6},{6,7},{7,4},{8,9},{9,10},{10,1... | collective-permute-start | bytes 393224 | tf_op jit(solution)/shard_map/cond/branch_7_fun/ppermute | solution.py:95
  110.8 9.9 %collective-permute-start.162 = (bf16[4,128,128]{2,1,0:T(8,128)(2,1)S(1)}, bf16[4,128,128]{2,1,0:T(8,128)(2,1)}, u32[]{:S(2)}, u32[]{:S(2)}) collective-permute-start(bf16[4,128,128]{2,1,0:T(8,128)(2,1)S(1)} %get-tuple-element.597), channel_id=1, source_target_pairs={{0,2},{1,3},{2,0},{3,1},{4,6},{5,7},{6,4},{7,5},{8,10},{9,11},{10,... | collective-permute-start | bytes 393224 | tf_op jit(solution)/shard_map/cond/branch_7_fun/ppermute | solution.py:95
  115.5 7.0 %collective-permute-start.163 = (bf16[4,128,128]{2,1,0:T(8,128)(2,1)S(1)}, bf16[4,128,128]{2,1,0:T(8,128)(2,1)}, u32[]{:S(2)}, u32[]{:S(2)}) collective-permute-start(bf16[4,128,128]{2,1,0:T(8,128)(2,1)S(1)} %get-tuple-element.598), channel_id=1, source_target_pairs={{0,3},{1,0},{2,1},{3,2},{4,7},{5,4},{6,5},{7,6},{8,11},{9,8},{10,9... | collective-permute-start | bytes 393224 | tf_op jit(solution)/shard_map/cond/branch_7_fun/ppermute | solution.py:95
  145.9 15.0 %collective-permute-start.192 = (bf16[4,128,128]{2,1,0:T(8,128)(2,1)S(1)}, bf16[4,128,128]{2,1,0:T(8,128)(2,1)S(1)}, u32[]{:S(2)}, u32[]{:S(2)}) collective-permute-start(bf16[4,128,128]{2,1,0:T(8,128)(2,1)S(1)} %bitcast.262), channel_id=1, source_target_pairs={{0,1},{1,2},{2,3},{3,0},{4,5},{5,6},{6,7},{7,4},{8,9},{9,10},{10,1... | collective-permute-start | bytes 393224 | tf_op jit(solution)/shard_map/ppermute | solution.py:95
  149.4 11.5 %collective-permute-start.193 = (bf16[4,128,128]{2,1,0:T(8,128)(2,1)S(1)}, bf16[4,128,128]{2,1,0:T(8,128)(2,1)S(1)}, u32[]{:S(2)}, u32[]{:S(2)}) collective-permute-start(bf16[4,128,128]{2,1,0:T(8,128)(2,1)S(1)} %bitcast.263), channel_id=1, source_target_pairs={{0,2},{1,3},{2,0},{3,1},{4,6},{5,7},{6,4},{7,5},{8,10},{9,11},{10,... | collective-permute-start | bytes 393224 | tf_op jit(solution)/shard_map/ppermute | solution.py:95
  154.2 6.9 %collective-permute-start.194 = (bf16[4,128,128]{2,1,0:T(8,128)(2,1)S(1)}, bf16[4,128,128]{2,1,0:T(8,128)(2,1)S(1)}, u32[]{:S(2)}, u32[]{:S(2)}) collective-permute-start(bf16[4,128,128]{2,1,0:T(8,128)(2,1)S(1)} %bitcast.264), channel_id=1, source_target_pairs={{0,3},{1,0},{2,1},{3,2},{4,7},{5,4},{6,5},{7,6},{8,11},{9,8},{10,9... | collective-permute-start | bytes 393224 | tf_op jit(solution)/shard_map/ppermute | solution.py:95

commit v4 on v3

--- a/solution.py
+++ b/solution.py
@@ -73,8 +73,8 @@
 
 def lag_terms(first, second, partner):
     return jnp.einsum(
-        "ctf,jf->tcj", first, partner[0], preferred_element_type=jnp.float32
-    ) + jnp.einsum("ctf,jf->tcj", second, partner[1], preferred_element_type=jnp.float32)
+        "ctf,kjf->tkcj", first, partner[:, 0], preferred_element_type=jnp.float32
+    ) + jnp.einsum("ctf,kjf->tkcj", second, partner[:, 1], preferred_element_type=jnp.float32)
 
 
 def split_for_win(corr):
@@ -121,27 +121,31 @@
         pairs = [(i + by, i) for i in range(n_chan - by)]
         return lambda x: lax.ppermute(x, "chan", pairs)
 
-    def with_win(move):
-        return lambda x, sent: (move(x), pass_over_win(sent))
-
     far = OFFCAP - 1
     farthest = shifted(far)(spectra)
     moves = [shifted(by) for by in range(1, far)] + [jnp.zeros_like]
-    paired = [with_win(move) for move in moves]
     cos_w, sin_w = phase_tables(groups)
     first, second = lag_factors(own_re, own_im, cos_w, sin_w)
-    parts = []
-    pending = None
-    for k in range(K):
-        if pending is None:
-            moved = lax.switch(offsets[k] - 1, moves, spectra)
-        else:
-            moved, arrived = lax.switch(offsets[k] - 1, paired, spectra, pending[1])
-            parts.append(sum_over_win(pending[0], arrived))
-        partner = jnp.where(offsets[k] == far, farthest, moved)
-        pending = split_for_win(lag_terms(first, second, partner))
-    parts.append(sum_over_win(pending[0], pass_over_win(pending[1])))
-    return jnp.stack(parts, axis=1)
+
+    def fetched(k, moved):
+        return jnp.where(offsets[k] == far, farthest, moved)
+
+    early = jnp.stack(
+        [fetched(k, lax.switch(offsets[k] - 1, moves, spectra)) for k in range(K - 1)], axis=0
+    )
+
+    early_own, early_sent = split_for_win(lag_terms(first, second, early))
+
+    def with_early(move):
+        return lambda x, sent: (move(x), pass_over_win(sent))
+
+    last, early_arrived = lax.switch(
+        offsets[K - 1] - 1, [with_early(move) for move in moves], spectra, early_sent
+    )
+    last_own, last_sent = split_for_win(lag_terms(first, second, fetched(K - 1, last)[None]))
+    early_sum = sum_over_win(early_own, early_arrived)
+    last_sum = sum_over_win(last_own, pass_over_win(last_sent))
+    return jnp.concatenate([early_sum, last_sum], axis=1)
 
 
 def solution(mesh):

time: 163 us -> 148 us (0.908)
  the two profiles are of different devices: /device:TPU:224 before, /device:TPU:248 now
where the time goes in v4:
time: 148 us; the launch traced here: 147 us
  waiting for transfers between devices  79.1 us (53%)
  starting transfers between devices  30.7 us (21%)
  matrix products  15.2 us (10%)
  local copies, waits for them, and re-layouts  8.8 us (6%)
  other arithmetic  7.15 us (5%)
  between operations  6.02 us (4%)
    ppermute x4, waiting for transfers between devices, shifted(): return lambda x: lax.ppermute(x, 'chan', pairs)  62 us
    ppermute x6, starting transfers between devices, pass_over_win(): lax.ppermute(piece, 'win', [(w, (w + by) % groups) for w in range(groups)])  21 us
    ppermute x6, waiting for transfers between devices, pass_over_win(): lax.ppermute(piece, 'win', [(w, (w + by) % groups) for w in range(groups)])  17.2 us
    ppermute x4, starting transfers between devices, shifted(): return lambda x: lax.ppermute(x, 'chan', pairs)  9.79 us
    unnamed x18, local copies, waits for them, and re-layouts  5.41 us
    dot_general x1, matrix products, whiten(): spec = jnp.dot(shaped, table, preferred_element_type=jnp.float32)  4.94 us
    dot_general x2, matrix products, lag_terms(): jnp.einsum('ctf,kjf->tkcj', second, partner[:, 1], preferred_element_type...  4.69 us
    dot_general x2, matrix products, lag_terms(): jnp.einsum('ctf,kjf->tkcj', first, partner[:, 0], preferred_element_type=...  3.47 us
  transfers between devices with their start and end apart: 10, of which 8 were waited for; matrix products, arithmetic and copies ran while one was open for 2% of the time, Pallas kernels for 0%

profile of v4, /device:TPU:248, one launch (start us, length us, event | category | flops | bytes accessed | tf_op | source)
XLA Modules:
  0.0 147.2 jit_solution(4960657377811478731)
XLA Ops:
  0.9 1.4 convert_reduce_fusion.1
  2.3 4.9 %fusion.38 = f32[128,2048]{1,0:T(8,128)S(1)} fusion(bf16[2048,2048]{1,0:T(8,128)(2,1)} %constant.136.clone, f32[2048]{0:T(1024)S(1)} %multiply_subtract_fusion, f32[128]{0:T(128)S(1)} %broadcast_multiply_fusion, bf16[128,4096]{1,0:T(8,128)(2,1)} %param.64, s32[]{:T(128)S(6)} %select_n.102), kind=kOutput, calls=%fused_computation.55 | convolution fusion | flops 1074790400 | bytes 9970180 | tf_op jit(solution)/shard_map/dot_general | solution.py:57
  7.3 2.1 %fusion.53 = (f32[128,1024]{1,0:T(8,128)S(1)}, bf16[128,1024]{1,0:T(8,128)(2,1)S(1)}, f32[128,1024]{1,0:T(8,128)S(1)}, bf16[128,1024]{1,0:T(8,128)(2,1)S(1)}) fusion(f32[128,2048]{1,0:T(8,128)S(1)} %fusion.38, f32[1024]{0:T(1024)S(1)} %convert_reduce_fusion), kind=kOutput, calls=%fused_computation.96 | convolution fusion | flops 1617166336 | bytes 3674112 | tf_op jit(solution)/shard_map/dot_general | solution.py:61
  9.5 1.9 %collective-permute-start.101 = (bf16[2,128,1024]{2,1,0:T(8,128)(2,1)S(1)}, bf16[2,128,1024]{2,1,0:T(8,128)(2,1)S(1)}, u32[]{:S(2)}, u32[]{:S(2)}) collective-permute-start(bf16[2,128,1024]{2,1,0:T(8,128)(2,1)S(1)} %pad_maximum_fusion.2), channel_id=1, source_target_pairs={{60,0},{64,4},{68,8},{72,12},{76,16},{80,20},{84,24},{88,28},{92,3... | collective-permute-start | bytes 1572872 | tf_op jit(solution)/shard_map/ppermute | solution.py:122
  17.2 31.0 %conditional.8 = (bf16[2,128,1024]{2,1,0:T(8,128)(2,1)}) conditional(s32[]{:T(128)} %bitcast.10, bf16[2,128,1024]{2,1,0:T(8,128)(2,1)S(1)} %pad_maximum_fusion.2, bf16[2,128,1024]{2,1,0:T(8,128)(2,1)S(1)} %pad_maximum_fusion.2, bf16[2,128,1024]{2,1,0:T(8,128)(2,1)S(1)} %pad_maximum_fusion.2, ...), branch_computations={%region_32.33_spmd, %region_33.34_spmd, %region_34.35_spmd, %regio... | conditional | bytes 2097200 | solution.py:134
  17.2 4.0 %collective-permute-start.31 = (bf16[2,128,1024]{2,1,0:T(8,128)(2,1)S(1)}, bf16[2,128,1024]{2,1,0:T(8,128)(2,1)}, u32[]{:S(2)}, u32[]{:S(2)}) collective-permute-start(bf16[2,128,1024]{2,1,0:T(8,128)(2,1)S(1)} %param.33), channel_id=1, source_target_pairs={{16,0},{20,4},{24,8},{28,12},{32,16},{36,20},{40,24},{44,28},{48,3... | collective-permute-start | bytes 1572872 | tf_op jit(solution)/shard_map/cond/branch_3_fun/ppermute | solution.py:122
  21.2 27.0 %collective-permute-done.31 = bf16[2,128,1024]{2,1,0:T(8,128)(2,1)} collective-permute-done((bf16[2,128,1024]{2,1,0:T(8,128)(2,1)S(1)}, bf16[2,128,1024]{2,1,0:T(8,128)(2,1)}, u32[]{:S(2)}, u32[]{:S(2)}) %collective-permute-start.31) | collective-permute-done | bytes 524320 | tf_op jit(solution)/shard_map/cond/branch_3_fun/ppermute | solution.py:122
  49.0 34.0 %conditional.6 = (bf16[2,128,1024]{2,1,0:T(8,128)(2,1)}) conditional(s32[]{:T(128)} %bitcast.4, bf16[2,128,1024]{2,1,0:T(8,128)(2,1)S(1)} %pad_maximum_fusion.2, bf16[2,128,1024]{2,1,0:T(8,128)(2,1)S(1)} %pad_maximum_fusion.2, bf16[2,128,1024]{2,1,0:T(8,128)(2,1)S(1)} %pad_maximum_fusion.2, ...), branch_computations={%region_2.3_spmd, %region_3.4_spmd, %region_4.5_spmd, %region_5.6_... | conditional | bytes 2097200 | solution.py:134
  49.0 1.9 %collective-permute-start.4 = (bf16[2,128,1024]{2,1,0:T(8,128)(2,1)S(1)}, bf16[2,128,1024]{2,1,0:T(8,128)(2,1)}, u32[]{:S(2)}, u32[]{:S(2)}) collective-permute-start(bf16[2,128,1024]{2,1,0:T(8,128)(2,1)S(1)} %param.4), channel_id=1, source_target_pairs={{20,0},{24,4},{28,8},{32,12},{36,16},{40,20},{44,24},{48,28},{52,3... | collective-permute-start | bytes 1572872 | tf_op jit(solution)/shard_map/cond/branch_4_fun/ppermute | solution.py:122
  51.0 32.1 %collective-permute-done.4 = bf16[2,128,1024]{2,1,0:T(8,128)(2,1)} collective-permute-done((bf16[2,128,1024]{2,1,0:T(8,128)(2,1)S(1)}, bf16[2,128,1024]{2,1,0:T(8,128)(2,1)}, u32[]{:S(2)}, u32[]{:S(2)}) %collective-permute-start.4) | collective-permute-done | bytes 524320 | tf_op jit(solution)/shard_map/cond/branch_4_fun/ppermute | solution.py:122
  83.4 1.3 select_bitcast_fusion.3
  84.9 1.9 %fusion.4 = f32[3,128,128,16]{2,1,3,0:T(8,128)S(1)} fusion(f32[16,1024]{1,0:T(8,128)S(1)} %get-tuple-element.326, f32[128,1024]{1,0:T(8,128)S(1)} %get-tuple-element.317, f32[16,1024]{1,0:T(8,128)S(1)} %get-tuple-element.325, f32[128,1024]{1,0:T(8,128)S(1)} %get-tuple-element.310, bf16[3,2,128,1024]{3,2,1,0:T(8,128)(2,1)S(1)} %pad_maximum_fusion), kind=kOutput, calls=%fused_computation.8 | convolution fusion | flops 1619001344 | bytes 5111808 | tf_op jit(solution)/shard_map/ctf,kjf->tkcj/dot_general | solution.py:77
  86.8 1.9 %fusion.27 = f32[3,128,128,16]{2,1,3,0:T(8,128)S(1)} fusion(f32[3,128,128,16]{2,1,3,0:T(8,128)S(1)} %fusion.4, f32[16,1024]{1,0:T(8,128)S(1)} %get-tuple-element.326, f32[128,1024]{1,0:T(8,128)S(1)} %get-tuple-element.317, f32[16,1024]{1,0:T(8,128)S(1)} %get-tuple-element.325, f32[128,1024]{1,0:T(8,128)S(1)} %get-tuple-element.310, ...), kind=kOutput, calls=%fused_computation.30 | convolution fusion | flops 1619787776 | bytes 8257536 | tf_op jit(solution)/shard_map/ctf,kjf->tkcj/dot_general | solution.py:75
  88.8 1.7 %copy-done = f32[3,128,128,16]{2,1,3,0:T(8,128)} copy-done((f32[3,128,128,16]{2,1,3,0:T(8,128)}, f32[3,128,128,16]{2,1,3,0:T(8,128)S(1)}, u32[]{:S(2)}) %copy-start) | copy-done | bytes 3145752
  92.0 1.2 constant_dynamic-slice_fusion.7
  93.5 29.1 %conditional.10 = (bf16[2,128,1024]{2,1,0:T(8,128)(2,1)}, bf16[4,3,128,128]{3,2,1,0:T(8,128)(2,1)}, bf16[4,3,128,128]{3,2,1,0:T(8,128)(2,1)}, bf16[4,3,128,128]{3,2,1,0:T(8,128)(2,1)}) conditional(s32[]{:T(128)} %bitcast.23, (bf16[2,128,1024]{2,1,0:T(8,128)(2,1)S(1)}, bf16[4,3,128,128]{3,2,1,0:T(8,128)(2,1)}, ...), branch_computations={%region_47.48_spmd, %region_48.49_spmd, %region_49.50_spmd, %regio... | conditional | bytes 6815936
  93.5 1.9 %collective-permute-start.86 = (bf16[2,128,1024]{2,1,0:T(8,128)(2,1)S(1)}, bf16[2,128,1024]{2,1,0:T(8,128)(2,1)}, u32[]{:S(2)}, u32[]{:S(2)}) collective-permute-start(bf16[2,128,1024]{2,1,0:T(8,128)(2,1)S(1)} %get-tuple-element.277), channel_id=1, source_target_pairs={{48,0},{52,4},{56,8},{60,12},{64,16},{68,20},{72,24},{76,28},{80,3... | collective-permute-start | bytes 1572872 | tf_op jit(solution)/shard_map/cond/branch_11_fun/ppermute | solution.py:122
  95.4 3.3 %collective-permute-start.87 = (bf16[4,3,128,128]{3,2,1,0:T(8,128)(2,1)}, bf16[4,3,128,128]{3,2,1,0:T(8,128)(2,1)}, u32[]{:S(2)}, u32[]{:S(2)}) collective-permute-start(bf16[4,3,128,128]{3,2,1,0:T(8,128)(2,1)} %get-tuple-element.278), channel_id=1, source_target_pairs={{0,1},{1,2},{2,3},{3,0},{4,5},{5,6},{6,7},{7,4},{8,9},{9,10},{10,1... | collective-permute-start | bytes 1179656 | tf_op jit(solution)/shard_map/cond/branch_11_fun/ppermute | solution.py:95
  98.7 4.6 %collective-permute-start.88 = (bf16[4,3,128,128]{3,2,1,0:T(8,128)(2,1)S(1)}, bf16[4,3,128,128]{3,2,1,0:T(8,128)(2,1)}, u32[]{:S(2)}, u32[]{:S(2)}) collective-permute-start(bf16[4,3,128,128]{3,2,1,0:T(8,128)(2,1)S(1)} %get-tuple-element.279), channel_id=1, source_target_pairs={{0,2},{1,3},{2,0},{3,1},{4,6},{5,7},{6,4},{7,5},{8,10},{9,11},{10,... | collective-permute-start | bytes 1179656 | tf_op jit(solution)/shard_map/cond/branch_11_fun/ppermute | solution.py:95
  103.4 3.4 %collective-permute-start.89 = (bf16[4,3,128,128]{3,2,1,0:T(8,128)(2,1)S(1)}, bf16[4,3,128,128]{3,2,1,0:T(8,128)(2,1)}, u32[]{:S(2)}, u32[]{:S(2)}) collective-permute-start(bf16[4,3,128,128]{3,2,1,0:T(8,128)(2,1)S(1)} %get-tuple-element.280), channel_id=1, source_target_pairs={{0,3},{1,0},{2,1},{3,2},{4,7},{5,4},{6,5},{7,6},{8,11},{9,8},{10,9... | collective-permute-start | bytes 1179656 | tf_op jit(solution)/shard_map/cond/branch_11_fun/ppermute | solution.py:95
  106.8 3.6 %collective-permute-done.87 = bf16[4,3,128,128]{3,2,1,0:T(8,128)(2,1)} collective-permute-done((bf16[4,3,128,128]{3,2,1,0:T(8,128)(2,1)}, bf16[4,3,128,128]{3,2,1,0:T(8,128)(2,1)}, u32[]{:S(2)}, u32[]{:S(2)}) %collective-permute-start.87) | collective-permute-done | bytes 393248 | tf_op jit(solution)/shard_map/cond/branch_11_fun/ppermute | solution.py:95
  110.4 7.7 %collective-permute-done.88 = bf16[4,3,128,128]{3,2,1,0:T(8,128)(2,1)} collective-permute-done((bf16[4,3,128,128]{3,2,1,0:T(8,128)(2,1)S(1)}, bf16[4,3,128,128]{3,2,1,0:T(8,128)(2,1)}, u32[]{:S(2)}, u32[]{:S(2)}) %collective-permute-start.88) | collective-permute-done | bytes 393248 | tf_op jit(solution)/shard_map/cond/branch_11_fun/ppermute | solution.py:95
  118.0 1.6 %collective-permute-done.89 = bf16[4,3,128,128]{3,2,1,0:T(8,128)(2,1)} collective-permute-done((bf16[4,3,128,128]{3,2,1,0:T(8,128)(2,1)S(1)}, bf16[4,3,128,128]{3,2,1,0:T(8,128)(2,1)}, u32[]{:S(2)}, u32[]{:S(2)}) %collective-permute-start.89) | collective-permute-done | bytes 393248 | tf_op jit(solution)/shard_map/cond/branch_11_fun/ppermute | solution.py:95
  119.7 2.9 %collective-permute-done.86 = bf16[2,128,1024]{2,1,0:T(8,128)(2,1)} collective-permute-done((bf16[2,128,1024]{2,1,0:T(8,128)(2,1)S(1)}, bf16[2,128,1024]{2,1,0:T(8,128)(2,1)}, u32[]{:S(2)}, u32[]{:S(2)}) %collective-permute-start.86) | collective-permute-done | bytes 524320 | tf_op jit(solution)/shard_map/cond/branch_11_fun/ppermute | solution.py:122
  123.7 2.8 %fusion.2 = f32[128,128,16]{1,0,2:T(8,128)S(1)} fusion(f32[16,1024]{1,0:T(8,128)S(1)} %get-tuple-element.326, f32[128,1024]{1,0:T(8,128)} %copy-done.4, f32[16,1024]{1,0:T(8,128)S(1)} %get-tuple-element.325, f32[128,1024]{1,0:T(8,128)} %copy-done.2, bf16[1,2,128,1024]{3,2,1,0:T(8,128)(2,1)S(1)} %select_bitcast_fusion), kind=kOutput, calls=%fused_computation.6 | convolution fusion | flops 545259520 | bytes 2490368 | tf_op jit(solution)/shard_map/ctf,kjf->tkcj/dot_general | solution.py:77
  126.6 1.6 %fusion.30 = f32[128,128,16]{1,0,2:T(8,128)S(1)} fusion(f32[128,128,16]{1,0,2:T(8,128)S(1)} %fusion.2, f32[16,1024]{1,0:T(8,128)S(1)} %get-tuple-element.326, f32[128,1024]{1,0:T(8,128)S(1)} %copy-done.5, f32[16,1024]{1,0:T(8,128)S(1)} %get-tuple-element.325, f32[128,1024]{1,0:T(8,128)S(1)} %copy-done.3, bf16[1,2,128,1024]{3,2,1,0:T(8,128)(2,1)S(1)} %select_bitcast_fusion), kind=kOutput, calls=%fused_computation.32 | convolution fusion | flops 545521664 | bytes 3538944 | tf_op jit(solution)/shard_map/ctf,kjf->tkcj/dot_general | solution.py:75
  130.5 4.1 %collective-permute-start.104 = (bf16[4,1,128,128]{3,2,1,0:T(8,128)(2,1)}, bf16[4,1,128,128]{3,2,1,0:T(8,128)(2,1)S(1)}, u32[]{:S(2)}, u32[]{:S(2)}) collective-permute-start(bf16[4,1,128,128]{3,2,1,0:T(8,128)(2,1)} %bitcast.80), channel_id=1, source_target_pairs={{0,3},{1,0},{2,1},{3,2},{4,7},{5,4},{6,5},{7,6},{8,11},{9,8},{10,9... | collective-permute-start | bytes 393224 | tf_op jit(solution)/shard_map/ppermute | solution.py:95
  134.7 2.6 %collective-permute-start.103 = (bf16[4,1,128,128]{3,2,1,0:T(8,128)(2,1)}, bf16[4,1,128,128]{3,2,1,0:T(8,128)(2,1)S(1)}, u32[]{:S(2)}, u32[]{:S(2)}) collective-permute-start(bf16[4,1,128,128]{3,2,1,0:T(8,128)(2,1)} %bitcast.81), channel_id=1, source_target_pairs={{0,2},{1,3},{2,0},{3,1},{4,6},{5,7},{6,4},{7,5},{8,10},{9,11},{10,... | collective-permute-start | bytes 393224 | tf_op jit(solution)/shard_map/ppermute | solution.py:95
  137.3 3.0 %collective-permute-start.102 = (bf16[4,1,128,128]{3,2,1,0:T(8,128)(2,1)}, bf16[4,1,128,128]{3,2,1,0:T(8,128)(2,1)S(1)}, u32[]{:S(2)}, u32[]{:S(2)}) collective-permute-start(bf16[4,1,128,128]{3,2,1,0:T(8,128)(2,1)} %bitcast.82), channel_id=1, source_target_pairs={{0,1},{1,2},{2,3},{3,0},{4,5},{5,6},{6,7},{7,4},{8,9},{9,10},{10,1... | collective-permute-start | bytes 393224 | tf_op jit(solution)/shard_map/ppermute | solution.py:95
  140.2 1.4 convert_add_fusion
  141.8 2.7 %collective-permute-done.103 = bf16[4,1,128,128]{3,2,1,0:T(8,128)(2,1)S(1)} collective-permute-done((bf16[4,1,128,128]{3,2,1,0:T(8,128)(2,1)}, bf16[4,1,128,128]{3,2,1,0:T(8,128)(2,1)S(1)}, u32[]{:S(2)}, u32[]{:S(2)}) %collective-permute-start.103) | collective-permute-done | bytes 131104 | tf_op jit(solution)/shard_map/ppermute | solution.py:95
  144.5 1.6 %collective-permute-done.102 = bf16[4,1,128,128]{3,2,1,0:T(8,128)(2,1)S(1)} collective-permute-done((bf16[4,1,128,128]{3,2,1,0:T(8,128)(2,1)}, bf16[4,1,128,128]{3,2,1,0:T(8,128)(2,1)S(1)}, u32[]{:S(2)}, u32[]{:S(2)}) %collective-permute-start.102) | collective-permute-done | bytes 131104 | tf_op jit(solution)/shard_map/ppermute | solution.py:95
  (38 shorter events, 9.9 us)
Async XLA Ops:
  7.2 4.2 %copy-start.1 = (s32[4]{0:T(128)S(1)}, s32[4]{0:T(128)}, u32[]{:S(2)}) copy-start(s32[4]{0:T(128)} %param.65) | copy-start | bytes 52
  9.4 77.4 %copy-start.4 = (f32[128,1024]{1,0:T(8,128)}, f32[128,1024]{1,0:T(8,128)S(1)}, u32[]{:S(2)}) copy-start(f32[128,1024]{1,0:T(8,128)S(1)} %get-tuple-element.317) | copy-start | bytes 1572868
  9.4 79.3 %copy-start.2 = (f32[128,1024]{1,0:T(8,128)}, f32[128,1024]{1,0:T(8,128)S(1)}, u32[]{:S(2)}) copy-start(f32[128,1024]{1,0:T(8,128)S(1)} %get-tuple-element.310) | copy-start | bytes 1572868
  9.5 73.9 %collective-permute-start.101 = (bf16[2,128,1024]{2,1,0:T(8,128)(2,1)S(1)}, bf16[2,128,1024]{2,1,0:T(8,128)(2,1)S(1)}, u32[]{:S(2)}, u32[]{:S(2)}) collective-permute-start(bf16[2,128,1024]{2,1,0:T(8,128)(2,1)S(1)} %pad_maximum_fusion.2), channel_id=1, source_target_pairs={{60,0},{64,4},{68,8},{72,12},{76,16},{80,20},{84,24},{88,28},{92,3... | collective-permute-start | bytes 1572872 | tf_op jit(solution)/shard_map/ppermute | solution.py:122
  17.2 31.0 %collective-permute-start.31 = (bf16[2,128,1024]{2,1,0:T(8,128)(2,1)S(1)}, bf16[2,128,1024]{2,1,0:T(8,128)(2,1)}, u32[]{:S(2)}, u32[]{:S(2)}) collective-permute-start(bf16[2,128,1024]{2,1,0:T(8,128)(2,1)S(1)} %param.33), channel_id=1, source_target_pairs={{16,0},{20,4},{24,8},{28,12},{32,16},{36,20},{40,24},{44,28},{48,3... | collective-permute-start | bytes 1572872 | tf_op jit(solution)/shard_map/cond/branch_3_fun/ppermute | solution.py:122
  49.0 34.0 %collective-permute-start.4 = (bf16[2,128,1024]{2,1,0:T(8,128)(2,1)S(1)}, bf16[2,128,1024]{2,1,0:T(8,128)(2,1)}, u32[]{:S(2)}, u32[]{:S(2)}) collective-permute-start(bf16[2,128,1024]{2,1,0:T(8,128)(2,1)S(1)} %param.4), channel_id=1, source_target_pairs={{20,0},{24,4},{28,8},{32,12},{36,16},{40,20},{44,24},{48,28},{52,3... | collective-permute-start | bytes 1572872 | tf_op jit(solution)/shard_map/cond/branch_4_fun/ppermute | solution.py:122
  88.7 1.7 %copy-start = (f32[3,128,128,16]{2,1,3,0:T(8,128)}, f32[3,128,128,16]{2,1,3,0:T(8,128)S(1)}, u32[]{:S(2)}) copy-start(f32[3,128,128,16]{2,1,3,0:T(8,128)S(1)} %fusion.27) | copy-start | bytes 9437188
  93.5 29.1 %collective-permute-start.86 = (bf16[2,128,1024]{2,1,0:T(8,128)(2,1)S(1)}, bf16[2,128,1024]{2,1,0:T(8,128)(2,1)}, u32[]{:S(2)}, u32[]{:S(2)}) collective-permute-start(bf16[2,128,1024]{2,1,0:T(8,128)(2,1)S(1)} %get-tuple-element.277), channel_id=1, source_target_pairs={{48,0},{52,4},{56,8},{60,12},{64,16},{68,20},{72,24},{76,28},{80,3... | collective-permute-start | bytes 1572872 | tf_op jit(solution)/shard_map/cond/branch_11_fun/ppermute | solution.py:122
  95.4 14.9 %collective-permute-start.87 = (bf16[4,3,128,128]{3,2,1,0:T(8,128)(2,1)}, bf16[4,3,128,128]{3,2,1,0:T(8,128)(2,1)}, u32[]{:S(2)}, u32[]{:S(2)}) collective-permute-start(bf16[4,3,128,128]{3,2,1,0:T(8,128)(2,1)} %get-tuple-element.278), channel_id=1, source_target_pairs={{0,1},{1,2},{2,3},{3,0},{4,5},{5,6},{6,7},{7,4},{8,9},{9,10},{10,1... | collective-permute-start | bytes 1179656 | tf_op jit(solution)/shard_map/cond/branch_11_fun/ppermute | solution.py:95
  98.7 19.3 %collective-permute-start.88 = (bf16[4,3,128,128]{3,2,1,0:T(8,128)(2,1)S(1)}, bf16[4,3,128,128]{3,2,1,0:T(8,128)(2,1)}, u32[]{:S(2)}, u32[]{:S(2)}) collective-permute-start(bf16[4,3,128,128]{3,2,1,0:T(8,128)(2,1)S(1)} %get-tuple-element.279), channel_id=1, source_target_pairs={{0,2},{1,3},{2,0},{3,1},{4,6},{5,7},{6,4},{7,5},{8,10},{9,11},{10,... | collective-permute-start | bytes 1179656 | tf_op jit(solution)/shard_map/cond/branch_11_fun/ppermute | solution.py:95
  103.4 16.3 %collective-permute-start.89 = (bf16[4,3,128,128]{3,2,1,0:T(8,128)(2,1)S(1)}, bf16[4,3,128,128]{3,2,1,0:T(8,128)(2,1)}, u32[]{:S(2)}, u32[]{:S(2)}) collective-permute-start(bf16[4,3,128,128]{3,2,1,0:T(8,128)(2,1)S(1)} %get-tuple-element.280), channel_id=1, source_target_pairs={{0,3},{1,0},{2,1},{3,2},{4,7},{5,4},{6,5},{7,6},{8,11},{9,8},{10,9... | collective-permute-start | bytes 1179656 | tf_op jit(solution)/shard_map/cond/branch_11_fun/ppermute | solution.py:95
  123.7 2.8 %copy-start.3 = (f32[128,1024]{1,0:T(8,128)S(1)}, f32[128,1024]{1,0:T(8,128)}, u32[]{:S(2)}) copy-start(f32[128,1024]{1,0:T(8,128)} %copy-done.2) | copy-start | bytes 1572868
  123.7 2.8 %copy-start.5 = (f32[128,1024]{1,0:T(8,128)S(1)}, f32[128,1024]{1,0:T(8,128)}, u32[]{:S(2)}) copy-start(f32[128,1024]{1,0:T(8,128)} %copy-done.4) | copy-start | bytes 1572868
  130.5 11.3 %collective-permute-start.104 = (bf16[4,1,128,128]{3,2,1,0:T(8,128)(2,1)}, bf16[4,1,128,128]{3,2,1,0:T(8,128)(2,1)S(1)}, u32[]{:S(2)}, u32[]{:S(2)}) collective-permute-start(bf16[4,1,128,128]{3,2,1,0:T(8,128)(2,1)} %bitcast.80), channel_id=1, source_target_pairs={{0,3},{1,0},{2,1},{3,2},{4,7},{5,4},{6,5},{7,6},{8,11},{9,8},{10,9... | collective-permute-start | bytes 393224 | tf_op jit(solution)/shard_map/ppermute | solution.py:95
  134.7 9.8 %collective-permute-start.103 = (bf16[4,1,128,128]{3,2,1,0:T(8,128)(2,1)}, bf16[4,1,128,128]{3,2,1,0:T(8,128)(2,1)S(1)}, u32[]{:S(2)}, u32[]{:S(2)}) collective-permute-start(bf16[4,1,128,128]{3,2,1,0:T(8,128)(2,1)} %bitcast.81), channel_id=1, source_target_pairs={{0,2},{1,3},{2,0},{3,1},{4,6},{5,7},{6,4},{7,5},{8,10},{9,11},{10,... | collective-permute-start | bytes 393224 | tf_op jit(solution)/shard_map/ppermute | solution.py:95
  137.3 8.8 %collective-permute-start.102 = (bf16[4,1,128,128]{3,2,1,0:T(8,128)(2,1)}, bf16[4,1,128,128]{3,2,1,0:T(8,128)(2,1)S(1)}, u32[]{:S(2)}, u32[]{:S(2)}) collective-permute-start(bf16[4,1,128,128]{3,2,1,0:T(8,128)(2,1)} %bitcast.82), channel_id=1, source_target_pairs={{0,1},{1,2},{2,3},{3,0},{4,5},{5,6},{6,7},{7,4},{8,9},{9,10},{10,1... | collective-permute-start | bytes 393224 | tf_op jit(solution)/shard_map/ppermute | solution.py:95

commit v5 on v4

--- a/solution.py
+++ b/solution.py
@@ -82,26 +82,19 @@
     me = lax.axis_index("win")
     pieces = corr.reshape(groups, -1, *corr.shape[1:])
     own = lax.dynamic_index_in_dim(pieces, me, 0, keepdims=False)
-    sent = [
-        lax.dynamic_index_in_dim(pieces, (me + by) % groups, 0, keepdims=False).astype(jnp.bfloat16)
-        for by in range(1, groups)
-    ]
-    return own, sent
+    return own, pieces.astype(jnp.bfloat16)
 
 
 def pass_over_win(sent):
-    groups = lax.axis_size("win")
-    return [
-        lax.ppermute(piece, "win", [(w, (w + by) % groups) for w in range(groups)])
-        for by, piece in enumerate(sent, start=1)
-    ]
+    return lax.all_to_all(sent, "win", split_axis=0, concat_axis=0, tiled=True)
 
 
 def sum_over_win(own, arrived):
-    total = own
-    for piece in arrived:
-        total = total + piece.astype(jnp.float32)
-    return total
+    groups = lax.axis_size("win")
+    me = lax.axis_index("win")
+    others = (jnp.arange(groups) != me).astype(jnp.float32)
+    weights = others.reshape(groups, *([1] * (arrived.ndim - 1)))
+    return own + jnp.sum(arrived.astype(jnp.float32) * weights, axis=0)
 
 
 def in_blocks(array, dim, size):

time: 148 us -> 173 us (1.17)
  the two profiles are of different devices: /device:TPU:248 before, /device:TPU:240 now
where the time goes in v5:
time: 173 us; the launch traced here: 172 us
  waiting for transfers between devices  96 us (55%)
  blocking collectives  26.6 us (15%)
  matrix products  15.1 us (9%)
  starting transfers between devices  13.4 us (8%)
  other arithmetic  9.01 us (5%)
  between operations  6.12 us (4%)
  local copies, waits for them, and re-layouts  5.72 us (3%)
    ppermute x4, waiting for transfers between devices, shifted(): return lambda x: lax.ppermute(x, 'chan', pairs)  88.1 us
    all_to_all x1, blocking collectives, pass_over_win(): return lax.all_to_all(sent, 'win', split_axis=0, concat_axis=0, tiled=True)  26.6 us
    ppermute x4, starting transfers between devices, shifted(): return lambda x: lax.ppermute(x, 'chan', pairs)  9.92 us
    all_to_all x1, waiting for transfers between devices, pass_over_win(): return lax.all_to_all(sent, 'win', split_axis=0, concat_axis=0, tiled=True)  7.87 us
    dot_general x1, matrix products, whiten(): spec = jnp.dot(shaped, table, preferred_element_type=jnp.float32)  4.94 us
    dot_general x2, matrix products, lag_terms(): jnp.einsum('ctf,kjf->tkcj', first, partner[:, 0], preferred_element_type=...  4.64 us
    all_to_all x1, starting transfers between devices, pass_over_win(): return lax.all_to_all(sent, 'win', split_axis=0, concat_axis=0, tiled=True)  3.47 us
  transfers between devices with their start and end apart: 5, of which 4 were waited for; matrix products, arithmetic and copies ran while one was open for 2% of the time, Pallas kernels for 0%

profile of v5, /device:TPU:240, one launch (start us, length us, event | category | flops | bytes accessed | tf_op | source)
XLA Modules:
  0.0 172.0 jit_solution(2393150796504216008)
XLA Ops:
  0.9 1.4 convert_reduce_fusion.1
  2.3 4.9 %fusion.39 = f32[128,2048]{1,0:T(8,128)S(1)} fusion(bf16[2048,2048]{1,0:T(8,128)(2,1)} %constant.95.clone, f32[2048]{0:T(1024)S(1)} %multiply_subtract_fusion, f32[128]{0:T(128)S(1)} %broadcast_multiply_fusion, bf16[128,4096]{1,0:T(8,128)(2,1)} %param.64, s32[]{:T(128)S(6)} %select_n.70), kind=kOutput, calls=%fused_computation.56 | convolution fusion | flops 1074790400 | bytes 9970180 | tf_op jit(solution)/shard_map/dot_general | solution.py:57
  7.3 2.1 %fusion.52 = (f32[128,1024]{1,0:T(8,128)S(1)}, bf16[128,1024]{1,0:T(8,128)(2,1)S(1)}, f32[128,1024]{1,0:T(8,128)S(1)}, bf16[128,1024]{1,0:T(8,128)(2,1)S(1)}) fusion(f32[128,2048]{1,0:T(8,128)S(1)} %fusion.39, f32[1024]{0:T(1024)S(1)} %convert_reduce_fusion), kind=kOutput, calls=%fused_computation.83 | convolution fusion | flops 1617166336 | bytes 3674112 | tf_op jit(solution)/shard_map/dot_general | solution.py:61
  9.4 1.0 pad_maximum_fusion.2
  10.4 1.9 %collective-permute-start.56 = (bf16[2,128,1024]{2,1,0:T(8,128)(2,1)}, bf16[2,128,1024]{2,1,0:T(8,128)(2,1)S(1)}, u32[]{:S(2)}, u32[]{:S(2)}) collective-permute-start(bf16[2,128,1024]{2,1,0:T(8,128)(2,1)} %pad_maximum_fusion.2), channel_id=1, source_target_pairs={{60,0},{64,4},{68,8},{72,12},{76,16},{80,20},{84,24},{88,28},{92,3... | collective-permute-start | bytes 1572872 | tf_op jit(solution)/shard_map/ppermute | solution.py:115
  12.3 0.7 fusion.54
  18.2 38.1 %conditional.8 = (bf16[2,128,1024]{2,1,0:T(8,128)(2,1)}) conditional(s32[]{:T(128)} %bitcast.10, bf16[2,128,1024]{2,1,0:T(8,128)(2,1)} %pad_maximum_fusion.2, bf16[2,128,1024]{2,1,0:T(8,128)(2,1)} %pad_maximum_fusion.2, bf16[2,128,1024]{2,1,0:T(8,128)(2,1)} %pad_maximum_fusion.2, ...), branch_computations={%region_32.33_spmd, %region_33.34_spmd, %region_34.35_spmd, %regio... | conditional | bytes 2097200 | solution.py:127
  18.2 4.2 %collective-permute-start.34 = (bf16[2,128,1024]{2,1,0:T(8,128)(2,1)}, bf16[2,128,1024]{2,1,0:T(8,128)(2,1)}, u32[]{:S(2)}, u32[]{:S(2)}) collective-permute-start(bf16[2,128,1024]{2,1,0:T(8,128)(2,1)} %param.36), channel_id=1, source_target_pairs={{28,0},{32,4},{36,8},{40,12},{44,16},{48,20},{52,24},{56,28},{60,3... | collective-permute-start | bytes 1572872 | tf_op jit(solution)/shard_map/cond/branch_6_fun/ppermute | solution.py:115
  22.4 33.9 %collective-permute-done.34 = bf16[2,128,1024]{2,1,0:T(8,128)(2,1)} collective-permute-done((bf16[2,128,1024]{2,1,0:T(8,128)(2,1)}, bf16[2,128,1024]{2,1,0:T(8,128)(2,1)}, u32[]{:S(2)}, u32[]{:S(2)}) %collective-permute-start.34) | collective-permute-done | bytes 524320 | tf_op jit(solution)/shard_map/cond/branch_6_fun/ppermute | solution.py:115
  56.3 24.7 %conditional.7 = (bf16[2,128,1024]{2,1,0:T(8,128)(2,1)}) conditional(s32[]{:T(128)} %bitcast.7, bf16[2,128,1024]{2,1,0:T(8,128)(2,1)} %pad_maximum_fusion.2, bf16[2,128,1024]{2,1,0:T(8,128)(2,1)} %pad_maximum_fusion.2, bf16[2,128,1024]{2,1,0:T(8,128)(2,1)} %pad_maximum_fusion.2, ...), branch_computations={%region_17.18_spmd, %region_18.19_spmd, %region_19.20_spmd, %regio... | conditional | bytes 2097200 | solution.py:127
  56.3 1.9 %collective-permute-start.26 = (bf16[2,128,1024]{2,1,0:T(8,128)(2,1)}, bf16[2,128,1024]{2,1,0:T(8,128)(2,1)}, u32[]{:S(2)}, u32[]{:S(2)}) collective-permute-start(bf16[2,128,1024]{2,1,0:T(8,128)(2,1)} %param.27), channel_id=1, source_target_pairs={{52,0},{56,4},{60,8},{64,12},{68,16},{72,20},{76,24},{80,28},{84,3... | collective-permute-start | bytes 1572872 | tf_op jit(solution)/shard_map/cond/branch_12_fun/ppermute | solution.py:115
  58.2 22.8 %collective-permute-done.26 = bf16[2,128,1024]{2,1,0:T(8,128)(2,1)} collective-permute-done((bf16[2,128,1024]{2,1,0:T(8,128)(2,1)}, bf16[2,128,1024]{2,1,0:T(8,128)(2,1)}, u32[]{:S(2)}, u32[]{:S(2)}) %collective-permute-start.26) | collective-permute-done | bytes 524320 | tf_op jit(solution)/shard_map/cond/branch_12_fun/ppermute | solution.py:115
  81.0 33.3 %conditional.6 = (bf16[2,128,1024]{2,1,0:T(8,128)(2,1)}) conditional(s32[]{:T(128)} %bitcast.4, bf16[2,128,1024]{2,1,0:T(8,128)(2,1)} %pad_maximum_fusion.2, bf16[2,128,1024]{2,1,0:T(8,128)(2,1)} %pad_maximum_fusion.2, bf16[2,128,1024]{2,1,0:T(8,128)(2,1)} %pad_maximum_fusion.2, ...), branch_computations={%region_2.3_spmd, %region_3.4_spmd, %region_4.5_spmd, %region_5.6_... | conditional | bytes 2097200 | solution.py:127
  81.0 1.9 %collective-permute-start.8 = (bf16[2,128,1024]{2,1,0:T(8,128)(2,1)}, bf16[2,128,1024]{2,1,0:T(8,128)(2,1)}, u32[]{:S(2)}, u32[]{:S(2)}) collective-permute-start(bf16[2,128,1024]{2,1,0:T(8,128)(2,1)} %param.8), channel_id=1, source_target_pairs={{36,0},{40,4},{44,8},{48,12},{52,16},{56,20},{60,24},{64,28},{68,3... | collective-permute-start | bytes 1572872 | tf_op jit(solution)/shard_map/cond/branch_8_fun/ppermute | solution.py:115
  82.9 31.4 %collective-permute-done.8 = bf16[2,128,1024]{2,1,0:T(8,128)(2,1)} collective-permute-done((bf16[2,128,1024]{2,1,0:T(8,128)(2,1)}, bf16[2,128,1024]{2,1,0:T(8,128)(2,1)}, u32[]{:S(2)}, u32[]{:S(2)}) %collective-permute-start.8) | collective-permute-done | bytes 524320 | tf_op jit(solution)/shard_map/cond/branch_8_fun/ppermute | solution.py:115
  114.4 0.3 cosine_multiply_fusion
  114.7 1.7 select_bitcast_fusion.3
  116.6 1.9 %fusion.4 = f32[3,128,128,16]{2,1,3,0:T(8,128)S(1)} fusion(f32[16,1024]{1,0:T(8,128)S(1)} %get-tuple-element.206, f32[128,1024]{1,0:T(8,128)S(1)} %get-tuple-element.200, f32[16,1024]{1,0:T(8,128)S(1)} %get-tuple-element.205, f32[128,1024]{1,0:T(8,128)S(1)} %get-tuple-element.196, bf16[3,2,128,1024]{3,2,1,0:T(8,128)(2,1)S(1)} %pad_maximum_fusion), kind=kOutput, calls=%fused_computation.8 | convolution fusion | flops 1619001344 | bytes 5111808 | tf_op jit(solution)/shard_map/ctf,kjf->tkcj/dot_general | solution.py:77
  118.5 3.0 %fusion.28 = f32[3,128,128,16]{2,1,3,0:T(8,128)S(1)} fusion(f32[3,128,128,16]{2,1,3,0:T(8,128)S(1)} %fusion.4, f32[16,1024]{1,0:T(8,128)S(1)} %get-tuple-element.206, f32[128,1024]{1,0:T(8,128)} %copy-done.6, f32[16,1024]{1,0:T(8,128)S(1)} %get-tuple-element.205, f32[128,1024]{1,0:T(8,128)} %copy-done.3, bf16[3,2,128,1024]{3,2,1,0:T(8,128)(2,1)S(1)} %pad_maximum_fusion), kind=kOutput, calls=%fused_computation.32 | convolution fusion | flops 1619787776 | bytes 8257536 | tf_op jit(solution)/shard_map/ctf,kjf->tkcj/dot_general | solution.py:75
  121.6 1.7 copy.14
  123.2 0.9 constant_dynamic-slice_fusion
  124.2 1.4 copy.13
  125.6 27.5 %conditional.10 = (bf16[2,128,1024]{2,1,0:T(8,128)(2,1)}, bf16[4,4,3,128,128]{4,3,2,1,0:T(8,128)(2,1)}) conditional(s32[]{:T(128)} %bitcast.23, (bf16[2,128,1024]{2,1,0:T(8,128)(2,1)}, bf16[4,4,3,128,128]{4,3,2,1,0:T(8,128)(2,1)}) %tuple.265, (bf16[2,128,1024]{2,1,0:T(8,128)(2,1)}, ...), branch_computations={%region_47.48_spmd, %region_48.49_spmd, %region_49.50_spmd, %regio... | conditional | bytes 6815832
  125.6 26.6 %all_to_all.65 = bf16[4,4,3,128,128]{4,3,2,1,0:T(8,128)(2,1)} all-to-all(bf16[4,4,3,128,128]{4,3,2,1,0:T(8,128)(2,1)} %param.59), channel_id=1, replica_groups=mesh['chan'=128,'win'=4] {'win'}, dimensions={0} | all-to-all | bytes 3145728 | tf_op jit(solution)/shard_map/cond/branch_14_fun/all_to_all | solution.py:89
  152.2 0.9 broadcast.154
  153.2 1.5 fusion.2
  154.7 1.6 fusion.31
  156.3 0.9 convert_element_type.119
  157.2 3.5 %all-to-all-start.15 = ((bf16[4,4,1,128,128]{3,4,1,2,0:T(8,128)(2,1)}), bf16[4,4,1,128,128]{3,4,1,2,0:T(8,128)(2,1)S(1)}, u32[]{:S(2)}, u32[]{:S(2)}) async-start(bf16[4,4,1,128,128]{3,4,1,2,0:T(8,128)(2,1)} %convert_element_type.119), calls=%async_computation.15 | async-start | bytes 1048576 | tf_op jit(solution)/shard_map/all_to_all | solution.py:89
  160.7 1.9 %fusion.25 = f32[4,3,128,128]{3,2,1,0:T(8,128)S(1)} fusion(bf16[4,4,3,128,128]{4,3,2,1,0:T(8,128)(2,1)} %get-tuple-element.195, f32[4]{0:T(128)S(1)} %compare_convert_fusion), kind=kLoop, calls=%fused_computation.29 | loop fusion | flops 2162688 | bytes 2359312 | tf_op jit(solution)/shard_map/reduce_sum | solution.py:97
  162.7 7.9 %all-to-all-done.15 = bf16[4,4,1,128,128]{3,4,1,2,0:T(8,128)(2,1)S(1)} async-done(((bf16[4,4,1,128,128]{3,4,1,2,0:T(8,128)(2,1)}), bf16[4,4,1,128,128]{3,4,1,2,0:T(8,128)(2,1)S(1)}, u32[]{:S(2)}, u32[]{:S(2)}) %all-to-all-start.15) | async-done | bytes 524320 | tf_op jit(solution)/shard_map/all_to_all | solution.py:89
  170.9 1.0 pad_maximum_fusion.1
  (31 shorter events, 1.0 us)
Async XLA Ops:
  7.2 5.0 %copy-start.2 = (s32[4]{0:T(128)S(1)}, s32[4]{0:T(128)}, u32[]{:S(2)}) copy-start(s32[4]{0:T(128)} %param.65) | copy-start | bytes 52
  9.4 107.2 %copy-start.3 = (f32[128,1024]{1,0:T(8,128)}, f32[128,1024]{1,0:T(8,128)S(1)}, u32[]{:S(2)}) copy-start(f32[128,1024]{1,0:T(8,128)S(1)} %get-tuple-element.196) | copy-start | bytes 1572868
  9.4 107.2 %copy-start.6 = (f32[128,1024]{1,0:T(8,128)}, f32[128,1024]{1,0:T(8,128)S(1)}, u32[]{:S(2)}) copy-start(f32[128,1024]{1,0:T(8,128)S(1)} %get-tuple-element.200) | copy-start | bytes 1572868
  10.4 104.3 %collective-permute-start.56 = (bf16[2,128,1024]{2,1,0:T(8,128)(2,1)}, bf16[2,128,1024]{2,1,0:T(8,128)(2,1)S(1)}, u32[]{:S(2)}, u32[]{:S(2)}) collective-permute-start(bf16[2,128,1024]{2,1,0:T(8,128)(2,1)} %pad_maximum_fusion.2), channel_id=1, source_target_pairs={{60,0},{64,4},{68,8},{72,12},{76,16},{80,20},{84,24},{88,28},{92,3... | collective-permute-start | bytes 1572872 | tf_op jit(solution)/shard_map/ppermute | solution.py:115
  18.2 38.1 %collective-permute-start.34 = (bf16[2,128,1024]{2,1,0:T(8,128)(2,1)}, bf16[2,128,1024]{2,1,0:T(8,128)(2,1)}, u32[]{:S(2)}, u32[]{:S(2)}) collective-permute-start(bf16[2,128,1024]{2,1,0:T(8,128)(2,1)} %param.36), channel_id=1, source_target_pairs={{28,0},{32,4},{36,8},{40,12},{44,16},{48,20},{52,24},{56,28},{60,3... | collective-permute-start | bytes 1572872 | tf_op jit(solution)/shard_map/cond/branch_6_fun/ppermute | solution.py:115
  56.3 24.7 %collective-permute-start.26 = (bf16[2,128,1024]{2,1,0:T(8,128)(2,1)}, bf16[2,128,1024]{2,1,0:T(8,128)(2,1)}, u32[]{:S(2)}, u32[]{:S(2)}) collective-permute-start(bf16[2,128,1024]{2,1,0:T(8,128)(2,1)} %param.27), channel_id=1, source_target_pairs={{52,0},{56,4},{60,8},{64,12},{68,16},{72,20},{76,24},{80,28},{84,3... | collective-permute-start | bytes 1572872 | tf_op jit(solution)/shard_map/cond/branch_12_fun/ppermute | solution.py:115
  81.0 33.3 %collective-permute-start.8 = (bf16[2,128,1024]{2,1,0:T(8,128)(2,1)}, bf16[2,128,1024]{2,1,0:T(8,128)(2,1)}, u32[]{:S(2)}, u32[]{:S(2)}) collective-permute-start(bf16[2,128,1024]{2,1,0:T(8,128)(2,1)} %param.8), channel_id=1, source_target_pairs={{36,0},{40,4},{44,8},{48,12},{52,16},{56,20},{60,24},{64,28},{68,3... | collective-permute-start | bytes 1572872 | tf_op jit(solution)/shard_map/cond/branch_8_fun/ppermute | solution.py:115
  114.7 1.9 %copy-start = (bf16[2,128,1024]{2,1,0:T(8,128)(2,1)}, bf16[2,128,1024]{2,1,0:T(8,128)(2,1)S(1)}, u32[]{:S(2)}) copy-start(bf16[2,128,1024]{2,1,0:T(8,128)(2,1)S(1)} %collective-permute-done.56) | copy-start | bytes 1572868
  125.6 27.5 %copy-start.1 = (bf16[2,128,1024]{2,1,0:T(8,128)(2,1)S(1)}, bf16[2,128,1024]{2,1,0:T(8,128)(2,1)}, u32[]{:S(2)}) copy-start(bf16[2,128,1024]{2,1,0:T(8,128)(2,1)} %copy-done) | copy-start | bytes 1572868
  125.6 27.6 %copy-start.4 = (f32[128,1024]{1,0:T(8,128)S(1)}, f32[128,1024]{1,0:T(8,128)}, u32[]{:S(2)}) copy-start(f32[128,1024]{1,0:T(8,128)} %copy-done.3) | copy-start | bytes 1572868
  125.6 27.6 %copy-start.7 = (f32[128,1024]{1,0:T(8,128)S(1)}, f32[128,1024]{1,0:T(8,128)}, u32[]{:S(2)}) copy-start(f32[128,1024]{1,0:T(8,128)} %copy-done.6) | copy-start | bytes 1572868
  153.2 1.6 copy-start.5
  153.2 1.6 copy-start.8
  157.2 13.4 %all-to-all-start.15 = ((bf16[4,4,1,128,128]{3,4,1,2,0:T(8,128)(2,1)}), bf16[4,4,1,128,128]{3,4,1,2,0:T(8,128)(2,1)S(1)}, u32[]{:S(2)}, u32[]{:S(2)}) async-start(bf16[4,4,1,128,128]{3,4,1,2,0:T(8,128)(2,1)} %convert_element_type.119), calls=%async_computation.15 | async-start | bytes 1048576 | tf_op jit(solution)/shard_map/all_to_all | solution.py:89

commit v6 on v5

--- a/solution.py
+++ b/solution.py
@@ -116,29 +116,26 @@
 
     far = OFFCAP - 1
     farthest = shifted(far)(spectra)
-    moves = [shifted(by) for by in range(1, far)] + [jnp.zeros_like]
+    moves = [shifted(by) for by in range(1, far)]
     cos_w, sin_w = phase_tables(groups)
     first, second = lag_factors(own_re, own_im, cos_w, sin_w)
-
-    def fetched(k, moved):
-        return jnp.where(offsets[k] == far, farthest, moved)
-
-    early = jnp.stack(
-        [fetched(k, lax.switch(offsets[k] - 1, moves, spectra)) for k in range(K - 1)], axis=0
-    )
-
+    order = jnp.sort(offsets)
+    rank = jnp.sum(offsets[None, :] < offsets[:, None], axis=1)
+    nearer = [lax.switch(order[k] - 1, moves, spectra) for k in range(K - 2)]
+    early = jnp.stack([farthest] + nearer, axis=0)
     early_own, early_sent = split_for_win(lag_terms(first, second, early))
 
     def with_early(move):
         return lambda x, sent: (move(x), pass_over_win(sent))
 
     last, early_arrived = lax.switch(
-        offsets[K - 1] - 1, [with_early(move) for move in moves], spectra, early_sent
+        order[K - 2] - 1, [with_early(move) for move in moves], spectra, early_sent
     )
-    last_own, last_sent = split_for_win(lag_terms(first, second, fetched(K - 1, last)[None]))
+    last_own, last_sent = split_for_win(lag_terms(first, second, last[None]))
     early_sum = sum_over_win(early_own, early_arrived)
     last_sum = sum_over_win(last_own, pass_over_win(last_sent))
-    return jnp.concatenate([early_sum, last_sum], axis=1)
+    by_rank = jnp.concatenate([early_sum[:, 1:], last_sum, early_sum[:, :1]], axis=1)
+    return jnp.take(by_rank, rank, axis=1)
 
 
 def solution(mesh):

time: 173 us -> 150 us (0.87)
  the two profiles are of different devices: /device:TPU:240 before, /device:TPU:248 now
where the time goes in v6:
time: 150 us; the launch traced here: 149 us
  waiting for transfers between devices  89.3 us (60%)
  starting transfers between devices  20.9 us (14%)
  matrix products  17.4 us (12%)
  other arithmetic  9.69 us (6%)
  local copies, waits for them, and re-layouts  8.6 us (6%)
  between operations  2.83 us (2%)
    ppermute x4, waiting for transfers between devices, shifted(): return lambda x: lax.ppermute(x, 'chan', pairs)  82.6 us
    ppermute x4, starting transfers between devices, shifted(): return lambda x: lax.ppermute(x, 'chan', pairs)  12.4 us
    all_to_all x2, starting transfers between devices, pass_over_win(): return lax.all_to_all(sent, 'win', split_axis=0, concat_axis=0, tiled=True)  8.49 us
    all_to_all x2, waiting for transfers between devices, pass_over_win(): return lax.all_to_all(sent, 'win', split_axis=0, concat_axis=0, tiled=True)  6.67 us
    dot_general x2, matrix products, lag_terms(): jnp.einsum('ctf,kjf->tkcj', first, partner[:, 0], preferred_element_type=...  5.92 us
    dot_general x1, matrix products, whiten(): spec = jnp.dot(shaped, table, preferred_element_type=jnp.float32)  4.94 us
    dot_general x2, matrix products, lag_terms(): jnp.einsum('ctf,kjf->tkcj', second, partner[:, 1], preferred_element_type...  4.4 us
    dynamic_slice x4, local copies, waits for them, and re-layouts, split_for_win(): own = lax.dynamic_index_in_dim(pieces, me, 0, keepdims=False)  3.45 us
  transfers between devices with their start and end apart: 6, of which 5 were waited for; matrix products, arithmetic and copies ran while one was open for 5% of the time, Pallas kernels for 0%

profile of v6, /device:TPU:248, one launch (start us, length us, event | category | flops | bytes accessed | tf_op | source)
XLA Modules:
  0.0 149.1 jit_solution(11969871646660416691)
XLA Ops:
  0.9 1.4 convert_reduce_fusion.1
  2.3 4.9 %fusion.39 = f32[128,2048]{1,0:T(8,128)S(1)} fusion(bf16[2048,2048]{1,0:T(8,128)(2,1)} %constant.91.clone, f32[2048]{0:T(1024)S(1)} %multiply_subtract_fusion, f32[128]{0:T(128)S(1)} %broadcast_multiply_fusion, bf16[128,4096]{1,0:T(8,128)(2,1)} %param.46, s32[]{:T(128)S(6)} %select_n.64), kind=kOutput, calls=%fused_computation.54 | convolution fusion | flops 1074790400 | bytes 9970180 | tf_op jit(solution)/shard_map/dot_general | solution.py:57
  7.3 2.1 %fusion.53 = (f32[128,1024]{1,0:T(8,128)S(1)}, bf16[128,1024]{1,0:T(8,128)(2,1)S(1)}, f32[128,1024]{1,0:T(8,128)S(1)}, bf16[128,1024]{1,0:T(8,128)(2,1)S(1)}) fusion(f32[128,2048]{1,0:T(8,128)S(1)} %fusion.39, f32[1024]{0:T(1024)S(1)} %convert_reduce_fusion), kind=kOutput, calls=%fused_computation.88 | convolution fusion | flops 1617166336 | bytes 3674112 | tf_op jit(solution)/shard_map/dot_general | solution.py:61
  9.4 0.9 pad_maximum_fusion.2
  10.3 1.9 %collective-permute-start.42 = (bf16[2,128,1024]{2,1,0:T(8,128)(2,1)}, bf16[2,128,1024]{2,1,0:T(8,128)(2,1)S(1)}, u32[]{:S(2)}, u32[]{:S(2)}) collective-permute-start(bf16[2,128,1024]{2,1,0:T(8,128)(2,1)} %pad_maximum_fusion.2), channel_id=1, source_target_pairs={{60,0},{64,4},{68,8},{72,12},{76,16},{80,20},{84,24},{88,28},{92,3... | collective-permute-start | bytes 1572872 | tf_op jit(solution)/shard_map/ppermute | solution.py:115
  14.6 43.2 %conditional.5 = (bf16[1,2,128,1024]{3,2,1,0:T(8,128)(2,1)}) conditional(s32[]{:T(128)} %bitcast.32, bf16[2,128,1024]{2,1,0:T(8,128)(2,1)} %pad_maximum_fusion.2, bf16[2,128,1024]{2,1,0:T(8,128)(2,1)} %pad_maximum_fusion.2, bf16[2,128,1024]{2,1,0:T(8,128)(2,1)} %pad_maximum_fusion.2, ...), branch_computations={%region_4.5_spmd, %region_5.6_spmd, %region_6.7_spmd, %region_7.8_... | conditional | bytes 2097200 | solution.py:124
  14.6 4.8 %collective-permute-start.5 = (bf16[2,128,1024]{2,1,0:T(8,128)(2,1)}, bf16[2,128,1024]{2,1,0:T(8,128)(2,1)}, u32[]{:S(2)}, u32[]{:S(2)}) collective-permute-start(bf16[2,128,1024]{2,1,0:T(8,128)(2,1)} %param.5), channel_id=1, source_target_pairs={{24,0},{28,4},{32,8},{36,12},{40,16},{44,20},{48,24},{52,28},{56,3... | collective-permute-start | bytes 1572872 | tf_op jit(solution)/shard_map/cond/branch_5_fun/ppermute | solution.py:115
  19.5 38.3 %collective-permute-done.5 = bf16[2,128,1024]{2,1,0:T(8,128)(2,1)} collective-permute-done((bf16[2,128,1024]{2,1,0:T(8,128)(2,1)}, bf16[2,128,1024]{2,1,0:T(8,128)(2,1)}, u32[]{:S(2)}, u32[]{:S(2)}) %collective-permute-start.5) | collective-permute-done | bytes 524320 | tf_op jit(solution)/shard_map/cond/branch_5_fun/ppermute | solution.py:115
  58.4 31.8 %conditional.6 = (bf16[1,2,128,1024]{3,2,1,0:T(8,128)(2,1)}) conditional(s32[]{:T(128)} %bitcast.33, bf16[2,128,1024]{2,1,0:T(8,128)(2,1)} %pad_maximum_fusion.2, bf16[2,128,1024]{2,1,0:T(8,128)(2,1)} %pad_maximum_fusion.2, bf16[2,128,1024]{2,1,0:T(8,128)(2,1)} %pad_maximum_fusion.2, ...), branch_computations={%region_18.19_spmd, %region_19.20_spmd, %region_20.21_spmd, %regio... | conditional | bytes 2097200 | solution.py:124
  58.4 3.7 %collective-permute-start.21 = (bf16[2,128,1024]{2,1,0:T(8,128)(2,1)}, bf16[2,128,1024]{2,1,0:T(8,128)(2,1)}, u32[]{:S(2)}, u32[]{:S(2)}) collective-permute-start(bf16[2,128,1024]{2,1,0:T(8,128)(2,1)} %param.21), channel_id=1, source_target_pairs={{32,0},{36,4},{40,8},{44,12},{48,16},{52,20},{56,24},{60,28},{64,3... | collective-permute-start | bytes 1572872 | tf_op jit(solution)/shard_map/cond/branch_7_fun/ppermute | solution.py:115
  62.2 28.1 %collective-permute-done.21 = bf16[2,128,1024]{2,1,0:T(8,128)(2,1)} collective-permute-done((bf16[2,128,1024]{2,1,0:T(8,128)(2,1)}, bf16[2,128,1024]{2,1,0:T(8,128)(2,1)}, u32[]{:S(2)}, u32[]{:S(2)}) %collective-permute-start.21) | collective-permute-done | bytes 524320 | tf_op jit(solution)/shard_map/cond/branch_7_fun/ppermute | solution.py:115
  91.2 1.4 pad_maximum_fusion
  92.6 1.9 %fusion.4 = f32[3,128,128,16]{2,1,3,0:T(8,128)S(1)} fusion(f32[16,1024]{1,0:T(8,128)S(1)} %get-tuple-element.301, f32[128,1024]{1,0:T(8,128)S(1)} %get-tuple-element.298, f32[16,1024]{1,0:T(8,128)S(1)} %get-tuple-element.300, f32[128,1024]{1,0:T(8,128)S(1)} %get-tuple-element.294, bf16[3,2,128,1024]{3,2,1,0:T(8,128)(2,1)S(1)} %pad_maximum_fusion), kind=kOutput, calls=%fused_computation.9 | convolution fusion | flops 1619001344 | bytes 5111808 | tf_op jit(solution)/shard_map/ctf,kjf->tkcj/dot_general | solution.py:77
  94.5 3.0 %fusion.28 = f32[3,128,128,16]{2,1,3,0:T(8,128)S(1)} fusion(f32[3,128,128,16]{2,1,3,0:T(8,128)S(1)} %fusion.4, f32[16,1024]{1,0:T(8,128)S(1)} %get-tuple-element.301, f32[128,1024]{1,0:T(8,128)} %copy-done.4, f32[16,1024]{1,0:T(8,128)S(1)} %get-tuple-element.300, f32[128,1024]{1,0:T(8,128)} %copy-done.2, bf16[3,2,128,1024]{3,2,1,0:T(8,128)(2,1)S(1)} %pad_maximum_fusion), kind=kOutput, calls=%fused_computation.33 | convolution fusion | flops 1619787776 | bytes 8257536 | tf_op jit(solution)/shard_map/ctf,kjf->tkcj/dot_general | solution.py:75
  97.5 27.6 %conditional.8 = (bf16[2,128,1024]{2,1,0:T(8,128)(2,1)}, bf16[4,4,3,128,128]{4,3,2,1,0:T(8,128)(2,1)}) conditional(s32[]{:T(128)} %bitcast.45, (bf16[2,128,1024]{2,1,0:T(8,128)(2,1)}, f32[4,4,3,128,128]{3,4,1,0,2:T(8,128)S(1)}) %tuple.366, (bf16[2,128,1024]{2,1,0:T(8,128)(2,1)}, ...), branch_computations={%region_32.33_spmd, %region_33.34_spmd, %region_34.35_spmd, %regio... | conditional | bytes 11534424
  97.8 1.7 %copy.70 = bf16[4,4,3,128,128]{4,3,2,1,0:T(8,128)(2,1)} copy(f32[4,4,3,128,128]{3,4,1,0,2:T(8,128)S(1)} %get-tuple-element.290) | data formatting | bytes 4718592 | tf_op jit(solution)/shard_map
  99.5 4.4 %all-to-all-start.13 = ((bf16[4,4,3,128,128]{4,3,2,1,0:T(8,128)(2,1)}), bf16[4,4,3,128,128]{4,3,2,1,0:T(8,128)(2,1)}, u32[]{:S(2)}, u32[]{:S(2)}) async-start(bf16[4,4,3,128,128]{4,3,2,1,0:T(8,128)(2,1)} %copy.70), calls=%async_computation.13 | async-start | bytes 3145728 | tf_op jit(solution)/shard_map/cond/branch_13_fun/all_to_all | solution.py:89
  103.9 1.9 %collective-permute-start.41 = (bf16[2,128,1024]{2,1,0:T(8,128)(2,1)}, bf16[2,128,1024]{2,1,0:T(8,128)(2,1)}, u32[]{:S(2)}, u32[]{:S(2)}) collective-permute-start(bf16[2,128,1024]{2,1,0:T(8,128)(2,1)} %get-tuple-element.170), channel_id=1, source_target_pairs={{56,0},{60,4},{64,8},{68,12},{72,16},{76,20},{80,24},{84,28},{88,3... | collective-permute-start | bytes 1572872 | tf_op jit(solution)/shard_map/cond/branch_13_fun/ppermute | solution.py:115
  105.8 16.2 %collective-permute-done.41 = bf16[2,128,1024]{2,1,0:T(8,128)(2,1)} collective-permute-done((bf16[2,128,1024]{2,1,0:T(8,128)(2,1)}, bf16[2,128,1024]{2,1,0:T(8,128)(2,1)}, u32[]{:S(2)}, u32[]{:S(2)}) %collective-permute-start.41) | collective-permute-done | bytes 524320 | tf_op jit(solution)/shard_map/cond/branch_13_fun/ppermute | solution.py:115
  122.0 3.1 %all-to-all-done.13 = bf16[4,4,3,128,128]{4,3,2,1,0:T(8,128)(2,1)} async-done(((bf16[4,4,3,128,128]{4,3,2,1,0:T(8,128)(2,1)}), bf16[4,4,3,128,128]{4,3,2,1,0:T(8,128)(2,1)}, u32[]{:S(2)}, u32[]{:S(2)}) %all-to-all-start.13) | async-done | bytes 1572896 | tf_op jit(solution)/shard_map/cond/branch_13_fun/all_to_all | solution.py:89
  125.1 2.9 %fusion = f32[128,128,16]{1,0,2:T(8,128)S(1)} fusion(f32[16,1024]{1,0:T(8,128)S(1)} %get-tuple-element.301, f32[128,1024]{1,0:T(8,128)} %copy-done.4, f32[16,1024]{1,0:T(8,128)S(1)} %get-tuple-element.300, f32[128,1024]{1,0:T(8,128)} %copy-done.2, bf16[1,2,128,1024]{3,2,1,0:T(8,128)(2,1)} %bitcast.47), kind=kOutput, calls=%fused_computation.5 | convolution fusion | flops 545259520 | bytes 2490368 | tf_op jit(solution)/shard_map/ctf,kjf->tkcj/dot_general | solution.py:75
  128.0 2.5 %fusion.31 = f32[128,128,16]{1,0,2:T(8,128)S(1)} fusion(f32[128,128,16]{1,0,2:T(8,128)S(1)} %fusion, f32[16,1024]{1,0:T(8,128)S(1)} %get-tuple-element.301, f32[128,1024]{1,0:T(8,128)S(1)} %copy-done.5, f32[16,1024]{1,0:T(8,128)S(1)} %get-tuple-element.300, f32[128,1024]{1,0:T(8,128)S(1)} %copy-done.3, bf16[1,2,128,1024]{3,2,1,0:T(8,128)(2,1)} %bitcast.47), kind=kOutput, calls=%fused_computation.35 | convolution fusion | flops 545521664 | bytes 3538944 | tf_op jit(solution)/shard_map/ctf,kjf->tkcj/dot_general | solution.py:77
  130.6 1.0 copy-done
  131.5 0.9 convert_element_type.157
  132.4 4.1 %all-to-all-start.14 = ((bf16[4,4,1,128,128]{3,4,1,2,0:T(8,128)(2,1)}), bf16[4,4,1,128,128]{3,4,1,2,0:T(8,128)(2,1)}, u32[]{:S(2)}, u32[]{:S(2)}) async-start(bf16[4,4,1,128,128]{3,4,1,2,0:T(8,128)(2,1)} %convert_element_type.157), calls=%async_computation.14 | async-start | bytes 1048576 | tf_op jit(solution)/shard_map/all_to_all | solution.py:89
  136.5 1.0 constant_dynamic-slice_fusion.1
  137.5 1.4 copy.56
  138.9 1.9 %fusion.25 = f32[4,3,128,128]{3,2,1,0:T(8,128)S(1)} fusion(bf16[4,4,3,128,128]{4,3,2,1,0:T(8,128)(2,1)} %get-tuple-element.293, f32[4]{0:T(128)S(1)} %compare_convert_fusion), kind=kLoop, calls=%fused_computation.30 | loop fusion | flops 2162688 | bytes 2359312 | tf_op jit(solution)/shard_map/reduce_sum | solution.py:97
  141.0 1.0 constant_dynamic-slice_fusion
  142.1 3.6 %all-to-all-done.14 = bf16[4,4,1,128,128]{3,4,1,2,0:T(8,128)(2,1)} async-done(((bf16[4,4,1,128,128]{3,4,1,2,0:T(8,128)(2,1)}), bf16[4,4,1,128,128]{3,4,1,2,0:T(8,128)(2,1)}, u32[]{:S(2)}, u32[]{:S(2)}) %all-to-all-start.14) | async-done | bytes 524320 | tf_op jit(solution)/shard_map/all_to_all | solution.py:89
  145.7 1.2 bitcast_reduce_fusion
  148.0 1.1 copy.75
  (35 shorter events, 3.6 us)
Async XLA Ops:
  7.2 5.0 %copy-start.1 = (s32[4]{0:T(128)S(1)}, s32[4]{0:T(128)}, u32[]{:S(2)}) copy-start(s32[4]{0:T(128)} %param.47) | copy-start | bytes 52
  9.4 83.2 %copy-start.2 = (f32[128,1024]{1,0:T(8,128)}, f32[128,1024]{1,0:T(8,128)S(1)}, u32[]{:S(2)}) copy-start(f32[128,1024]{1,0:T(8,128)S(1)} %get-tuple-element.294) | copy-start | bytes 1572868
  9.4 83.2 %copy-start.4 = (f32[128,1024]{1,0:T(8,128)}, f32[128,1024]{1,0:T(8,128)S(1)}, u32[]{:S(2)}) copy-start(f32[128,1024]{1,0:T(8,128)S(1)} %get-tuple-element.298) | copy-start | bytes 1572868
  10.3 80.9 %collective-permute-start.42 = (bf16[2,128,1024]{2,1,0:T(8,128)(2,1)}, bf16[2,128,1024]{2,1,0:T(8,128)(2,1)S(1)}, u32[]{:S(2)}, u32[]{:S(2)}) collective-permute-start(bf16[2,128,1024]{2,1,0:T(8,128)(2,1)} %pad_maximum_fusion.2), channel_id=1, source_target_pairs={{60,0},{64,4},{68,8},{72,12},{76,16},{80,20},{84,24},{88,28},{92,3... | collective-permute-start | bytes 1572872 | tf_op jit(solution)/shard_map/ppermute | solution.py:115
  14.6 43.2 %collective-permute-start.5 = (bf16[2,128,1024]{2,1,0:T(8,128)(2,1)}, bf16[2,128,1024]{2,1,0:T(8,128)(2,1)}, u32[]{:S(2)}, u32[]{:S(2)}) collective-permute-start(bf16[2,128,1024]{2,1,0:T(8,128)(2,1)} %param.5), channel_id=1, source_target_pairs={{24,0},{28,4},{32,8},{36,12},{40,16},{44,20},{48,24},{52,28},{56,3... | collective-permute-start | bytes 1572872 | tf_op jit(solution)/shard_map/cond/branch_5_fun/ppermute | solution.py:115
  58.4 31.8 %collective-permute-start.21 = (bf16[2,128,1024]{2,1,0:T(8,128)(2,1)}, bf16[2,128,1024]{2,1,0:T(8,128)(2,1)}, u32[]{:S(2)}, u32[]{:S(2)}) collective-permute-start(bf16[2,128,1024]{2,1,0:T(8,128)(2,1)} %param.21), channel_id=1, source_target_pairs={{32,0},{36,4},{40,8},{44,12},{48,16},{52,20},{56,24},{60,28},{64,3... | collective-permute-start | bytes 1572872 | tf_op jit(solution)/shard_map/cond/branch_7_fun/ppermute | solution.py:115
  99.5 25.6 %all-to-all-start.13 = ((bf16[4,4,3,128,128]{4,3,2,1,0:T(8,128)(2,1)}), bf16[4,4,3,128,128]{4,3,2,1,0:T(8,128)(2,1)}, u32[]{:S(2)}, u32[]{:S(2)}) async-start(bf16[4,4,3,128,128]{4,3,2,1,0:T(8,128)(2,1)} %copy.70), calls=%async_computation.13 | async-start | bytes 3145728 | tf_op jit(solution)/shard_map/cond/branch_13_fun/all_to_all | solution.py:89
  103.9 18.2 %collective-permute-start.41 = (bf16[2,128,1024]{2,1,0:T(8,128)(2,1)}, bf16[2,128,1024]{2,1,0:T(8,128)(2,1)}, u32[]{:S(2)}, u32[]{:S(2)}) collective-permute-start(bf16[2,128,1024]{2,1,0:T(8,128)(2,1)} %get-tuple-element.170), channel_id=1, source_target_pairs={{56,0},{60,4},{64,8},{68,12},{72,16},{76,20},{80,24},{84,28},{88,3... | collective-permute-start | bytes 1572872 | tf_op jit(solution)/shard_map/cond/branch_13_fun/ppermute | solution.py:115
  125.1 2.9 %copy-start.3 = (f32[128,1024]{1,0:T(8,128)S(1)}, f32[128,1024]{1,0:T(8,128)}, u32[]{:S(2)}) copy-start(f32[128,1024]{1,0:T(8,128)} %copy-done.2) | copy-start | bytes 1572868
  125.1 2.9 %copy-start.5 = (f32[128,1024]{1,0:T(8,128)S(1)}, f32[128,1024]{1,0:T(8,128)}, u32[]{:S(2)}) copy-start(f32[128,1024]{1,0:T(8,128)} %copy-done.4) | copy-start | bytes 1572868
  130.5 1.0 copy-start
  132.4 13.3 %all-to-all-start.14 = ((bf16[4,4,1,128,128]{3,4,1,2,0:T(8,128)(2,1)}), bf16[4,4,1,128,128]{3,4,1,2,0:T(8,128)(2,1)}, u32[]{:S(2)}, u32[]{:S(2)}) async-start(bf16[4,4,1,128,128]{3,4,1,2,0:T(8,128)(2,1)} %convert_element_type.157), calls=%async_computation.14 | async-start | bytes 1048576 | tf_op jit(solution)/shard_map/all_to_all | solution.py:89

commit v7 on v6

--- a/solution.py
+++ b/solution.py
@@ -60,21 +60,19 @@
     level = (
         jnp.dot(jnp.sqrt(real * real + imag * imag), band, precision=lax.Precision.HIGHEST) + 1e-05
     )
-    return ((real / level).astype(jnp.bfloat16), (imag / level).astype(jnp.bfloat16))
+    return (spec / jnp.concatenate([level, level], axis=1)).astype(jnp.bfloat16)
 
 
-def lag_factors(own_re, own_im, cos_w, sin_w):
-    ar = own_re.astype(jnp.float32)[:, None, :]
-    ai = own_im.astype(jnp.float32)[:, None, :]
-    first = (ar * cos_w[None] - ai * sin_w[None]).astype(jnp.bfloat16)
-    second = (ar * sin_w[None] + ai * cos_w[None]).astype(jnp.bfloat16)
-    return first, second
+def lag_factors(white, cos_w, sin_w):
+    ar = white[:, None, :NBIN].astype(jnp.float32)
+    ai = white[:, None, NBIN:].astype(jnp.float32)
+    first = ar * cos_w[None] - ai * sin_w[None]
+    second = ar * sin_w[None] + ai * cos_w[None]
+    return jnp.concatenate([first, second], axis=2).astype(jnp.bfloat16)
 
 
-def lag_terms(first, second, partner):
-    return jnp.einsum(
-        "ctf,kjf->tkcj", first, partner[:, 0], preferred_element_type=jnp.float32
-    ) + jnp.einsum("ctf,kjf->tkcj", second, partner[:, 1], preferred_element_type=jnp.float32)
+def lag_terms(factors, partner):
+    return jnp.einsum("ctf,kjf->tkcj", factors, partner, preferred_element_type=jnp.float32)
 
 
 def split_for_win(corr):
@@ -107,8 +105,7 @@
     groups = lax.axis_size("win")
     me = lax.axis_index("chan")
     frames = lax.dynamic_slice_in_dim(records, starts[0], WIN, 1)
-    own_re, own_im = whiten(frames, dft_table(), taper_weights(), band_matrix())
-    spectra = jnp.stack((own_re, own_im), axis=0)
+    spectra = whiten(frames, dft_table(), taper_weights(), band_matrix())
 
     def shifted(by):
         pairs = [(i + by, i) for i in range(n_chan - by)]
@@ -118,12 +115,12 @@
     farthest = shifted(far)(spectra)
     moves = [shifted(by) for by in range(1, far)]
     cos_w, sin_w = phase_tables(groups)
-    first, second = lag_factors(own_re, own_im, cos_w, sin_w)
+    factors = lag_factors(spectra, cos_w, sin_w)
     order = jnp.sort(offsets)
     rank = jnp.sum(offsets[None, :] < offsets[:, None], axis=1)
     nearer = [lax.switch(order[k] - 1, moves, spectra) for k in range(K - 2)]
     early = jnp.stack([farthest] + nearer, axis=0)
-    early_own, early_sent = split_for_win(lag_terms(first, second, early))
+    early_own, early_sent = split_for_win(lag_terms(factors, early))
 
     def with_early(move):
         return lambda x, sent: (move(x), pass_over_win(sent))
@@ -131,7 +128,7 @@
     last, early_arrived = lax.switch(
         order[K - 2] - 1, [with_early(move) for move in moves], spectra, early_sent
     )
-    last_own, last_sent = split_for_win(lag_terms(first, second, last[None]))
+    last_own, last_sent = split_for_win(lag_terms(factors, last[None]))
     early_sum = sum_over_win(early_own, early_arrived)
     last_sum = sum_over_win(last_own, pass_over_win(last_sent))
     by_rank = jnp.concatenate([early_sum[:, 1:], last_sum, early_sum[:, :1]], axis=1)

time: 150 us -> 151 us (level)
  the two profiles are of different devices: /device:TPU:248 before, /device:TPU:320 now
where the time goes in v7:
time: 151 us; the launch traced here: 150 us
  waiting for transfers between devices  79.1 us (52%)
  starting transfers between devices  28.1 us (19%)
  matrix products  18.4 us (12%)
  other arithmetic  12.2 us (8%)
  local copies, waits for them, and re-layouts  9.52 us (6%)
  between operations  2.9 us (2%)
    ppermute x4, waiting for transfers between devices, shifted(): return lambda x: lax.ppermute(x, 'chan', pairs)  74.4 us
    ppermute x4, starting transfers between devices, shifted(): return lambda x: lax.ppermute(x, 'chan', pairs)  18.6 us
    dot_general x2, matrix products, lag_terms(): jnp.einsum('ctf,kjf->tkcj', factors, partner, preferred_element_type=jnp....  11.3 us
    all_to_all x2, starting transfers between devices, pass_over_win(): return lax.all_to_all(sent, 'win', split_axis=0, concat_axis=0, tiled=True)  9.45 us
    dot_general x1, matrix products, whiten(): spec = jnp.dot(shaped, table, preferred_element_type=jnp.float32)  4.93 us
    all_to_all x2, waiting for transfers between devices, pass_over_win(): return lax.all_to_all(sent, 'win', split_axis=0, concat_axis=0, tiled=True)  4.62 us
    dynamic_slice x4, local copies, waits for them, and re-layouts, split_for_win(): own = lax.dynamic_index_in_dim(pieces, me, 0, keepdims=False)  3.47 us
    reduce_sum x2, other arithmetic, sum_over_win(): return own + jnp.sum(arrived.astype(jnp.float32) * weights, axis=0)  3.13 us
  transfers between devices with their start and end apart: 6, of which 4 were waited for; matrix products, arithmetic and copies ran while one was open for 8% of the time, Pallas kernels for 0%

profile of v7, /device:TPU:320, one launch (start us, length us, event | category | flops | bytes accessed | tf_op | source)
XLA Modules:
  0.0 150.5 jit_solution(155581189411607157)
XLA Ops:
  0.9 1.3 convert_reduce_fusion.1
  2.3 4.9 %fusion.19 = f32[128,2048]{1,0:T(8,128)S(1)} fusion(bf16[2048,2048]{1,0:T(8,128)(2,1)} %constant.91.clone, f32[2048]{0:T(1024)S(1)} %multiply_subtract_fusion, f32[128]{0:T(128)S(1)} %broadcast_multiply_fusion, bf16[128,4096]{1,0:T(8,128)(2,1)} %param.46, s32[]{:T(128)S(6)} %select_n.64), kind=kOutput, calls=%fused_computation.36 | convolution fusion | flops 1074790400 | bytes 9970180 | tf_op jit(solution)/shard_map/dot_general | solution.py:57
  7.2 2.1 %fusion.11 = f32[128,1024]{1,0:T(8,128)S(1)} fusion(f32[1024]{0:T(1024)S(1)} %convert_reduce_fusion, f32[128,2048]{1,0:T(8,128)S(1)} %fusion.19), kind=kOutput, calls=%fused_computation.22 | convolution fusion | flops 1616379904 | bytes 1576960 | tf_op jit(solution)/shard_map/dot_general | solution.py:61
  9.3 1.0 fusion.14
  10.3 1.9 %collective-permute-start.42 = (bf16[128,2048]{1,0:T(8,128)(2,1)}, bf16[128,2048]{1,0:T(8,128)(2,1)S(1)}, u32[]{:S(2)}, u32[]{:S(2)}) collective-permute-start(bf16[128,2048]{1,0:T(8,128)(2,1)} %fusion.14), channel_id=1, source_target_pairs={{60,0},{64,4},{68,8},{72,12},{76,16},{80,20},{84,24},{88,28},{92,3... | collective-permute-start | bytes 1572872 | tf_op jit(solution)/shard_map/ppermute | solution.py:112
  12.2 1.1 slice_convert_fusion.1
  13.6 0.8 sort.15
  15.8 28.9 %conditional.5 = (bf16[1,128,2048]{2,1,0:T(8,128)(2,1)}) conditional(s32[]{:T(128)} %bitcast.30, bf16[128,2048]{1,0:T(8,128)(2,1)} %fusion.14, bf16[128,2048]{1,0:T(8,128)(2,1)} %fusion.14, bf16[128,2048]{1,0:T(8,128)(2,1)} %fusion.14, bf16[128,2048]{1,0:T(8,128)(2,1)} %fusion.14, ...), branch_computations={%region_4.5_spmd, %region_5.6_spmd, %region_6.7_spmd, %region_7.8_... | conditional | bytes 2097200 | solution.py:121
  15.8 6.2 %collective-permute-start.3 = (bf16[128,2048]{1,0:T(8,128)(2,1)}, bf16[128,2048]{1,0:T(8,128)(2,1)}, u32[]{:S(2)}, u32[]{:S(2)}) collective-permute-start(bf16[128,2048]{1,0:T(8,128)(2,1)} %param.3), channel_id=1, source_target_pairs={{16,0},{20,4},{24,8},{28,12},{32,16},{36,20},{40,24},{44,28},{48,3... | collective-permute-start | bytes 1572872 | tf_op jit(solution)/shard_map/cond/branch_3_fun/ppermute | solution.py:112
  22.0 22.7 %collective-permute-done.3 = bf16[128,2048]{1,0:T(8,128)(2,1)} collective-permute-done((bf16[128,2048]{1,0:T(8,128)(2,1)}, bf16[128,2048]{1,0:T(8,128)(2,1)}, u32[]{:S(2)}, u32[]{:S(2)}) %collective-permute-start.3) | collective-permute-done | bytes 524320 | tf_op jit(solution)/shard_map/cond/branch_3_fun/ppermute | solution.py:112
  45.3 32.9 %conditional.6 = (bf16[1,128,2048]{2,1,0:T(8,128)(2,1)}) conditional(s32[]{:T(128)} %bitcast.31, bf16[128,2048]{1,0:T(8,128)(2,1)} %fusion.14, bf16[128,2048]{1,0:T(8,128)(2,1)} %fusion.14, bf16[128,2048]{1,0:T(8,128)(2,1)} %fusion.14, bf16[128,2048]{1,0:T(8,128)(2,1)} %fusion.14, ...), branch_computations={%region_18.19_spmd, %region_19.20_spmd, %region_20.21_spmd, %regio... | conditional | bytes 2097200 | solution.py:121
  45.3 5.9 %collective-permute-start.20 = (bf16[128,2048]{1,0:T(8,128)(2,1)}, bf16[128,2048]{1,0:T(8,128)(2,1)}, u32[]{:S(2)}, u32[]{:S(2)}) collective-permute-start(bf16[128,2048]{1,0:T(8,128)(2,1)} %param.20), channel_id=1, source_target_pairs={{28,0},{32,4},{36,8},{40,12},{44,16},{48,20},{52,24},{56,28},{60,3... | collective-permute-start | bytes 1572872 | tf_op jit(solution)/shard_map/cond/branch_6_fun/ppermute | solution.py:112
  51.2 26.9 %collective-permute-done.20 = bf16[128,2048]{1,0:T(8,128)(2,1)} collective-permute-done((bf16[128,2048]{1,0:T(8,128)(2,1)}, bf16[128,2048]{1,0:T(8,128)(2,1)}, u32[]{:S(2)}, u32[]{:S(2)}) %collective-permute-start.20) | collective-permute-done | bytes 524320 | tf_op jit(solution)/shard_map/cond/branch_6_fun/ppermute | solution.py:112
  79.2 2.7 %subtract_convert_fusion = (bf16[128,16,1024]{2,0,1:T(8,128)(2,1)S(1)}, bf16[128,16,1024]{2,0,1:T(8,128)(2,1)S(1)}) fusion(f32[16,1024]{1,0:T(8,128)S(1)} %get-tuple-element.299, f32[128,1024]{1,0:T(8,128)S(1)} %get-tuple-element.297, f32[16,1024]{1,0:T(8,128)S(1)} %get-tuple-element.298, f32[128,1024]{1,0:T(8,128)S(1)} %get-tuple-element.296), kind=kLoop, calls=%fused_computation.5 | loop fusion | flops 16777216 | bytes 9568256 | tf_op jit(solution)/shard_map/convert
  81.9 0.9 copy-done.3
  82.8 6.0 %fusion = f32[3,128,128,16]{2,1,3,0:T(8,128)S(1)} fusion(bf16[128,16,1024]{2,0,1:T(8,128)(2,1)S(1)} %get-tuple-element.295, bf16[128,16,1024]{2,0,1:T(8,128)(2,1)S(1)} %get-tuple-element.294, bf16[1,128,2048]{2,1,0:T(8,128)(2,1)} %get-tuple-element.332, bf16[1,128,2048]{2,1,0:T(8,128)(2,1)} %get-tuple-element.331, bf16[1,128,2048]{2,1,0:T(8,128)(2,1)} %bitcast.89), kind=kOutput, calls=%fused_computation.2 | convolution fusion | flops 3242721280 | bytes 13107200 | tf_op jit(solution)/shard_map/ctf,kjf->tkcj/dot_general | solution.py:75
  88.8 35.8 %conditional.8 = (bf16[128,2048]{1,0:T(8,128)(2,1)}, bf16[4,4,3,128,128]{4,3,2,1,0:T(8,128)(2,1)}) conditional(s32[]{:T(128)} %bitcast.38, (bf16[128,2048]{1,0:T(8,128)(2,1)}, f32[4,4,3,128,128]{3,4,1,0,2:T(8,128)S(1)}) %tuple.364, (bf16[128,2048]{1,0:T(8,128)(2,1)}, f32[4,4,3,128,128]{3,4,1,0,2:T(8,128)S(1)}) %tuple.365, ...), branch_computations={%region_32.33_spmd, %region_33.34_spmd, %region_34.35_spmd, %regio... | conditional | bytes 11534424
  89.1 1.7 %copy.68 = bf16[4,4,3,128,128]{4,3,2,1,0:T(8,128)(2,1)} copy(f32[4,4,3,128,128]{3,4,1,0,2:T(8,128)S(1)} %get-tuple-element.286) | data formatting | bytes 4718592 | tf_op jit(solution)/shard_map
  90.7 4.3 %all-to-all-start.11 = ((bf16[4,4,3,128,128]{4,3,2,1,0:T(8,128)(2,1)}), bf16[4,4,3,128,128]{4,3,2,1,0:T(8,128)(2,1)}, u32[]{:S(2)}, u32[]{:S(2)}) async-start(bf16[4,4,3,128,128]{4,3,2,1,0:T(8,128)(2,1)} %copy.68), calls=%async_computation.11 | async-start | bytes 3145728 | tf_op jit(solution)/shard_map/cond/branch_11_fun/all_to_all | solution.py:87
  95.1 4.7 %collective-permute-start.39 = (bf16[128,2048]{1,0:T(8,128)(2,1)}, bf16[128,2048]{1,0:T(8,128)(2,1)}, u32[]{:S(2)}, u32[]{:S(2)}) collective-permute-start(bf16[128,2048]{1,0:T(8,128)(2,1)} %get-tuple-element.166), channel_id=1, source_target_pairs={{48,0},{52,4},{56,8},{60,12},{64,16},{68,20},{72,24},{76,28},{80,3... | collective-permute-start | bytes 1572872 | tf_op jit(solution)/shard_map/cond/branch_11_fun/ppermute | solution.py:112
  99.8 24.8 %collective-permute-done.39 = bf16[128,2048]{1,0:T(8,128)(2,1)} collective-permute-done((bf16[128,2048]{1,0:T(8,128)(2,1)}, bf16[128,2048]{1,0:T(8,128)(2,1)}, u32[]{:S(2)}, u32[]{:S(2)}) %collective-permute-start.39) | collective-permute-done | bytes 524320 | tf_op jit(solution)/shard_map/cond/branch_11_fun/ppermute | solution.py:112
  124.6 5.4 %fusion.2 = f32[128,128,16]{1,0,2:T(8,128)S(1)} fusion(bf16[128,16,1024]{2,0,1:T(8,128)(2,1)} %copy-done.1, bf16[128,16,1024]{2,0,1:T(8,128)(2,1)} %copy-done, bf16[128,2048]{1,0:T(8,128)(2,1)} %get-tuple-element.177), kind=kOutput, calls=%fused_computation.8 | convolution fusion | flops 1090519040 | bytes 9961472 | tf_op jit(solution)/shard_map/ctf,kjf->tkcj/dot_general | solution.py:75
  130.0 1.0 copy-done.2
  130.9 0.9 convert_element_type.232
  131.8 5.1 %all-to-all-start.14 = ((bf16[4,4,1,128,128]{3,4,1,2,0:T(8,128)(2,1)}), bf16[4,4,1,128,128]{3,4,1,2,0:T(8,128)(2,1)}, u32[]{:S(2)}, u32[]{:S(2)}) async-start(bf16[4,4,1,128,128]{3,4,1,2,0:T(8,128)(2,1)} %convert_element_type.232), calls=%async_computation.14 | async-start | bytes 1048576 | tf_op jit(solution)/shard_map/all_to_all | solution.py:87
  136.9 1.0 constant_dynamic-slice_fusion.1
  137.9 1.4 copy.56
  139.3 1.9 %fusion.4 = f32[4,3,128,128]{3,2,1,0:T(8,128)S(1)} fusion(bf16[4,4,3,128,128]{4,3,2,1,0:T(8,128)(2,1)} %get-tuple-element.293, f32[4]{0:T(128)S(1)} %compare_convert_fusion), kind=kLoop, calls=%fused_computation.12 | loop fusion | flops 2162688 | bytes 2359312 | tf_op jit(solution)/shard_map/reduce_sum | solution.py:95
  141.4 1.0 constant_dynamic-slice_fusion
  142.5 4.6 %all-to-all-done.14 = bf16[4,4,1,128,128]{3,4,1,2,0:T(8,128)(2,1)} async-done(((bf16[4,4,1,128,128]{3,4,1,2,0:T(8,128)(2,1)}), bf16[4,4,1,128,128]{3,4,1,2,0:T(8,128)(2,1)}, u32[]{:S(2)}, u32[]{:S(2)}) %all-to-all-start.14) | async-done | bytes 524320 | tf_op jit(solution)/shard_map/all_to_all | solution.py:87
  147.1 1.2 bitcast_reduce_fusion
  149.4 1.1 copy.75
  (32 shorter events, 2.8 us)
Async XLA Ops:
  7.2 6.2 %copy-start.4 = (s32[4]{0:T(128)S(1)}, s32[4]{0:T(128)}, u32[]{:S(2)}) copy-start(s32[4]{0:T(128)} %param.47) | copy-start | bytes 52
  10.3 71.6 %collective-permute-start.42 = (bf16[128,2048]{1,0:T(8,128)(2,1)}, bf16[128,2048]{1,0:T(8,128)(2,1)S(1)}, u32[]{:S(2)}, u32[]{:S(2)}) collective-permute-start(bf16[128,2048]{1,0:T(8,128)(2,1)} %fusion.14), channel_id=1, source_target_pairs={{60,0},{64,4},{68,8},{72,12},{76,16},{80,20},{84,24},{88,28},{92,3... | collective-permute-start | bytes 1572872 | tf_op jit(solution)/shard_map/ppermute | solution.py:112
  15.8 28.9 %collective-permute-start.3 = (bf16[128,2048]{1,0:T(8,128)(2,1)}, bf16[128,2048]{1,0:T(8,128)(2,1)}, u32[]{:S(2)}, u32[]{:S(2)}) collective-permute-start(bf16[128,2048]{1,0:T(8,128)(2,1)} %param.3), channel_id=1, source_target_pairs={{16,0},{20,4},{24,8},{28,12},{32,16},{36,20},{40,24},{44,28},{48,3... | collective-permute-start | bytes 1572872 | tf_op jit(solution)/shard_map/cond/branch_3_fun/ppermute | solution.py:112
  45.3 32.8 %collective-permute-start.20 = (bf16[128,2048]{1,0:T(8,128)(2,1)}, bf16[128,2048]{1,0:T(8,128)(2,1)}, u32[]{:S(2)}, u32[]{:S(2)}) collective-permute-start(bf16[128,2048]{1,0:T(8,128)(2,1)} %param.20), channel_id=1, source_target_pairs={{28,0},{32,4},{36,8},{40,12},{44,16},{48,20},{52,24},{56,28},{60,3... | collective-permute-start | bytes 1572872 | tf_op jit(solution)/shard_map/cond/branch_6_fun/ppermute | solution.py:112
  81.9 6.9 %copy-start = (bf16[128,16,1024]{2,0,1:T(8,128)(2,1)}, bf16[128,16,1024]{2,0,1:T(8,128)(2,1)S(1)}, u32[]{:S(2)}) copy-start(bf16[128,16,1024]{2,0,1:T(8,128)(2,1)S(1)} %get-tuple-element.294) | copy-start | bytes 12582916
  81.9 6.9 %copy-start.1 = (bf16[128,16,1024]{2,0,1:T(8,128)(2,1)}, bf16[128,16,1024]{2,0,1:T(8,128)(2,1)S(1)}, u32[]{:S(2)}) copy-start(bf16[128,16,1024]{2,0,1:T(8,128)(2,1)S(1)} %get-tuple-element.295) | copy-start | bytes 12582916
  81.9 0.9 copy-start.3
  90.7 33.8 %all-to-all-start.11 = ((bf16[4,4,3,128,128]{4,3,2,1,0:T(8,128)(2,1)}), bf16[4,4,3,128,128]{4,3,2,1,0:T(8,128)(2,1)}, u32[]{:S(2)}, u32[]{:S(2)}) async-start(bf16[4,4,3,128,128]{4,3,2,1,0:T(8,128)(2,1)} %copy.68), calls=%async_computation.11 | async-start | bytes 3145728 | tf_op jit(solution)/shard_map/cond/branch_11_fun/all_to_all | solution.py:87
  95.1 29.5 %collective-permute-start.39 = (bf16[128,2048]{1,0:T(8,128)(2,1)}, bf16[128,2048]{1,0:T(8,128)(2,1)}, u32[]{:S(2)}, u32[]{:S(2)}) collective-permute-start(bf16[128,2048]{1,0:T(8,128)(2,1)} %get-tuple-element.166), channel_id=1, source_target_pairs={{48,0},{52,4},{56,8},{60,12},{64,16},{68,20},{72,24},{76,28},{80,3... | collective-permute-start | bytes 1572872 | tf_op jit(solution)/shard_map/cond/branch_11_fun/ppermute | solution.py:112
  129.9 1.0 copy-start.2
  131.8 15.3 %all-to-all-start.14 = ((bf16[4,4,1,128,128]{3,4,1,2,0:T(8,128)(2,1)}), bf16[4,4,1,128,128]{3,4,1,2,0:T(8,128)(2,1)}, u32[]{:S(2)}, u32[]{:S(2)}) async-start(bf16[4,4,1,128,128]{3,4,1,2,0:T(8,128)(2,1)} %convert_element_type.232), calls=%async_computation.14 | async-start | bytes 1048576 | tf_op jit(solution)/shard_map/all_to_all | solution.py:87

commit v8 on v6

--- a/solution.py
+++ b/solution.py
@@ -119,8 +119,10 @@
     moves = [shifted(by) for by in range(1, far)]
     cos_w, sin_w = phase_tables(groups)
     first, second = lag_factors(own_re, own_im, cos_w, sin_w)
-    order = jnp.sort(offsets)
-    rank = jnp.sum(offsets[None, :] < offsets[:, None], axis=1)
+    hops = jnp.minimum(offsets, OFFCAP - offsets)
+    key = jnp.where(offsets == far, -1, hops * OFFCAP + offsets)
+    order = jnp.sort(key)[1:] % OFFCAP
+    rank = jnp.sum(key[None, :] < key[:, None], axis=1)
     nearer = [lax.switch(order[k] - 1, moves, spectra) for k in range(K - 2)]
     early = jnp.stack([farthest] + nearer, axis=0)
     early_own, early_sent = split_for_win(lag_terms(first, second, early))
@@ -134,7 +136,7 @@
     last_own, last_sent = split_for_win(lag_terms(first, second, last[None]))
     early_sum = sum_over_win(early_own, early_arrived)
     last_sum = sum_over_win(last_own, pass_over_win(last_sent))
-    by_rank = jnp.concatenate([early_sum[:, 1:], last_sum, early_sum[:, :1]], axis=1)
+    by_rank = jnp.concatenate([early_sum, last_sum], axis=1)
     return jnp.take(by_rank, rank, axis=1)
 
 

time: 150 us -> 129 us (0.86)
  waiting for transfers between devices: 89.3 us -> 72.8 us
  starting transfers between devices: 20.9 us -> 19.3 us
    ppermute x4, waiting for transfers between devices: 82.6 us -> 65.3 us  [shifted(): return lambda x: lax.ppermute(x, 'chan', pairs)]
    ppermute x4, starting transfers between devices: 12.4 us -> 10.2 us  [shifted(): return lambda x: lax.ppermute(x, 'chan', pairs)]
  transfers between devices with their start and end apart: 6 -> 6, of which waited for: 5 -> 4; matrix products, arithmetic and copies ran while one was open for 5% -> 3% of each run, Pallas kernels for 0% -> 0%
where the time goes in v8:
time: 129 us; the launch traced here: 128 us
  waiting for transfers between devices  72.8 us (56%)
  starting transfers between devices  19.3 us (15%)
  matrix products  17.4 us (13%)
  other arithmetic  8.67 us (7%)
  local copies, waits for them, and re-layouts  7.51 us (6%)
  between operations  2.77 us (2%)
    ppermute x4, waiting for transfers between devices, shifted(): return lambda x: lax.ppermute(x, 'chan', pairs)  65.3 us
    ppermute x4, starting transfers between devices, shifted(): return lambda x: lax.ppermute(x, 'chan', pairs)  10.2 us
    all_to_all x2, starting transfers between devices, pass_over_win(): return lax.all_to_all(sent, 'win', split_axis=0, concat_axis=0, tiled=True)  9.1 us
    all_to_all x2, waiting for transfers between devices, pass_over_win(): return lax.all_to_all(sent, 'win', split_axis=0, concat_axis=0, tiled=True)  7.48 us
    dot_general x2, matrix products, lag_terms(): jnp.einsum('ctf,kjf->tkcj', first, partner[:, 0], preferred_element_type=...  5.92 us
    dot_general x1, matrix products, whiten(): spec = jnp.dot(shaped, table, preferred_element_type=jnp.float32)  4.93 us
    dot_general x2, matrix products, lag_terms(): jnp.einsum('ctf,kjf->tkcj', second, partner[:, 1], preferred_element_type...  4.42 us
    dynamic_slice x4, local copies, waits for them, and re-layouts, split_for_win(): own = lax.dynamic_index_in_dim(pieces, me, 0, keepdims=False)  3.38 us
  transfers between devices with their start and end apart: 6, of which 4 were waited for; matrix products, arithmetic and copies ran while one was open for 3% of the time, Pallas kernels for 0%

profile of v8, /device:TPU:248, one launch (start us, length us, event | category | flops | bytes accessed | tf_op | source)
XLA Modules:
  0.0 128.5 jit_solution(558820019045183775)
XLA Ops:
  0.9 1.3 %convert_reduce_fusion.1 = f32[128]{0:T(128)S(1)} fusion(bf16[128,4096]{1,0:T(8,128)(2,1)} %param.46, s32[]{:T(128)S(6)} %select_n.75), kind=kLoop, calls=%fused_computation.37 | loop fusion | flops 524160 | bytes 524804 | tf_op jit(solution)/shard_map/reduce_sum | solution.py:54
  2.3 4.9 %fusion.39 = f32[128,2048]{1,0:T(8,128)S(1)} fusion(bf16[2048,2048]{1,0:T(8,128)(2,1)} %constant.109.clone, f32[2048]{0:T(1024)S(1)} %multiply_subtract_fusion, f32[128]{0:T(128)S(1)} %broadcast_multiply_fusion, bf16[128,4096]{1,0:T(8,128)(2,1)} %param.46, s32[]{:T(128)S(6)} %select_n.75), kind=kOutput, calls=%fused_computation.54 | convolution fusion | flops 1074790400 | bytes 9970180 | tf_op jit(solution)/shard_map/dot_general | solution.py:57
  7.2 2.1 %fusion.56 = (f32[128,1024]{1,0:T(8,128)S(1)}, bf16[128,1024]{1,0:T(8,128)(2,1)S(1)}, f32[128,1024]{1,0:T(8,128)S(1)}, bf16[128,1024]{1,0:T(8,128)(2,1)S(1)}) fusion(f32[128,2048]{1,0:T(8,128)S(1)} %fusion.39, f32[1024]{0:T(1024)S(1)} %convert_reduce_fusion), kind=kOutput, calls=%fused_computation.96 | convolution fusion | flops 1617166336 | bytes 3674112 | tf_op jit(solution)/shard_map/dot_general | solution.py:61
  9.4 0.9 pad_maximum_fusion.2
  10.3 1.9 %collective-permute-start.42 = (bf16[2,128,1024]{2,1,0:T(8,128)(2,1)}, bf16[2,128,1024]{2,1,0:T(8,128)(2,1)S(1)}, u32[]{:S(2)}, u32[]{:S(2)}) collective-permute-start(bf16[2,128,1024]{2,1,0:T(8,128)(2,1)} %pad_maximum_fusion.2), channel_id=1, source_target_pairs={{60,0},{64,4},{68,8},{72,12},{76,16},{80,20},{84,24},{88,28},{92,3... | collective-permute-start | bytes 1572872 | tf_op jit(solution)/shard_map/ppermute | solution.py:115
  12.5 0.8 sort.15
  13.3 0.6 fusion.58
  14.6 20.0 %conditional.5 = (bf16[1,2,128,1024]{3,2,1,0:T(8,128)(2,1)}) conditional(s32[]{:T(128)} %bitcast.32, bf16[2,128,1024]{2,1,0:T(8,128)(2,1)} %pad_maximum_fusion.2, bf16[2,128,1024]{2,1,0:T(8,128)(2,1)} %pad_maximum_fusion.2, bf16[2,128,1024]{2,1,0:T(8,128)(2,1)} %pad_maximum_fusion.2, ...), branch_computations={%region_4.5_spmd, %region_5.6_spmd, %region_6.7_spmd, %region_7.8_... | conditional | bytes 2097200 | solution.py:126
  14.6 3.3 %collective-permute-start.1 = (bf16[2,128,1024]{2,1,0:T(8,128)(2,1)}, bf16[2,128,1024]{2,1,0:T(8,128)(2,1)}, u32[]{:S(2)}, u32[]{:S(2)}) collective-permute-start(bf16[2,128,1024]{2,1,0:T(8,128)(2,1)} %param.1), channel_id=1, source_target_pairs={{8,0},{12,4},{16,8},{20,12},{24,16},{28,20},{32,24},{36,28},{40,32... | collective-permute-start | bytes 1572872 | tf_op jit(solution)/shard_map/cond/branch_1_fun/ppermute | solution.py:115
  17.9 16.7 %collective-permute-done.1 = bf16[2,128,1024]{2,1,0:T(8,128)(2,1)} collective-permute-done((bf16[2,128,1024]{2,1,0:T(8,128)(2,1)}, bf16[2,128,1024]{2,1,0:T(8,128)(2,1)}, u32[]{:S(2)}, u32[]{:S(2)}) %collective-permute-start.1) | collective-permute-done | bytes 524320 | tf_op jit(solution)/shard_map/cond/branch_1_fun/ppermute | solution.py:115
  35.2 21.3 %conditional.6 = (bf16[1,2,128,1024]{3,2,1,0:T(8,128)(2,1)}) conditional(s32[]{:T(128)} %bitcast.33, bf16[2,128,1024]{2,1,0:T(8,128)(2,1)} %pad_maximum_fusion.2, bf16[2,128,1024]{2,1,0:T(8,128)(2,1)} %pad_maximum_fusion.2, bf16[2,128,1024]{2,1,0:T(8,128)(2,1)} %pad_maximum_fusion.2, ...), branch_computations={%region_18.19_spmd, %region_19.20_spmd, %region_20.21_spmd, %regio... | conditional | bytes 2097200 | solution.py:126
  35.2 1.9 %collective-permute-start.16 = (bf16[2,128,1024]{2,1,0:T(8,128)(2,1)}, bf16[2,128,1024]{2,1,0:T(8,128)(2,1)}, u32[]{:S(2)}, u32[]{:S(2)}) collective-permute-start(bf16[2,128,1024]{2,1,0:T(8,128)(2,1)} %param.16), channel_id=1, source_target_pairs={{12,0},{16,4},{20,8},{24,12},{28,16},{32,20},{36,24},{40,28},{44,3... | collective-permute-start | bytes 1572872 | tf_op jit(solution)/shard_map/cond/branch_2_fun/ppermute | solution.py:115
  37.2 19.4 %collective-permute-done.16 = bf16[2,128,1024]{2,1,0:T(8,128)(2,1)} collective-permute-done((bf16[2,128,1024]{2,1,0:T(8,128)(2,1)}, bf16[2,128,1024]{2,1,0:T(8,128)(2,1)}, u32[]{:S(2)}, u32[]{:S(2)}) %collective-permute-start.16) | collective-permute-done | bytes 524320 | tf_op jit(solution)/shard_map/cond/branch_2_fun/ppermute | solution.py:115
  57.2 0.3 cosine_multiply_fusion
  57.5 1.4 %pad_maximum_fusion = bf16[3,2,128,1024]{3,2,1,0:T(8,128)(2,1)S(1)} fusion(bf16[1,2,128,1024]{3,2,1,0:T(8,128)(2,1)} %get-tuple-element.334, bf16[1,2,128,1024]{3,2,1,0:T(8,128)(2,1)} %get-tuple-element.333, bf16[1,2,128,1024]{3,2,1,0:T(8,128)(2,1)S(1)} %bitcast.111), kind=kLoop, calls=%fused_computation.34 | loop fusion | flops 1572864 | bytes 3145728 | tf_op jit(solution)/shard_map/stack | solution.py:127
  58.9 1.9 %fusion.4 = f32[3,128,128,16]{2,1,3,0:T(8,128)S(1)} fusion(f32[16,1024]{1,0:T(8,128)S(1)} %get-tuple-element.301, f32[128,1024]{1,0:T(8,128)S(1)} %get-tuple-element.298, f32[16,1024]{1,0:T(8,128)S(1)} %get-tuple-element.300, f32[128,1024]{1,0:T(8,128)S(1)} %get-tuple-element.294, bf16[3,2,128,1024]{3,2,1,0:T(8,128)(2,1)S(1)} %pad_maximum_fusion), kind=kOutput, calls=%fused_computation.9 | convolution fusion | flops 1619001344 | bytes 5111808 | tf_op jit(solution)/shard_map/ctf,kjf->tkcj/dot_general | solution.py:77
  60.8 3.0 %fusion.28 = f32[3,128,128,16]{2,1,3,0:T(8,128)S(1)} fusion(f32[3,128,128,16]{2,1,3,0:T(8,128)S(1)} %fusion.4, f32[16,1024]{1,0:T(8,128)S(1)} %get-tuple-element.301, f32[128,1024]{1,0:T(8,128)} %copy-done.4, f32[16,1024]{1,0:T(8,128)S(1)} %get-tuple-element.300, f32[128,1024]{1,0:T(8,128)} %copy-done.2, bf16[3,2,128,1024]{3,2,1,0:T(8,128)(2,1)S(1)} %pad_maximum_fusion), kind=kOutput, calls=%fused_computation.33 | convolution fusion | flops 1619787776 | bytes 8257536 | tf_op jit(solution)/shard_map/ctf,kjf->tkcj/dot_general | solution.py:75
  63.8 0.9 constant_dynamic-slice_fusion.1
  64.8 2.3 %copy.56 = f32[1,4,3,128,128]{4,3,2,1,0:T(8,128)} copy(f32[1,4,3,128,128]{3,4,1,0,2:T(8,128)} %constant_dynamic-slice_fusion.1) | data formatting | bytes 1572864 | tf_op jit(solution)/shard_map/jit(dynamic_index_in_dim)/dynamic_slice | solution.py:84
  67.1 38.3 %conditional.8 = (bf16[2,128,1024]{2,1,0:T(8,128)(2,1)}, bf16[4,4,3,128,128]{4,3,2,1,0:T(8,128)(2,1)}) conditional(s32[]{:T(128)} %bitcast.45, (bf16[2,128,1024]{2,1,0:T(8,128)(2,1)}, f32[4,4,3,128,128]{3,4,1,0,2:T(8,128)S(1)}) %tuple.366, (bf16[2,128,1024]{2,1,0:T(8,128)(2,1)}, ...), branch_computations={%region_32.33_spmd, %region_33.34_spmd, %region_34.35_spmd, %regio... | conditional | bytes 11534424
  67.1 1.7 %copy.64 = bf16[4,4,3,128,128]{4,3,2,1,0:T(8,128)(2,1)} copy(f32[4,4,3,128,128]{3,4,1,0,2:T(8,128)S(1)} %get-tuple-element.278) | data formatting | bytes 4718592 | tf_op jit(solution)/shard_map
  68.8 4.4 %all-to-all-start.7 = ((bf16[4,4,3,128,128]{4,3,2,1,0:T(8,128)(2,1)}), bf16[4,4,3,128,128]{4,3,2,1,0:T(8,128)(2,1)}, u32[]{:S(2)}, u32[]{:S(2)}) async-start(bf16[4,4,3,128,128]{4,3,2,1,0:T(8,128)(2,1)} %copy.64), calls=%async_computation.7 | async-start | bytes 3145728 | tf_op jit(solution)/shard_map/cond/branch_7_fun/all_to_all | solution.py:89
  73.1 3.1 %collective-permute-start.35 = (bf16[2,128,1024]{2,1,0:T(8,128)(2,1)}, bf16[2,128,1024]{2,1,0:T(8,128)(2,1)}, u32[]{:S(2)}, u32[]{:S(2)}) collective-permute-start(bf16[2,128,1024]{2,1,0:T(8,128)(2,1)} %get-tuple-element.158), channel_id=1, source_target_pairs={{32,0},{36,4},{40,8},{44,12},{48,16},{52,20},{56,24},{60,28},{64,3... | collective-permute-start | bytes 1572872 | tf_op jit(solution)/shard_map/cond/branch_7_fun/ppermute | solution.py:115
  76.2 29.2 %collective-permute-done.35 = bf16[2,128,1024]{2,1,0:T(8,128)(2,1)} collective-permute-done((bf16[2,128,1024]{2,1,0:T(8,128)(2,1)}, bf16[2,128,1024]{2,1,0:T(8,128)(2,1)}, u32[]{:S(2)}, u32[]{:S(2)}) %collective-permute-start.35) | collective-permute-done | bytes 524320 | tf_op jit(solution)/shard_map/cond/branch_7_fun/ppermute | solution.py:115
  105.4 2.9 %fusion = f32[128,128,16]{1,0,2:T(8,128)S(1)} fusion(f32[16,1024]{1,0:T(8,128)S(1)} %get-tuple-element.301, f32[128,1024]{1,0:T(8,128)} %copy-done.4, f32[16,1024]{1,0:T(8,128)S(1)} %get-tuple-element.300, f32[128,1024]{1,0:T(8,128)} %copy-done.2, bf16[1,2,128,1024]{3,2,1,0:T(8,128)(2,1)} %bitcast.47), kind=kOutput, calls=%fused_computation.5 | convolution fusion | flops 545259520 | bytes 2490368 | tf_op jit(solution)/shard_map/ctf,kjf->tkcj/dot_general | solution.py:75
  108.3 2.5 %fusion.31 = f32[128,128,16]{1,0,2:T(8,128)S(1)} fusion(f32[128,128,16]{1,0,2:T(8,128)S(1)} %fusion, f32[16,1024]{1,0:T(8,128)S(1)} %get-tuple-element.301, f32[128,1024]{1,0:T(8,128)S(1)} %copy-done.5, f32[16,1024]{1,0:T(8,128)S(1)} %get-tuple-element.300, f32[128,1024]{1,0:T(8,128)S(1)} %copy-done.3, bf16[1,2,128,1024]{3,2,1,0:T(8,128)(2,1)} %bitcast.47), kind=kOutput, calls=%fused_computation.35 | convolution fusion | flops 545521664 | bytes 3538944 | tf_op jit(solution)/shard_map/ctf,kjf->tkcj/dot_general | solution.py:77
  110.9 0.9 convert_element_type.157
  111.7 4.7 %all-to-all-start.14 = ((bf16[4,4,1,128,128]{3,4,1,2,0:T(8,128)(2,1)}), bf16[4,4,1,128,128]{3,4,1,2,0:T(8,128)(2,1)S(1)}, u32[]{:S(2)}, u32[]{:S(2)}) async-start(bf16[4,4,1,128,128]{3,4,1,2,0:T(8,128)(2,1)} %convert_element_type.157), calls=%async_computation.14 | async-start | bytes 1048576 | tf_op jit(solution)/shard_map/all_to_all | solution.py:89
  116.6 1.9 %fusion.25 = f32[4,3,128,128]{3,2,1,0:T(8,128)S(1)} fusion(bf16[4,4,3,128,128]{4,3,2,1,0:T(8,128)(2,1)} %get-tuple-element.293, f32[4]{0:T(128)S(1)} %compare_convert_fusion), kind=kLoop, calls=%fused_computation.30 | loop fusion | flops 2162688 | bytes 2359312 | tf_op jit(solution)/shard_map/reduce_sum | solution.py:97
  118.7 7.5 %all-to-all-done.14 = bf16[4,4,1,128,128]{3,4,1,2,0:T(8,128)(2,1)S(1)} async-done(((bf16[4,4,1,128,128]{3,4,1,2,0:T(8,128)(2,1)}), bf16[4,4,1,128,128]{3,4,1,2,0:T(8,128)(2,1)S(1)}, u32[]{:S(2)}, u32[]{:S(2)}) %all-to-all-start.14) | async-done | bytes 524320 | tf_op jit(solution)/shard_map/all_to_all | solution.py:89
  126.6 0.6 gather_fusion
  127.4 1.1 copy.75
  (35 shorter events, 1.5 us)
Async XLA Ops:
  7.2 5.0 %copy-start.1 = (s32[4]{0:T(128)S(1)}, s32[4]{0:T(128)}, u32[]{:S(2)}) copy-start(s32[4]{0:T(128)} %param.47) | copy-start | bytes 52
  9.4 49.5 %copy-start.2 = (f32[128,1024]{1,0:T(8,128)}, f32[128,1024]{1,0:T(8,128)S(1)}, u32[]{:S(2)}) copy-start(f32[128,1024]{1,0:T(8,128)S(1)} %get-tuple-element.294) | copy-start | bytes 1572868
  9.4 49.5 %copy-start.4 = (f32[128,1024]{1,0:T(8,128)}, f32[128,1024]{1,0:T(8,128)S(1)}, u32[]{:S(2)}) copy-start(f32[128,1024]{1,0:T(8,128)S(1)} %get-tuple-element.298) | copy-start | bytes 1572868
  10.3 47.2 %collective-permute-start.42 = (bf16[2,128,1024]{2,1,0:T(8,128)(2,1)}, bf16[2,128,1024]{2,1,0:T(8,128)(2,1)S(1)}, u32[]{:S(2)}, u32[]{:S(2)}) collective-permute-start(bf16[2,128,1024]{2,1,0:T(8,128)(2,1)} %pad_maximum_fusion.2), channel_id=1, source_target_pairs={{60,0},{64,4},{68,8},{72,12},{76,16},{80,20},{84,24},{88,28},{92,3... | collective-permute-start | bytes 1572872 | tf_op jit(solution)/shard_map/ppermute | solution.py:115
  14.6 20.0 %collective-permute-start.1 = (bf16[2,128,1024]{2,1,0:T(8,128)(2,1)}, bf16[2,128,1024]{2,1,0:T(8,128)(2,1)}, u32[]{:S(2)}, u32[]{:S(2)}) collective-permute-start(bf16[2,128,1024]{2,1,0:T(8,128)(2,1)} %param.1), channel_id=1, source_target_pairs={{8,0},{12,4},{16,8},{20,12},{24,16},{28,20},{32,24},{36,28},{40,32... | collective-permute-start | bytes 1572872 | tf_op jit(solution)/shard_map/cond/branch_1_fun/ppermute | solution.py:115
  35.2 21.3 %collective-permute-start.16 = (bf16[2,128,1024]{2,1,0:T(8,128)(2,1)}, bf16[2,128,1024]{2,1,0:T(8,128)(2,1)}, u32[]{:S(2)}, u32[]{:S(2)}) collective-permute-start(bf16[2,128,1024]{2,1,0:T(8,128)(2,1)} %param.16), channel_id=1, source_target_pairs={{12,0},{16,4},{20,8},{24,12},{28,16},{32,20},{36,24},{40,28},{44,3... | collective-permute-start | bytes 1572872 | tf_op jit(solution)/shard_map/cond/branch_2_fun/ppermute | solution.py:115
  68.8 36.6 %all-to-all-start.7 = ((bf16[4,4,3,128,128]{4,3,2,1,0:T(8,128)(2,1)}), bf16[4,4,3,128,128]{4,3,2,1,0:T(8,128)(2,1)}, u32[]{:S(2)}, u32[]{:S(2)}) async-start(bf16[4,4,3,128,128]{4,3,2,1,0:T(8,128)(2,1)} %copy.64), calls=%async_computation.7 | async-start | bytes 3145728 | tf_op jit(solution)/shard_map/cond/branch_7_fun/all_to_all | solution.py:89
  73.1 32.3 %collective-permute-start.35 = (bf16[2,128,1024]{2,1,0:T(8,128)(2,1)}, bf16[2,128,1024]{2,1,0:T(8,128)(2,1)}, u32[]{:S(2)}, u32[]{:S(2)}) collective-permute-start(bf16[2,128,1024]{2,1,0:T(8,128)(2,1)} %get-tuple-element.158), channel_id=1, source_target_pairs={{32,0},{36,4},{40,8},{44,12},{48,16},{52,20},{56,24},{60,28},{64,3... | collective-permute-start | bytes 1572872 | tf_op jit(solution)/shard_map/cond/branch_7_fun/ppermute | solution.py:115
  105.4 2.9 %copy-start.3 = (f32[128,1024]{1,0:T(8,128)S(1)}, f32[128,1024]{1,0:T(8,128)}, u32[]{:S(2)}) copy-start(f32[128,1024]{1,0:T(8,128)} %copy-done.2) | copy-start | bytes 1572868
  105.4 2.9 %copy-start.5 = (f32[128,1024]{1,0:T(8,128)S(1)}, f32[128,1024]{1,0:T(8,128)}, u32[]{:S(2)}) copy-start(f32[128,1024]{1,0:T(8,128)} %copy-done.4) | copy-start | bytes 1572868
  110.8 7.7 %copy-start = (f32[1,4,3,128,128]{4,3,2,1,0:T(8,128)S(1)}, f32[1,4,3,128,128]{4,3,2,1,0:T(8,128)}, u32[]{:S(2)}) copy-start(f32[1,4,3,128,128]{4,3,2,1,0:T(8,128)} %copy.56) | copy-start | bytes 2359300
  111.7 14.4 %all-to-all-start.14 = ((bf16[4,4,1,128,128]{3,4,1,2,0:T(8,128)(2,1)}), bf16[4,4,1,128,128]{3,4,1,2,0:T(8,128)(2,1)S(1)}, u32[]{:S(2)}, u32[]{:S(2)}) async-start(bf16[4,4,1,128,128]{3,4,1,2,0:T(8,128)(2,1)} %convert_element_type.157), calls=%async_computation.14 | async-start | bytes 1048576 | tf_op jit(solution)/shard_map/all_to_all | solution.py:89

commit v9 on v8

--- a/solution.py
+++ b/solution.py
@@ -79,22 +79,15 @@
 
 def split_for_win(corr):
     groups = lax.axis_size("win")
-    me = lax.axis_index("win")
-    pieces = corr.reshape(groups, -1, *corr.shape[1:])
-    own = lax.dynamic_index_in_dim(pieces, me, 0, keepdims=False)
-    return own, pieces.astype(jnp.bfloat16)
+    return corr.reshape(groups, -1, *corr.shape[1:]).astype(jnp.bfloat16)
 
 
 def pass_over_win(sent):
     return lax.all_to_all(sent, "win", split_axis=0, concat_axis=0, tiled=True)
 
 
-def sum_over_win(own, arrived):
-    groups = lax.axis_size("win")
-    me = lax.axis_index("win")
-    others = (jnp.arange(groups) != me).astype(jnp.float32)
-    weights = others.reshape(groups, *([1] * (arrived.ndim - 1)))
-    return own + jnp.sum(arrived.astype(jnp.float32) * weights, axis=0)
+def sum_over_win(arrived):
+    return jnp.sum(arrived.astype(jnp.float32), axis=0)
 
 
 def in_blocks(array, dim, size):
@@ -125,7 +118,7 @@
     rank = jnp.sum(key[None, :] < key[:, None], axis=1)
     nearer = [lax.switch(order[k] - 1, moves, spectra) for k in range(K - 2)]
     early = jnp.stack([farthest] + nearer, axis=0)
-    early_own, early_sent = split_for_win(lag_terms(first, second, early))
+    early_sent = split_for_win(lag_terms(first, second, early))
 
     def with_early(move):
         return lambda x, sent: (move(x), pass_over_win(sent))
@@ -133,9 +126,9 @@
     last, early_arrived = lax.switch(
         order[K - 2] - 1, [with_early(move) for move in moves], spectra, early_sent
     )
-    last_own, last_sent = split_for_win(lag_terms(first, second, last[None]))
-    early_sum = sum_over_win(early_own, early_arrived)
-    last_sum = sum_over_win(last_own, pass_over_win(last_sent))
+    last_sent = split_for_win(lag_terms(first, second, last[None]))
+    early_sum = sum_over_win(early_arrived)
+    last_sum = sum_over_win(pass_over_win(last_sent))
     by_rank = jnp.concatenate([early_sum, last_sum], axis=1)
     return jnp.take(by_rank, rank, axis=1)
 

time: 129 us -> 158 us (1.22)
  the two profiles are of different devices: /device:TPU:248 before, /device:TPU:240 now
where the time goes in v9:
time: 158 us
  waiting for transfers between devices  88.4 us (56%)
  starting transfers between devices  26.1 us (17%)
  matrix products  19.6 us (12%)
  other arithmetic  12.4 us (8%)
  local copies, waits for them, and re-layouts  8.41 us (5%)
  between operations  2.83 us (2%)
    ppermute x4, waiting for transfers between devices, shifted(): return lambda x: lax.ppermute(x, 'chan', pairs)  66.8 us
    all_to_all x2, waiting for transfers between devices, pass_over_win(): return lax.all_to_all(sent, 'win', split_axis=0, concat_axis=0, tiled=True)  21.6 us
    ppermute x4, starting transfers between devices, shifted(): return lambda x: lax.ppermute(x, 'chan', pairs)  16.8 us
    all_to_all x2, starting transfers between devices, pass_over_win(): return lax.all_to_all(sent, 'win', split_axis=0, concat_axis=0, tiled=True)  9.35 us
    dot_general x2, matrix products, lag_terms(): jnp.einsum('ctf,kjf->tkcj', first, partner[:, 0], preferred_element_type=...  6.35 us
    another operation x3, local copies, waits for them, and re-layouts  5.97 us
    dot_general x2, matrix products, lag_terms(): jnp.einsum('ctf,kjf->tkcj', second, partner[:, 1], preferred_element_type...  5.2 us
    dot_general x1, matrix products, whiten(): spec = jnp.dot(shaped, table, preferred_element_type=jnp.float32)  4.94 us
  transfers between devices with their start and end apart: 6, of which 5 were waited for; matrix products, arithmetic and copies ran while one was open for 2% of the time, Pallas kernels for 0%

profile of v9, /device:TPU:240, one launch (start us, length us, event | category | flops | bytes accessed | tf_op | source)
XLA Modules:
  0.0 157.9 jit_solution(13152457274610154940)
XLA Ops:
  0.9 1.4 convert_reduce_fusion.15
  2.3 4.9 %fusion.42 = f32[128,2048]{1,0:T(8,128)S(1)} fusion(bf16[2048,2048]{1,0:T(8,128)(2,1)} %constant.111.clone, f32[2048]{0:T(1024)S(1)} %multiply_subtract_fusion, f32[128]{0:T(128)S(1)} %broadcast_multiply_fusion, bf16[128,4096]{1,0:T(8,128)(2,1)} %param.46, s32[]{:T(128)S(6)} %select_n.70), kind=kOutput, calls=%fused_computation.81 | convolution fusion | flops 1074790400 | bytes 9970180 | tf_op jit(solution)/shard_map/dot_general | solution.py:57
  7.3 3.1 %fusion.59 = (f32[128,1024]{1,0:T(8,128)}, bf16[128,1024]{1,0:T(8,128)(2,1)S(1)}, f32[128,1024]{1,0:T(8,128)}, bf16[128,1024]{1,0:T(8,128)(2,1)S(1)}) fusion(f32[128,2048]{1,0:T(8,128)S(1)} %fusion.42, f32[1024]{0:T(1024)S(1)} %convert_reduce_fusion.14), kind=kOutput, calls=%fused_computation.119 | convolution fusion | flops 1617166336 | bytes 3674112 | tf_op jit(solution)/shard_map/dot_general | solution.py:61
  10.4 0.9 pad_maximum_fusion.2
  11.2 1.9 %collective-permute-start.42 = (bf16[2,128,1024]{2,1,0:T(8,128)(2,1)}, bf16[2,128,1024]{2,1,0:T(8,128)(2,1)S(1)}, u32[]{:S(2)}, u32[]{:S(2)}) collective-permute-start(bf16[2,128,1024]{2,1,0:T(8,128)(2,1)} %pad_maximum_fusion.2), channel_id=1, source_target_pairs={{60,0},{64,4},{68,8},{72,12},{76,16},{80,20},{84,24},{88,28},{92,3... | collective-permute-start | bytes 1572872 | tf_op jit(solution)/shard_map/ppermute | solution.py:108
  13.2 0.7 sort.15
  14.0 0.6 fusion.61
  15.3 20.9 %conditional.3 = (bf16[1,2,128,1024]{3,2,1,0:T(8,128)(2,1)}) conditional(s32[]{:T(128)} %bitcast.47, bf16[2,128,1024]{2,1,0:T(8,128)(2,1)} %pad_maximum_fusion.2, bf16[2,128,1024]{2,1,0:T(8,128)(2,1)} %pad_maximum_fusion.2, bf16[2,128,1024]{2,1,0:T(8,128)(2,1)} %pad_maximum_fusion.2, ...), branch_computations={%region_4.5_spmd, %region_5.6_spmd, %region_6.7_spmd, %region_7.8_... | conditional | bytes 2097200 | solution.py:119
  15.3 3.5 %collective-permute-start.2 = (bf16[2,128,1024]{2,1,0:T(8,128)(2,1)}, bf16[2,128,1024]{2,1,0:T(8,128)(2,1)}, u32[]{:S(2)}, u32[]{:S(2)}) collective-permute-start(bf16[2,128,1024]{2,1,0:T(8,128)(2,1)} %param.2), channel_id=1, source_target_pairs={{12,0},{16,4},{20,8},{24,12},{28,16},{32,20},{36,24},{40,28},{44,3... | collective-permute-start | bytes 1572872 | tf_op jit(solution)/shard_map/cond/branch_2_fun/ppermute | solution.py:108
  18.8 17.4 %collective-permute-done.2 = bf16[2,128,1024]{2,1,0:T(8,128)(2,1)} collective-permute-done((bf16[2,128,1024]{2,1,0:T(8,128)(2,1)}, bf16[2,128,1024]{2,1,0:T(8,128)(2,1)}, u32[]{:S(2)}, u32[]{:S(2)}) %collective-permute-start.2) | collective-permute-done | bytes 524320 | tf_op jit(solution)/shard_map/cond/branch_2_fun/ppermute | solution.py:108
  36.8 39.1 %conditional.4 = (bf16[1,2,128,1024]{3,2,1,0:T(8,128)(2,1)}) conditional(s32[]{:T(128)} %bitcast.48, bf16[2,128,1024]{2,1,0:T(8,128)(2,1)} %pad_maximum_fusion.2, bf16[2,128,1024]{2,1,0:T(8,128)(2,1)} %pad_maximum_fusion.2, bf16[2,128,1024]{2,1,0:T(8,128)(2,1)} %pad_maximum_fusion.2, ...), branch_computations={%region_18.19_spmd, %region_19.20_spmd, %region_20.21_spmd, %regio... | conditional | bytes 2097200 | solution.py:119
  36.8 3.5 %collective-permute-start.19 = (bf16[2,128,1024]{2,1,0:T(8,128)(2,1)}, bf16[2,128,1024]{2,1,0:T(8,128)(2,1)}, u32[]{:S(2)}, u32[]{:S(2)}) collective-permute-start(bf16[2,128,1024]{2,1,0:T(8,128)(2,1)} %param.19), channel_id=1, source_target_pairs={{24,0},{28,4},{32,8},{36,12},{40,16},{44,20},{48,24},{52,28},{56,3... | collective-permute-start | bytes 1572872 | tf_op jit(solution)/shard_map/cond/branch_5_fun/ppermute | solution.py:108
  40.3 35.6 %collective-permute-done.19 = bf16[2,128,1024]{2,1,0:T(8,128)(2,1)} collective-permute-done((bf16[2,128,1024]{2,1,0:T(8,128)(2,1)}, bf16[2,128,1024]{2,1,0:T(8,128)(2,1)}, u32[]{:S(2)}, u32[]{:S(2)}) %collective-permute-start.19) | collective-permute-done | bytes 524320 | tf_op jit(solution)/shard_map/cond/branch_5_fun/ppermute | solution.py:108
  77.2 1.4 pad_maximum_fusion
  78.6 1.8 %fusion.30 = f32[16,3,128,128]{2,3,0,1:T(8,128)S(1)} fusion(f32[16,1024]{1,0:T(8,128)S(1)} %get-tuple-element.416, f32[128,1024]{1,0:T(8,128)S(1)} %copy-done.3, f32[16,1024]{1,0:T(8,128)S(1)} %get-tuple-element.415, f32[128,1024]{1,0:T(8,128)S(1)} %copy-done.1, bf16[3,2,128,1024]{3,2,1,0:T(8,128)(2,1)S(1)} %pad_maximum_fusion), kind=kOutput, calls=%fused_computation.60 | convolution fusion | flops 1619001344 | bytes 5111808 | tf_op jit(solution)/shard_map/ctf,kjf->tkcj/dot_general | solution.py:77
  80.5 3.5 %fusion.27 = f32[16,3,128,128]{2,3,0,1:T(8,128)} fusion(f32[16,1024]{1,0:T(8,128)S(1)} %get-tuple-element.416, f32[128,1024]{1,0:T(8,128)S(1)} %copy-done.3, f32[16,1024]{1,0:T(8,128)S(1)} %get-tuple-element.415, f32[128,1024]{1,0:T(8,128)S(1)} %copy-done.1, bf16[3,2,128,1024]{3,2,1,0:T(8,128)(2,1)S(1)} %pad_maximum_fusion), kind=kOutput, calls=%fused_computation.59 | convolution fusion | flops 1619001344 | bytes 5111808 | tf_op jit(solution)/shard_map/ctf,kjf->tkcj/dot_general | solution.py:75
  84.0 49.1 %conditional.5 = (bf16[2,128,1024]{2,1,0:T(8,128)(2,1)}, f32[4,3,128,128]{3,2,1,0:T(8,128)}) conditional(s32[]{:T(128)} %bitcast.42, (bf16[2,128,1024]{2,1,0:T(8,128)(2,1)}, f32[16,3,128,128]{2,3,0,1:T(8,128)}, f32[16,3,128,128]{2,3,0,1:T(8,128)S(1)}) %tuple.187, (bf16[2,128,1024]{2,1,0:T(8,128)(2,1)}, ...), branch_computations={%region_32.34_spmd, %region_34.36_spmd, %region_36.38_spmd, %regio... | conditional | flops 2949120 | bytes 29622360 | solution.py:126
  84.0 3.6 %copy.108 = f32[16,3,128,128]{3,2,1,0:T(8,128)} copy(f32[16,3,128,128]{2,3,0,1:T(8,128)} %get-tuple-element.389) | data formatting | bytes 6291456 | tf_op jit(solution)/shard_map
  87.5 2.4 %copy.109 = f32[16,3,128,128]{3,2,1,0:T(8,128)} copy(f32[16,3,128,128]{2,3,0,1:T(8,128)S(1)} %get-tuple-element.390) | data formatting | bytes 6291456 | tf_op jit(solution)/shard_map
  89.9 4.6 %add_convert_fusion.7 = bf16[16,3,128,128]{3,2,1,0:T(8,128)(2,1)} fusion(f32[16,3,128,128]{3,2,1,0:T(8,128)} %copy.108, f32[16,3,128,128]{3,2,1,0:T(8,128)} %copy.109), kind=kLoop, calls=%fused_computation.16 | loop fusion | flops 1572864 | bytes 7864320 | tf_op jit(solution)/shard_map/convert_element_type | solution.py:82
  94.5 4.3 %all-to-all-start.7 = ((bf16[4,4,3,128,128]{4,3,2,1,0:T(8,128)(2,1)}), bf16[4,4,3,128,128]{4,3,2,1,0:T(8,128)(2,1)S(1)}, u32[]{:S(2)}, u32[]{:S(2)}) async-start(bf16[4,4,3,128,128]{4,3,2,1,0:T(8,128)(2,1)} %bitcast.35), calls=%async_computation.7 | async-start | bytes 3145728 | tf_op jit(solution)/shard_map/cond/branch_7_fun/all_to_all | solution.py:86
  98.8 7.9 %collective-permute-start.35 = (bf16[2,128,1024]{2,1,0:T(8,128)(2,1)}, bf16[2,128,1024]{2,1,0:T(8,128)(2,1)}, u32[]{:S(2)}, u32[]{:S(2)}) collective-permute-start(bf16[2,128,1024]{2,1,0:T(8,128)(2,1)} %get-tuple-element.214), channel_id=1, source_target_pairs={{32,0},{36,4},{40,8},{44,12},{48,16},{52,20},{56,24},{60,28},{64,3... | collective-permute-start | bytes 1572872 | tf_op jit(solution)/shard_map/cond/branch_7_fun/ppermute | solution.py:108
  106.7 11.4 %all-to-all-done.7 = bf16[4,4,3,128,128]{4,3,2,1,0:T(8,128)(2,1)S(1)} async-done(((bf16[4,4,3,128,128]{4,3,2,1,0:T(8,128)(2,1)}), bf16[4,4,3,128,128]{4,3,2,1,0:T(8,128)(2,1)S(1)}, u32[]{:S(2)}, u32[]{:S(2)}) %all-to-all-start.7) | async-done | bytes 1572896 | tf_op jit(solution)/shard_map/cond/branch_7_fun/all_to_all | solution.py:86
  118.1 1.1 convert_reduce_fusion.7
  119.2 13.8 %collective-permute-done.35 = bf16[2,128,1024]{2,1,0:T(8,128)(2,1)} collective-permute-done((bf16[2,128,1024]{2,1,0:T(8,128)(2,1)}, bf16[2,128,1024]{2,1,0:T(8,128)(2,1)}, u32[]{:S(2)}, u32[]{:S(2)}) %collective-permute-start.35) | collective-permute-done | bytes 524320 | tf_op jit(solution)/shard_map/cond/branch_7_fun/ppermute | solution.py:108
  133.0 2.9 %fusion = f32[128,128,16]{1,0,2:T(8,128)S(1)} fusion(f32[16,1024]{1,0:T(8,128)S(1)} %get-tuple-element.416, f32[128,1024]{1,0:T(8,128)} %get-tuple-element.413, f32[16,1024]{1,0:T(8,128)S(1)} %get-tuple-element.415, f32[128,1024]{1,0:T(8,128)} %get-tuple-element.409, bf16[1,2,128,1024]{3,2,1,0:T(8,128)(2,1)} %bitcast.59), kind=kOutput, calls=%fused_computation.33 | convolution fusion | flops 545259520 | bytes 2490368 | tf_op jit(solution)/shard_map/ctf,kjf->tkcj/dot_general | solution.py:75
  135.9 3.4 %fusion.34 = bf16[128,128,16]{1,0,2:T(8,128)(2,1)} fusion(f32[128,128,16]{1,0,2:T(8,128)S(1)} %fusion, f32[16,1024]{1,0:T(8,128)S(1)} %get-tuple-element.416, f32[128,1024]{1,0:T(8,128)S(1)} %copy-done.4, f32[16,1024]{1,0:T(8,128)S(1)} %get-tuple-element.415, f32[128,1024]{1,0:T(8,128)S(1)} %copy-done.2, bf16[1,2,128,1024]{3,2,1,0:T(8,128)(2,1)} %bitcast.59), kind=kOutput, calls=%fused_computation.65 | convolution fusion | flops 545783808 | bytes 3014656 | tf_op jit(solution)/shard_map/ctf,kjf->tkcj/dot_general | solution.py:77
  139.3 5.1 %all-to-all-start.14 = ((bf16[4,4,1,128,128]{3,4,1,2,0:T(8,128)(2,1)}), bf16[4,4,1,128,128]{3,4,1,2,0:T(8,128)(2,1)S(1)}, u32[]{:S(2)}, u32[]{:S(2)}) async-start(bf16[4,4,1,128,128]{3,4,1,2,0:T(8,128)(2,1)} %bitcast.67), calls=%async_computation.14 | async-start | bytes 1048576 | tf_op jit(solution)/shard_map/all_to_all | solution.py:86
  144.4 10.2 %all-to-all-done.14 = bf16[4,4,1,128,128]{3,4,1,2,0:T(8,128)(2,1)S(1)} async-done(((bf16[4,4,1,128,128]{3,4,1,2,0:T(8,128)(2,1)}), bf16[4,4,1,128,128]{3,4,1,2,0:T(8,128)(2,1)S(1)}, u32[]{:S(2)}, u32[]{:S(2)}) %all-to-all-start.14) | async-done | bytes 524320 | tf_op jit(solution)/shard_map/all_to_all | solution.py:86
  154.8 1.2 pad_maximum_fusion.1
  156.0 0.6 gather_fusion
  156.8 1.1 copy.125
  (27 shorter events, 1.3 us)
Async XLA Ops:
  7.2 5.9 %copy-start = (s32[4]{0:T(128)S(1)}, s32[4]{0:T(128)}, u32[]{:S(2)}) copy-start(s32[4]{0:T(128)} %param.47) | copy-start | bytes 52
  11.2 66.0 %collective-permute-start.42 = (bf16[2,128,1024]{2,1,0:T(8,128)(2,1)}, bf16[2,128,1024]{2,1,0:T(8,128)(2,1)S(1)}, u32[]{:S(2)}, u32[]{:S(2)}) collective-permute-start(bf16[2,128,1024]{2,1,0:T(8,128)(2,1)} %pad_maximum_fusion.2), channel_id=1, source_target_pairs={{60,0},{64,4},{68,8},{72,12},{76,16},{80,20},{84,24},{88,28},{92,3... | collective-permute-start | bytes 1572872 | tf_op jit(solution)/shard_map/ppermute | solution.py:108
  15.3 20.9 %collective-permute-start.2 = (bf16[2,128,1024]{2,1,0:T(8,128)(2,1)}, bf16[2,128,1024]{2,1,0:T(8,128)(2,1)}, u32[]{:S(2)}, u32[]{:S(2)}) collective-permute-start(bf16[2,128,1024]{2,1,0:T(8,128)(2,1)} %param.2), channel_id=1, source_target_pairs={{12,0},{16,4},{20,8},{24,12},{28,16},{32,20},{36,24},{40,28},{44,3... | collective-permute-start | bytes 1572872 | tf_op jit(solution)/shard_map/cond/branch_2_fun/ppermute | solution.py:108
  36.8 39.1 %collective-permute-start.19 = (bf16[2,128,1024]{2,1,0:T(8,128)(2,1)}, bf16[2,128,1024]{2,1,0:T(8,128)(2,1)}, u32[]{:S(2)}, u32[]{:S(2)}) collective-permute-start(bf16[2,128,1024]{2,1,0:T(8,128)(2,1)} %param.19), channel_id=1, source_target_pairs={{24,0},{28,4},{32,8},{36,12},{40,16},{44,20},{48,24},{52,28},{56,3... | collective-permute-start | bytes 1572872 | tf_op jit(solution)/shard_map/cond/branch_5_fun/ppermute | solution.py:108
  75.9 2.7 %copy-start.1 = (f32[128,1024]{1,0:T(8,128)S(1)}, f32[128,1024]{1,0:T(8,128)}, u32[]{:S(2)}) copy-start(f32[128,1024]{1,0:T(8,128)} %get-tuple-element.409) | copy-start | bytes 1572868
  75.9 2.7 %copy-start.3 = (f32[128,1024]{1,0:T(8,128)S(1)}, f32[128,1024]{1,0:T(8,128)}, u32[]{:S(2)}) copy-start(f32[128,1024]{1,0:T(8,128)} %get-tuple-element.413) | copy-start | bytes 1572868
  94.5 23.6 %all-to-all-start.7 = ((bf16[4,4,3,128,128]{4,3,2,1,0:T(8,128)(2,1)}), bf16[4,4,3,128,128]{4,3,2,1,0:T(8,128)(2,1)S(1)}, u32[]{:S(2)}, u32[]{:S(2)}) async-start(bf16[4,4,3,128,128]{4,3,2,1,0:T(8,128)(2,1)} %bitcast.35), calls=%async_computation.7 | async-start | bytes 3145728 | tf_op jit(solution)/shard_map/cond/branch_7_fun/all_to_all | solution.py:86
  98.8 34.2 %collective-permute-start.35 = (bf16[2,128,1024]{2,1,0:T(8,128)(2,1)}, bf16[2,128,1024]{2,1,0:T(8,128)(2,1)}, u32[]{:S(2)}, u32[]{:S(2)}) collective-permute-start(bf16[2,128,1024]{2,1,0:T(8,128)(2,1)} %get-tuple-element.214), channel_id=1, source_target_pairs={{32,0},{36,4},{40,8},{44,12},{48,16},{52,20},{56,24},{60,28},{64,3... | collective-permute-start | bytes 1572872 | tf_op jit(solution)/shard_map/cond/branch_7_fun/ppermute | solution.py:108
  133.0 2.9 %copy-start.2 = (f32[128,1024]{1,0:T(8,128)S(1)}, f32[128,1024]{1,0:T(8,128)}, u32[]{:S(2)}) copy-start(f32[128,1024]{1,0:T(8,128)} %get-tuple-element.409) | copy-start | bytes 1572868
  133.0 2.9 %copy-start.4 = (f32[128,1024]{1,0:T(8,128)S(1)}, f32[128,1024]{1,0:T(8,128)}, u32[]{:S(2)}) copy-start(f32[128,1024]{1,0:T(8,128)} %get-tuple-element.413) | copy-start | bytes 1572868
  139.3 15.3 %all-to-all-start.14 = ((bf16[4,4,1,128,128]{3,4,1,2,0:T(8,128)(2,1)}), bf16[4,4,1,128,128]{3,4,1,2,0:T(8,128)(2,1)S(1)}, u32[]{:S(2)}, u32[]{:S(2)}) async-start(bf16[4,4,1,128,128]{3,4,1,2,0:T(8,128)(2,1)} %bitcast.67), calls=%async_computation.14 | async-start | bytes 1048576 | tf_op jit(solution)/shard_map/all_to_all | solution.py:86
